TPU v7x, 256 devices: a whole 4x4x8 slice. The times are simulated.
256 devices in a mesh: seq: 32 (over y, z_hi, core), head: 8 (over z_lo, x).
Axes of the slice: x: 4, y: 4, z: 8 (z_hi: 4, z_lo: 2; z = z_hi * 2 + z_lo), core: 2. Of those that a mesh axis runs over, the one named last changes fastest.
Arguments:
- xin: bfloat16 [16384, 8192], P('seq', 'head'), may hold values from -6 to 6
- gate_z: bfloat16 [16384, 8192], P('seq', 'head'), may hold values from -6 to 6
- b_proj: bfloat16 [16384, 8, 256], P('seq', 'head'), may hold values from -0.375 to 0.375
- c_proj: bfloat16 [16384, 8, 256], P('seq', 'head'), may hold values from -0.375 to 0.375
- log_retain: float32 [16384, 128], P('seq', 'head'), may hold values from -2 to 0, as said below
- skip_d: float32 [128], P('head'), may hold values from 0.5 to 2
- norm_gain: float32 [8192], P('head'), may hold values from 0.5 to 1.5
- w_out: bfloat16 [8192, 4096], P('head', 'seq'), may hold values from -0.0625 to 0.0625
- residual: bfloat16 [16384, 4096], P(('seq', 'head')), may hold values from -24 to 24
- refusal: float32 [4096], replicated, may hold values from -6 to 6
- stream_gain: float32 [4096], replicated, may hold values from 0.5 to 1.5
- w_in: bfloat16 [4096, 8192], P('seq', 'head'), may hold values from -0.09375 to 0.09375
Outputs:
- stream: bfloat16 [16384, 4096], P(('seq', 'head'))
- next_x: bfloat16 [16384, 8192], P('seq', 'head')
Inputs may be any that keep to these rules, and one draw needn't show every extreme that they name: `log_retain`: every entry is negative.
All inputs are finite; a program needn't handle non-finite values.
Results may differ from a plain program's by a relative error of at most 0.02.
Values may be sent and summed in bfloat16 or wider, within the bound.
No kernel may reach another device: no remote copies, remote signals or barrier semaphores. Data moves between devices by JAX's collectives and lax.ppermute only.
A program may use at most 192 MiB of HBM per device.

v0:
```python
import jax
import jax.numpy as jnp
from jax import lax
from jax.sharding import PartitionSpec as P

SPAN = 256


def prefix(array, axis, combine, identity):
    devices, place = (lax.axis_size(axis), lax.axis_index(axis))
    everything = jax.tree.map(
        lambda part, kind: lax.all_gather(part.astype(kind), axis),
        array,
        (jnp.bfloat16, jnp.bfloat16),
    )
    start = jax.tree.map(
        lambda part, zero: jnp.broadcast_to(jnp.asarray(zero, part.dtype), part.shape),
        array,
        identity,
    )

    def turn(k, before):
        reached = k < place
        new = combine(
            before, jax.tree.map(lambda part, own: part[k].astype(own.dtype), everything, array)
        )
        return jax.tree.map(lambda a, b: jnp.where(reached, a, b), new, before)

    return lax.fori_loop(0, devices, turn, start)


def carry_combine(earlier, later):
    decay_early, state_early = earlier
    decay_later, state_later = later
    return (
        decay_early + decay_later,
        jnp.exp(decay_later)[:, None, None] * state_early + state_later,
    )


def body(
    xin,
    gate_z,
    b_proj,
    c_proj,
    log_retain,
    skip_d,
    norm_gain,
    w_out,
    residual,
    refusal,
    stream_gain,
    w_in,
):
    seq_rows, channels = xin.shape
    head_count = log_retain.shape[1]
    head_width = channels // head_count
    group_count = b_proj.shape[1]
    state_width = b_proj.shape[2]
    per_group = head_count // group_count
    block_count = seq_rows // SPAN
    inputs = xin.reshape(block_count, SPAN, head_count, head_width)
    b_grouped = b_proj.reshape(block_count, SPAN, group_count, state_width)
    c_grouped = c_proj.reshape(block_count, SPAN, group_count, state_width)
    scores = jnp.einsum("klgn,ksgn->kgls", c_grouped, b_grouped, preferred_element_type=jnp.float32)
    scores = jnp.repeat(scores, per_group, axis=1)
    cum = jnp.cumsum(log_retain.reshape(block_count, SPAN, head_count), axis=1)
    cum_heads = jnp.transpose(cum, (0, 2, 1))
    later_pos = lax.broadcasted_iota(jnp.int32, (SPAN, SPAN), 0)
    earlier_pos = lax.broadcasted_iota(jnp.int32, (SPAN, SPAN), 1)
    causal = later_pos >= earlier_pos
    gap = cum_heads[:, :, :, None] - cum_heads[:, :, None, :]
    mixing = (jnp.where(causal, jnp.exp(jnp.where(causal, gap, 0.0)), 0.0) * scores).astype(
        jnp.bfloat16
    )
    intra = jnp.einsum("khls,kshp->klhp", mixing, inputs, preferred_element_type=jnp.float32)
    tail_decay = jnp.exp(cum_heads[:, :, -1:] - cum_heads)
    b_heads = jnp.repeat(b_grouped, per_group, axis=2)
    weighted_b = (
        b_heads.astype(jnp.float32) * jnp.transpose(tail_decay, (0, 2, 1))[..., None]
    ).astype(jnp.bfloat16)
    block_state = jnp.einsum(
        "klhn,klhp->khnp", weighted_b, inputs, preferred_element_type=jnp.float32
    )
    block_decay = cum_heads[:, :, -1]

    def advance(carried_state, pair):
        decay_here, state_here = pair
        return (jnp.exp(decay_here)[:, None, None] * carried_state + state_here, carried_state)

    zero_state = jnp.zeros((head_count, state_width, head_width), jnp.float32)
    device_state, local_starts = lax.scan(advance, zero_state, (block_decay, block_state))
    device_decay = jnp.sum(block_decay, axis=0)
    zero_decay = jnp.zeros((head_count,), jnp.float32)
    total_decay, incoming = prefix(
        (device_decay, device_state), "seq", carry_combine, (zero_decay, zero_state)
    )
    before_block = jnp.cumsum(block_decay, axis=0) - block_decay
    starts = local_starts + jnp.exp(before_block)[:, :, None, None] * incoming[None]
    c_heads = jnp.repeat(c_grouped, per_group, axis=2).astype(jnp.float32)
    carried = jnp.einsum("klhn,khnp->klhp", c_heads, starts, precision=lax.Precision.HIGHEST)
    carried = carried * jnp.exp(cum)[..., None]
    mixed = intra + carried + skip_d[None, None, :, None] * inputs.astype(jnp.float32)
    gated = mixed * jax.nn.silu(
        gate_z.reshape(block_count, SPAN, head_count, head_width).astype(jnp.float32)
    )
    grouped = gated.reshape(seq_rows, group_count, per_group * head_width)
    grouped = grouped * lax.rsqrt(jnp.mean(grouped * grouped, axis=-1, keepdims=True) + 1e-05)
    ssd_out = (grouped.reshape(seq_rows, channels) * norm_gain[None, :]).astype(jnp.bfloat16)
    partial_sum = jnp.dot(
        ssd_out,
        lax.all_gather(w_out, "seq", axis=1, tiled=True),
        preferred_element_type=jnp.float32,
    )
    mixer_out = lax.psum_scatter(
        partial_sum.astype(jnp.bfloat16), "head", scatter_dimension=0, tiled=True
    ).astype(jnp.float32)
    unit = refusal / jnp.sqrt(jnp.sum(refusal * refusal) + 1e-06)
    hidden = residual.astype(jnp.float32) + mixer_out
    coef = jnp.dot(hidden, unit, precision=lax.Precision.HIGHEST)
    stream = (hidden - coef[:, None] * unit[None, :]).astype(jnp.bfloat16)
    stream_float = stream.astype(jnp.float32)
    normed = (
        stream_float
        * lax.rsqrt(jnp.mean(stream_float * stream_float, axis=-1, keepdims=True) + 1e-05)
        * stream_gain[None, :]
    ).astype(jnp.bfloat16)
    all_rows = lax.all_gather(normed, "head", axis=0, tiled=True)
    next_float = jnp.dot(
        all_rows,
        lax.all_gather(w_in, "seq", axis=0, tiled=True),
        preferred_element_type=jnp.float32,
    )
    return (stream, next_float.astype(jnp.bfloat16))


def solution(mesh):
    in_specs = (
        P("seq", "head"),
        P("seq", "head"),
        P("seq", "head", None),
        P("seq", "head", None),
        P("seq", "head"),
        P("head"),
        P("head"),
        P("head", "seq"),
        P(("seq", "head"), None),
        P(),
        P(),
        P("seq", "head"),
    )
    out_specs = (P(("seq", "head"), None), P("seq", "head"))
    return jax.shard_map(body, mesh=mesh, in_specs=in_specs, out_specs=out_specs, check_vma=False)
```

profile of v0, /device:TPU:1, one launch (start us, length us, event | category | flops | bytes accessed | tf_op | source)
XLA Modules:
  0.0 529.7 jit_solution(17022700494069063450)
XLA Ops:
  10.4 4.0 reshape.182
  14.4 2.8 copy.50
  17.2 2.0 convert_element_type.84
  19.1 5.1 fusion.4
  24.2 6.9 %while.27 = (s32[]{:T(128)}, f32[16,256,64]{2,1,0:T(8,128)S(1)}, f32[2,16,256,64]{3,2,1,0:T(8,128)}, f32[2,16]{1,0:T(2,128)S(1)}, f32[2,16,256,64]{3,2,1,0:T(8,128)}, /*index=5*/s32[]{:T(128)}, s32[]{:T(128)}) while((s32[]{:T(128)}, f32[16,256,64]{2,1,0:T(8,128)S(1)}, f32[2,16,256,64]{3,2,1,0:T(8,128)}, f32[2,16]{1,0:T(2,128)S(1)}, ...), condition=%wide.region_3.4_spmd.clone, body=%wide.region_2.3_spmd.clone.sunk | while | flops 1048579 | bytes 14680892 | solution.py:92
  34.7 76.6 %all-reduce = bf16[512]{0:T(512)(128)(2,1)S(1)} all-reduce(bf16[512]{0:T(512)(128)(2,1)S(1)} %dynamic-update-slice), channel_id=2, replica_groups=mesh['seq'=32,'head'=8] {'seq'}, use_global_device_ids=true, to_apply=%add | all-reduce | flops 512 | bytes 2048
  111.4 2.0 fusion.27
  113.4 2.6 reshape.183
  116.0 4.6 copy.59
  120.6 25.5 %all-gather.13.cloned.1.call-done = bf16[512,256,64]{1,2,0:T(8,128)(2,1)} async-done(((bf16[16,256,64]{1,2,0:T(8,128)(2,1)}), bf16[512,256,64]{1,2,0:T(8,128)(2,1)}) %all-gather.13.cloned.1.call-update) | async-done | bytes 16777232 | tf_op jit(solution)/shard_map/all_gather | solution.py:12
  146.1 144.1 %while.28 = (s32[]{:T(128)}, f32[16,256,64]{2,1,0:T(8,128)S(1)}, s32[]{:T(128)}, bf16[32,16]{1,0:T(8,128)(2,1)S(1)}, bf16[32,16,256,64]{2,3,1,0:T(8,128)(2,1)}, /*index=5*/s32[]{:T(128)}, s32[]{:T(128)}) while((s32[]{:T(128)}, f32[16,256,64]{2,1,0:T(8,128)S(1)}, s32[]{:T(128)}, bf16[32,16]{1,0:T(8,128)(2,1)S(1)}, ...), condition=%wide.region_7.8_spmd.clone, body=%wide.region_6.7_spmd.clone.sunk | while | flops 1310740 | bytes 4718857 | solution.py:29
  150.6 1.9 constant_dynamic-slice_fusion.3
  168.5 1.9 constant_dynamic-slice_fusion.3
  177.6 1.9 constant_dynamic-slice_fusion.3
  213.5 1.9 constant_dynamic-slice_fusion.3
  227.0 2.0 constant_dynamic-slice_fusion.3
  290.3 6.0 %fusion.5 = f32[2,16,64,256]{3,2,1,0:T(8,128)S(1)} fusion(f32[2,16,256,64]{3,2,1,0:T(8,128)} %get-tuple-element.124, bf16[2,256,256]{2,1,0:T(8,128)(2,1)S(1)} %bitcast.79, f32[16,256,64]{2,1,0:T(8,128)S(1)} %get-tuple-element.126, f32[2,16]{1,0:T(2,128)S(1)} %subtract_exponential_fusion), kind=kOutput, calls=%fused_computation.14 | convolution fusion | flops 1611661312 | bytes 5505152 | tf_op jit(solution)/shard_map/klhn,khnp->klhp/dot_general | solution.py:101
  296.4 3.0 multiply_reduce_fusion
  302.6 10.9 %convolution_convert_fusion = bf16[512,4096]{1,0:T(8,128)(2,1)} fusion(bf16[1024,4096]{1,0:T(8,128)(2,1)} %all-gather.7.cloned.1.call-done, f32[512,1024]{0,1:T(8,128)} %bitcast.81, f32[1024]{0:T(1024)S(1)} %copy-done.13, f32[512]{0:T(512)S(1)} %bitcast.87), kind=kOutput, calls=%fused_computation.11 | convolution fusion | flops 4298637312 | bytes 14686208 | tf_op jit(solution)/shard_map/dot_general | solution.py:110
  315.6 61.8 %reduce-scatter.2.cloned.1.call-done = bf16[64,4096]{1,0:T(8,128)(2,1)} async-done(((bf16[512,4096]{1,0:T(8,128)(2,1)}), bf16[64,4096]{1,0:T(8,128)(2,1)}) %reduce-scatter.2.cloned.1.call-update) | async-done | bytes 524304 | tf_op jit(solution)/shard_map/reduce_scatter | solution.py:115
  377.4 2.0 convolution_bitcast_fusion
  381.8 73.2 %all-gather.11.cloned.1.call-done = bf16[4096,1024]{1,0:T(8,128)(2,1)} async-done(((bf16[128,1024]{1,0:T(8,128)(2,1)}), bf16[4096,1024]{1,0:T(8,128)(2,1)}) %all-gather.11.cloned.1.call-update) | async-done | bytes 8388624 | tf_op jit(solution)/shard_map/all_gather | solution.py:131
  455.0 57.9 %all-gather.9.cloned.1.call-done = bf16[512,4096]{1,0:T(8,128)(2,1)} async-done(((bf16[64,4096]{1,0:T(8,128)(2,1)}), bf16[512,4096]{1,0:T(8,128)(2,1)}) %all-gather.9.cloned.1.call-update) | async-done | bytes 4194320 | tf_op jit(solution)/shard_map/all_gather | solution.py:128
  513.0 10.1 %convolution_convert_fusion.1 = bf16[512,1024]{1,0:T(8,128)(2,1)} fusion(bf16[512,4096]{1,0:T(8,128)(2,1)} %all-gather.9.cloned.1.call-done, bf16[4096,1024]{1,0:T(8,128)(2,1)} %all-gather.11.cloned.1.call-done), kind=kOutput, calls=%fused_computation.33 | convolution fusion | flops 4295491584 | bytes 13631488 | tf_op jit(solution)/shard_map/dot_general | solution.py:129
  (202 shorter events, 152.9 us)
Async XLA Ops:
  7.2 104.2 %copy-start = (bf16[512,1,256]{2,0,1:T(8,128)(2,1)S(1)}, bf16[512,1,256]{2,0,1:T(8,128)(2,1)}, u32[]{:S(2)}) copy-start(bf16[512,1,256]{2,0,1:T(8,128)(2,1)} %param.19) | copy-start | bytes 786436
  7.2 138.9 %all-gather.13.cloned.1.call-start = ((), (), s32[]{:S(2)}) async-start(), calls=%async_computation.5 | async-start | bytes 17301504 | tf_op jit(solution)/shard_map/all_gather | solution.py:12
  17.2 7.1 %copy-start.3 = (bf16[2,256,16,64]{1,3,2,0:T(8,128)(2,1)}, bf16[2,256,16,64]{1,3,2,0:T(8,128)(2,1)S(1)}, u32[]{:S(2)}) copy-start(bf16[2,256,16,64]{1,3,2,0:T(8,128)(2,1)S(1)} %copy.50) | copy-start | bytes 3145732
  24.2 2.9 copy-start.2
  27.7 2.9 copy-start.2
  31.2 2.1 copy-start.15
  31.2 82.2 %copy-start.8 = (bf16[512,1024]{1,0:T(8,128)(2,1)S(1)}, bf16[512,1024]{1,0:T(8,128)(2,1)}, u32[]{:S(2)}) copy-start(bf16[512,1024]{1,0:T(8,128)(2,1)} %param.17) | copy-start | bytes 3145732
  32.3 270.3 %all-gather.7.cloned.1.call-start = ((), (), s32[]{:S(2)}) async-start(), calls=%async_computation.1 | async-start | bytes 8650752 | tf_op jit(solution)/shard_map/all_gather | solution.py:112
  33.1 344.3 %reduce-scatter.2.cloned.1.call-start = ((), (), s32[]{:S(2)}) async-start(), calls=%async_computation.2 | async-start | bytes 4718592 | tf_op jit(solution)/shard_map/reduce_scatter | solution.py:115
  290.2 6.1 %copy-start.4 = (bf16[2,256,16,64]{1,3,2,0:T(8,128)(2,1)S(1)}, bf16[2,256,16,64]{1,3,2,0:T(8,128)(2,1)}, u32[]{:S(2)}) copy-start(bf16[2,256,16,64]{1,3,2,0:T(8,128)(2,1)} %copy-done.3) | copy-start | bytes 3145732
  290.2 6.1 %copy-start.5 = (f32[2,256,16,64]{1,3,2,0:T(8,128)S(1)}, f32[2,256,16,64]{1,3,2,0:T(8,128)}, u32[]{:S(2)}) copy-start(f32[2,256,16,64]{1,3,2,0:T(8,128)} %copy.59) | copy-start | bytes 6291460
  290.2 6.1 %copy-start.9 = (f32[2,256,256]{2,1,0:T(8,128)S(1)}, f32[2,256,256]{2,1,0:T(8,128)}, u32[]{:S(2)}) copy-start(f32[2,256,256]{2,1,0:T(8,128)} %fusion.27) | copy-start | bytes 1572868
  290.2 6.1 %copy-start.11 = (f32[2,256,16]{1,2,0:T(8,128)S(1)}, f32[2,256,16]{1,2,0:T(8,128)}, u32[]{:S(2)}) copy-start(f32[2,256,16]{1,2,0:T(8,128)} %get-tuple-element.212) | copy-start | bytes 98308
  290.3 6.1 %copy-start.14 = (f32[16]{0:T(128)S(1)}, f32[16]{0:T(128)}, u32[]{:S(2)}) copy-start(f32[16]{0:T(128)} %param.21) | copy-start | bytes 196
  301.1 1.6 copy-start.13
  313.5 0.7 copy-start.10
  313.5 63.8 %copy-start.6 = (bf16[64,4096]{1,0:T(8,128)(2,1)S(1)}, bf16[64,4096]{1,0:T(8,128)(2,1)}, u32[]{:S(2)}) copy-start(bf16[64,4096]{1,0:T(8,128)(2,1)} %param.24) | copy-start | bytes 1572868
  313.6 67.2 %copy-start.12 = (f32[4096]{0:T(1024)S(1)}, f32[4096]{0:T(1024)}, u32[]{:S(2)}) copy-start(f32[4096]{0:T(1024)} %param.26) | copy-start | bytes 49156
  313.6 141.4 %all-gather.11.cloned.1.call-start = ((), (), s32[]{:S(2)}) async-start(), calls=%async_computation.4 | async-start | bytes 8650752 | tf_op jit(solution)/shard_map/all_gather | solution.py:131
  314.2 198.8 %all-gather.9.cloned.1.call-start = ((), (), s32[]{:S(2)}) async-start(), calls=%async_computation.3 | async-start | bytes 4718592 | tf_op jit(solution)/shard_map/all_gather | solution.py:128
  380.8 142.3 %copy-start.7 = (bf16[64,4096]{1,0:T(8,128)(2,1)}, bf16[64,4096]{1,0:T(8,128)(2,1)S(1)}, u32[]{:S(2)}) copy-start(bf16[64,4096]{1,0:T(8,128)(2,1)S(1)} %get-tuple-element.211) | copy-start | bytes 1572868
  513.0 10.2 %copy-start.1 = (bf16[512,1,256]{2,0,1:T(8,128)(2,1)S(1)}, bf16[512,1,256]{2,0,1:T(8,128)(2,1)}, u32[]{:S(2)}) copy-start(bf16[512,1,256]{2,0,1:T(8,128)(2,1)} %param.19) | copy-start | bytes 786436
Sparse Core Ops, SparseCore 0:
  32.5 113.5 all-gather.12
  148.6 93.9 all-gather.6
  313.7 63.6 reduce-scatter.1
  379.8 75.2 all-gather.10
  457.2 55.6 all-gather.8
where the time goes:
time: 533 us; the launch traced here: 530 us
  waiting for transfers between devices  220 us (41%)
  local copies, waits for them, and re-layouts  132 us (25%)
  blocking collectives  76.6 us (14%)
  other arithmetic  44.8 us (8%)
  matrix products  39.3 us (7%)
  between operations  15.4 us (3%)
    dynamic_slice x64, local copies, waits for them, and re-layouts, turn(): part[k].astype(own.dtype)  109 us
    unnamed x1, blocking collectives  76.6 us
    all_gather x1, waiting for transfers between devices, body(): lax.all_gather(w_in, 'seq', axis=0, tiled=True)  73.2 us
    reduce_scatter x1, waiting for transfers between devices, body(): lax.psum_scatter(partial_sum.astype(jnp.bfloat16), 'head', scatter_dimens...  61.8 us
    all_gather x1, waiting for transfers between devices, body(): all_rows = lax.all_gather(normed, 'head', axis=0, tiled=True)  57.9 us
    select_n x32, other arithmetic, turn(): return jax.tree.map(lambda a, b: jnp.where(reached, a, b), new, before)  33 us
    all_gather x1, waiting for transfers between devices, prefix(): lax.all_gather(part.astype(kind), axis)  25.5 us
    dot_general x1, matrix products, body(): jnp.dot(ssd_out, lax.all_gather(w_out, 'seq', axis=1, tiled=True), prefer...  10.9 us
  transfers between devices with their start and end apart: 5, of which 4 were waited for; matrix products, arithmetic and copies ran while one was open for 32% of the time, Pallas kernels for 0%

commit v1 on v0

--- a/solution.py
+++ b/solution.py
@@ -6,27 +6,23 @@
 SPAN = 256
 
 
-def prefix(array, axis, combine, identity):
-    devices, place = (lax.axis_size(axis), lax.axis_index(axis))
-    everything = jax.tree.map(
-        lambda part, kind: lax.all_gather(part.astype(kind), axis),
-        array,
-        (jnp.bfloat16, jnp.bfloat16),
-    )
-    start = jax.tree.map(
-        lambda part, zero: jnp.broadcast_to(jnp.asarray(zero, part.dtype), part.shape),
-        array,
-        identity,
-    )
+def shift_scan(decay, state, axis):
+    devices = lax.axis_size(axis)
 
-    def turn(k, before):
-        reached = k < place
-        new = combine(
-            before, jax.tree.map(lambda part, own: part[k].astype(own.dtype), everything, array)
+    def shifted(parts, distance):
+        pairs = [(i, i + distance) for i in range(devices - distance)]
+        a, s = parts
+        return (
+            lax.ppermute(a, axis, pairs),
+            lax.ppermute(s.astype(jnp.bfloat16), axis, pairs).astype(jnp.float32),
         )
-        return jax.tree.map(lambda a, b: jnp.where(reached, a, b), new, before)
 
-    return lax.fori_loop(0, devices, turn, start)
+    acc = shifted((decay, state), 1)
+    distance = 1
+    while distance < devices:
+        acc = carry_combine(shifted(acc, distance), acc)
+        distance *= 2
+    return acc
 
 
 def carry_combine(earlier, later):
@@ -91,10 +87,7 @@
     zero_state = jnp.zeros((head_count, state_width, head_width), jnp.float32)
     device_state, local_starts = lax.scan(advance, zero_state, (block_decay, block_state))
     device_decay = jnp.sum(block_decay, axis=0)
-    zero_decay = jnp.zeros((head_count,), jnp.float32)
-    total_decay, incoming = prefix(
-        (device_decay, device_state), "seq", carry_combine, (zero_decay, zero_state)
-    )
+    total_decay, incoming = shift_scan(device_decay, device_state, "seq")
     before_block = jnp.cumsum(block_decay, axis=0) - block_decay
     starts = local_starts + jnp.exp(before_block)[:, :, None, None] * incoming[None]
     c_heads = jnp.repeat(c_grouped, per_group, axis=2).astype(jnp.float32)
@@ -107,6 +100,8 @@
     grouped = gated.reshape(seq_rows, group_count, per_group * head_width)
     grouped = grouped * lax.rsqrt(jnp.mean(grouped * grouped, axis=-1, keepdims=True) + 1e-05)
     ssd_out = (grouped.reshape(seq_rows, channels) * norm_gain[None, :]).astype(jnp.bfloat16)
+    w_in_all = lax.all_gather(w_in, "seq", axis=0, tiled=True)
+    ssd_out, w_in_all = lax.optimization_barrier((ssd_out, w_in_all))
     partial_sum = jnp.dot(
         ssd_out,
         lax.all_gather(w_out, "seq", axis=1, tiled=True),
@@ -128,7 +123,7 @@
     all_rows = lax.all_gather(normed, "head", axis=0, tiled=True)
     next_float = jnp.dot(
         all_rows,
-        lax.all_gather(w_in, "seq", axis=0, tiled=True),
+        w_in_all,
         preferred_element_type=jnp.float32,
     )
     return (stream, next_float.astype(jnp.bfloat16))

time: 533 us -> 372 us (0.70)
  local copies, waits for them, and re-layouts: 132 us -> 25.5 us
  blocking collectives: 76.6 us -> 0 us
  starting transfers between devices: 0.2 us -> 58.7 us
  other arithmetic: 44.8 us -> 16.1 us
    dynamic_slice x64 -> x0, local copies, waits for them, and re-layouts: 109 us -> none  [turn(): part[k].astype(own.dtype)]
    all_gather x2 -> x1, waiting for transfers between devices: 98.7 us -> 0.02 us  [body(): w_in_all = lax.all_gather(w_in, 'seq', axis=0, tiled=True)]
    ppermute x0 -> x11, waiting for transfers between devices: none -> 88.5 us  [the longest x5 59.5 us: shifted(): lax.ppermute(a, axis, pairs)]
    unnamed x1 -> x0, blocking collectives: 76.6 us -> none
    ppermute x0 -> x11, starting transfers between devices: none -> 58.3 us  [the longest x6 37.3 us: shifted(): lax.ppermute(s.astype(jnp.bfloat16), axis, pairs).astype(jnp.float32)]
    select_n x32 -> x0, other arithmetic: 33 us -> none  [turn(): return jax.tree.map(lambda a, b: jnp.where(reached, a, b), new, before)]
    reduce_scatter x1, waiting for transfers between devices: 61.8 us -> 67.4 us  [body(): lax.psum_scatter(partial_sum.astype(jnp.bfloat16), 'head', scatter_dimens...]
    all_gather x1, waiting for transfers between devices: 0.01 us -> 5.35 us  [body(): lax.all_gather(w_out, 'seq', axis=1, tiled=True)]
  transfers between devices with their start and end apart: 5 -> 15, of which waited for: 4 -> 10; matrix products, arithmetic and copies ran while one was open for 32% -> 14% of each run, Pallas kernels for 0% -> 0%
where the time goes in v1:
time: 372 us; the launch traced here: 371 us
  waiting for transfers between devices  217 us (58%)
  starting transfers between devices  58.7 us (16%)
  matrix products  39 us (10%)
  local copies, waits for them, and re-layouts  25.5 us (7%)
  other arithmetic  16.1 us (4%)
  between operations  14.8 us (4%)
    reduce_scatter x1, waiting for transfers between devices, body(): lax.psum_scatter(partial_sum.astype(jnp.bfloat16), 'head', scatter_dimens...  67.4 us
    ppermute x5, waiting for transfers between devices, shifted(): lax.ppermute(a, axis, pairs)  59.5 us
    all_gather x1, waiting for transfers between devices, body(): all_rows = lax.all_gather(normed, 'head', axis=0, tiled=True)  54.1 us
    ppermute x6, starting transfers between devices, shifted(): lax.ppermute(s.astype(jnp.bfloat16), axis, pairs).astype(jnp.float32)  37.3 us
    ppermute x6, waiting for transfers between devices, shifted(): lax.ppermute(s.astype(jnp.bfloat16), axis, pairs).astype(jnp.float32)  28.9 us
    ppermute x5, starting transfers between devices, shifted(): lax.ppermute(a, axis, pairs)  21.1 us
    dot_general x1, matrix products, body(): next_float = jnp.dot(all_rows, w_in_all, preferred_element_type=jnp.float32)  10.1 us
    dot_general x1, matrix products, body(): jnp.dot(ssd_out, lax.all_gather(w_out, 'seq', axis=1, tiled=True), prefer...  9.48 us
  transfers between devices with their start and end apart: 15, of which 10 were waited for; matrix products, arithmetic and copies ran while one was open for 14% of the time, Pallas kernels for 0%

profile of v1, /device:TPU:1, one launch (start us, length us, event | category | flops | bytes accessed | tf_op | source)
XLA Modules:
  0.0 370.9 jit_solution(16019038935914935023)
XLA Ops:
  19.8 5.1 %fusion.3 = f32[2,16,256,64]{3,2,1,0:T(8,128)} fusion(bf16[2,256,16,64]{1,3,2,0:T(8,128)(2,1)S(1)} %copy.50, f32[2,256,16]{1,2,0:T(8,128)S(1)} %get-tuple-element.95, f32[2,256,256]{2,1,0:T(8,128)} %convert_element_type.80), kind=kOutput, calls=%fused_computation.9 | convolution fusion | flops 272629760 | bytes 3702784 | tf_op jit(solution)/shard_map/klhn,klhp->khnp/dot_general | solution.py:78
  24.9 7.1 %while.13 = (s32[]{:T(128)}, f32[16,256,64]{2,1,0:T(8,128)S(1)}, f32[2,16,256,64]{3,2,1,0:T(8,128)}, f32[2,16]{1,0:T(2,128)S(1)}, f32[2,16,256,64]{3,2,1,0:T(8,128)}, /*index=5*/s32[]{:T(128)}, s32[]{:T(128)}) while((s32[]{:T(128)}, f32[16,256,64]{2,1,0:T(8,128)S(1)}, f32[2,16,256,64]{3,2,1,0:T(8,128)}, f32[2,16]{1,0:T(2,128)S(1)}, ...), condition=%wide.region_3.4_spmd.clone, body=%wide.region_2.3_spmd.clone.sunk | while | flops 1048579 | bytes 14680892 | solution.py:88
  33.1 6.4 %collective-permute-start.5 = (bf16[16,256,64]{1,2,0:T(8,128)(2,1)}, bf16[16,256,64]{1,2,0:T(8,128)(2,1)S(1)}, u32[]{:S(2)}, u32[]{:S(2)}) collective-permute-start(bf16[16,256,64]{1,2,0:T(8,128)(2,1)} %copy.53), channel_id=1, source_target_pairs={{0,8},{8,16},{16,24},{24,32},{32,40},{40,48},{48,56},{56,64},{64,7... | collective-permute-start | bytes 1572872 | tf_op jit(solution)/shard_map/ppermute | solution.py:17
  39.4 9.6 %collective-permute-done.5 = bf16[16,256,64]{1,2,0:T(8,128)(2,1)S(1)} collective-permute-done((bf16[16,256,64]{1,2,0:T(8,128)(2,1)}, bf16[16,256,64]{1,2,0:T(8,128)(2,1)S(1)}, u32[]{:S(2)}, u32[]{:S(2)}) %collective-permute-start.5) | collective-permute-done | bytes 524320 | tf_op jit(solution)/shard_map/ppermute | solution.py:17
  49.1 5.2 %collective-permute-start.6 = (bf16[16,256,64]{1,2,0:T(8,128)(2,1)S(1)}, bf16[16,256,64]{1,2,0:T(8,128)(2,1)S(1)}, u32[]{:S(2)}, u32[]{:S(2)}) collective-permute-start(bf16[16,256,64]{1,2,0:T(8,128)(2,1)S(1)} %collective-permute-done.5), channel_id=1, source_target_pairs={{0,8},{8,16},{16,24},{24,32},{32,40},{40,48},{48,56},{56,64},{64,7... | collective-permute-start | bytes 1572872 | tf_op jit(solution)/shard_map/ppermute | solution.py:17
  54.3 5.2 %collective-permute-start = (f32[16]{0:T(128)S(1)}, f32[16]{0:T(128)S(1)}, u32[]{:S(2)}, u32[]{:S(2)}) collective-permute-start(f32[16]{0:T(128)S(1)} %get-tuple-element.74), channel_id=1, source_target_pairs={{0,8},{8,16},{16,24},{24,32},{32,40},{40,48},{48,56},{56,64},{64,7... | collective-permute-start | bytes 200 | tf_op jit(solution)/shard_map/ppermute | solution.py:16
  59.4 23.0 %collective-permute-done = f32[16]{0:T(128)S(1)} collective-permute-done((f32[16]{0:T(128)S(1)}, f32[16]{0:T(128)S(1)}, u32[]{:S(2)}, u32[]{:S(2)}) %collective-permute-start) | collective-permute-done | bytes 96 | tf_op jit(solution)/shard_map/ppermute | solution.py:16
  82.4 5.2 %collective-permute-start.1 = (f32[16]{0:T(128)S(1)}, f32[16]{0:T(128)S(1)}, u32[]{:S(2)}, u32[]{:S(2)}) collective-permute-start(f32[16]{0:T(128)S(1)} %collective-permute-done), channel_id=1, source_target_pairs={{0,8},{8,16},{16,24},{24,32},{32,40},{40,48},{48,56},{56,64},{64,7... | collective-permute-start | bytes 200 | tf_op jit(solution)/shard_map/ppermute | solution.py:16
  88.6 12.1 %collective-permute-start.7 = (bf16[16,256,64]{1,2,0:T(8,128)(2,1)S(1)}, bf16[16,256,64]{1,2,0:T(8,128)(2,1)S(1)}, u32[]{:S(2)}, u32[]{:S(2)}) collective-permute-start(bf16[16,256,64]{1,2,0:T(8,128)(2,1)S(1)} %fusion.27), channel_id=1, source_target_pairs={{0,16},{8,24},{16,32},{24,40},{32,48},{40,56},{48,64},{56,72},{64,... | collective-permute-start | bytes 1572872 | tf_op jit(solution)/shard_map/ppermute | solution.py:17
  100.7 11.6 %collective-permute-done.7 = bf16[16,256,64]{1,2,0:T(8,128)(2,1)S(1)} collective-permute-done((bf16[16,256,64]{1,2,0:T(8,128)(2,1)S(1)}, bf16[16,256,64]{1,2,0:T(8,128)(2,1)S(1)}, u32[]{:S(2)}, u32[]{:S(2)}) %collective-permute-start.7) | collective-permute-done | bytes 524320 | tf_op jit(solution)/shard_map/ppermute | solution.py:17
  116.3 5.0 %collective-permute-start.2 = (f32[16]{0:T(128)S(1)}, f32[16]{0:T(128)S(1)}, u32[]{:S(2)}, u32[]{:S(2)}) collective-permute-start(f32[16]{0:T(128)S(1)} %get-tuple-element.93), channel_id=1, source_target_pairs={{0,16},{8,24},{16,32},{24,40},{32,48},{40,56},{48,64},{56,72},{64,... | collective-permute-start | bytes 200 | tf_op jit(solution)/shard_map/ppermute | solution.py:16
  121.3 35.2 %collective-permute-done.2 = f32[16]{0:T(128)S(1)} collective-permute-done((f32[16]{0:T(128)S(1)}, f32[16]{0:T(128)S(1)}, u32[]{:S(2)}, u32[]{:S(2)}) %collective-permute-start.2) | collective-permute-done | bytes 96 | tf_op jit(solution)/shard_map/ppermute | solution.py:16
  157.0 5.3 %collective-permute-start.9 = (bf16[16,256,64]{1,2,0:T(8,128)(2,1)S(1)}, bf16[16,256,64]{1,2,0:T(8,128)(2,1)S(1)}, u32[]{:S(2)}, u32[]{:S(2)}) collective-permute-start(bf16[16,256,64]{1,2,0:T(8,128)(2,1)S(1)} %fusion.28), channel_id=1, source_target_pairs={{0,64},{8,72},{16,80},{24,88},{32,96},{40,104},{48,112},{56,120},{... | collective-permute-start | bytes 1572872 | tf_op jit(solution)/shard_map/ppermute | solution.py:17
  167.3 7.6 %collective-permute-done.9 = bf16[16,256,64]{1,2,0:T(8,128)(2,1)S(1)} collective-permute-done((bf16[16,256,64]{1,2,0:T(8,128)(2,1)S(1)}, bf16[16,256,64]{1,2,0:T(8,128)(2,1)S(1)}, u32[]{:S(2)}, u32[]{:S(2)}) %collective-permute-start.9) | collective-permute-done | bytes 524320 | tf_op jit(solution)/shard_map/ppermute | solution.py:17
  177.1 4.8 %collective-permute-start.10 = (bf16[16,256,64]{1,2,0:T(8,128)(2,1)}, bf16[16,256,64]{1,2,0:T(8,128)(2,1)}, u32[]{:S(2)}, u32[]{:S(2)}) collective-permute-start(bf16[16,256,64]{1,2,0:T(8,128)(2,1)} %fusion.30), channel_id=1, source_target_pairs={{0,128},{8,136},{16,144},{24,152},{32,160},{40,168},{48,176},{56,1... | collective-permute-start | bytes 1572872 | tf_op jit(solution)/shard_map/ppermute | solution.py:17
  182.0 4.1 %fusion.2 = f32[2,16,256,64]{2,3,1,0:T(8,128)} fusion(bf16[2,256,16,64]{1,3,2,0:T(8,128)(2,1)S(1)} %copy.50, f32[2,256,256]{2,1,0:T(8,128)S(1)} %fusion.35, f32[2,16,256]{2,1,0:T(8,128)S(1)} %copy_bitcast_fusion, pred[256,256]{1,0:T(8,128)(4,1)S(1)} %iota_compare_fusion), kind=kOutput, calls=%fused_computation.8 | convolution fusion | flops 278921216 | bytes 3768320 | tf_op jit(solution)/shard_map/khls,kshp->klhp/dot_general | solution.py:72
  186.1 4.2 %reshape.159 = f32[2,256,16,64]{3,2,1,0:T(8,128)} reshape(bf16[512,1024]{1,0:T(8,128)(2,1)} %param.15) | data formatting | bytes 3145728 | tf_op jit(solution)/shard_map/convert_element_type | solution.py:98
  191.9 4.6 %copy.59 = f32[2,256,16,64]{1,3,2,0:T(8,128)} copy(f32[2,256,16,64]{3,2,1,0:T(8,128)} %reshape.159) | data formatting | bytes 4194304 | tf_op jit(solution)/shard_map/convert_element_type | solution.py:98
  201.2 7.9 %multiply_reduce_fusion = (f32[2,256]{1,0:T(2,128)S(1)}, f32[2,256,16,64]{1,3,2,0:T(8,128)S(1)}) fusion(f32[2,256,16,64]{1,3,2,0:T(8,128)} %copy.59, bf16[2,256,16,64]{1,3,2,0:T(8,128)(2,1)S(1)} %copy.50, f32[16]{0:T(128)S(1)} %copy-done.10, f32[2,256,16]{1,2,0:T(8,128)S(1)} %get-tuple-element.94, bf16[2,256,256]{2,1,0:T(8,128)(2,1)S(1)} %bitcast.69, ...), kind=kOutput, calls=%fused_computation.25 | convolution fusion | flops 1617952256 | bytes 10782912 | tf_op jit(solution)/shard_map/klhn,khnp->klhp/dot_general | solution.py:94
  211.3 5.4 %all-gather.6.cloned.1.call-done = bf16[1024,4096]{1,0:T(8,128)(2,1)} async-done(((bf16[1024,128]{1,0:T(8,128)(2,1)}), bf16[1024,4096]{1,0:T(8,128)(2,1)}) %all-gather.6.cloned.1.call-update) | async-done | bytes 8388624 | tf_op jit(solution)/shard_map/all_gather | solution.py:107
  216.7 9.5 %convolution_convert_fusion = bf16[512,4096]{1,0:T(8,128)(2,1)} fusion(bf16[512,1024]{0,1:T(8,128)(2,1)S(1)} %multiply_convert_fusion.4, bf16[1024,4096]{1,0:T(8,128)(2,1)} %all-gather.6.cloned.1.call-done), kind=kOutput, calls=%fused_computation.7 | convolution fusion | flops 4297064448 | bytes 13631488 | tf_op jit(solution)/shard_map/dot_general | solution.py:105
  228.2 67.4 %reduce-scatter.2.cloned.1.call-done = bf16[64,4096]{1,0:T(8,128)(2,1)} async-done(((bf16[512,4096]{1,0:T(8,128)(2,1)}), bf16[64,4096]{1,0:T(8,128)(2,1)}) %reduce-scatter.2.cloned.1.call-update) | async-done | bytes 524304 | tf_op jit(solution)/shard_map/reduce_scatter | solution.py:110
  300.1 54.1 %all-gather.8.cloned.1.call-done = bf16[512,4096]{1,0:T(8,128)(2,1)} async-done(((bf16[64,4096]{1,0:T(8,128)(2,1)}), bf16[512,4096]{1,0:T(8,128)(2,1)}) %all-gather.8.cloned.1.call-update) | async-done | bytes 4194320 | tf_op jit(solution)/shard_map/all_gather | solution.py:123
  354.2 10.1 %convolution_convert_fusion.1 = bf16[512,1024]{1,0:T(8,128)(2,1)} fusion(bf16[512,4096]{1,0:T(8,128)(2,1)} %all-gather.8.cloned.1.call-done, bf16[4096,1024]{1,0:T(8,128)(2,1)} %all-gather.4.cloned.1.call-done), kind=kOutput, calls=%fused_computation.29 | convolution fusion | flops 4295491584 | bytes 13631488 | tf_op jit(solution)/shard_map/dot_general | solution.py:124
  (87 shorter events, 47.6 us)
Async XLA Ops:
  7.2 155.2 %copy-start = (bf16[512,1,256]{2,0,1:T(8,128)(2,1)S(1)}, bf16[512,1,256]{2,0,1:T(8,128)(2,1)}, u32[]{:S(2)}) copy-start(bf16[512,1,256]{2,0,1:T(8,128)(2,1)} %param.17) | copy-start | bytes 786436
  7.2 204.2 %all-gather.4.cloned.1.call-start = ((), (), s32[]{:S(2)}) async-start(), calls=%async_computation.1 | async-start | bytes 8650752 | tf_op jit(solution)/shard_map/all_gather | solution.py:103
  7.9 208.8 %all-gather.6.cloned.1.call-start = ((), (), s32[]{:S(2)}) async-start(), calls=%async_computation.2 | async-start | bytes 8650752 | tf_op jit(solution)/shard_map/all_gather | solution.py:107
  8.7 287.0 %reduce-scatter.2.cloned.1.call-start = ((), (), s32[]{:S(2)}) async-start(), calls=%async_computation.3 | async-start | bytes 4718592 | tf_op jit(solution)/shard_map/reduce_scatter | solution.py:110
  24.9 3.1 copy-start.2
  28.5 2.9 copy-start.2
  33.1 129.2 %copy-start.6 = (bf16[512,1,256]{2,0,1:T(8,128)(2,1)S(1)}, bf16[512,1,256]{2,0,1:T(8,128)(2,1)}, u32[]{:S(2)}) copy-start(bf16[512,1,256]{2,0,1:T(8,128)(2,1)} %param.16) | copy-start | bytes 786436
  33.1 16.0 %collective-permute-start.5 = (bf16[16,256,64]{1,2,0:T(8,128)(2,1)}, bf16[16,256,64]{1,2,0:T(8,128)(2,1)S(1)}, u32[]{:S(2)}, u32[]{:S(2)}) collective-permute-start(bf16[16,256,64]{1,2,0:T(8,128)(2,1)} %copy.53), channel_id=1, source_target_pairs={{0,8},{8,16},{16,24},{24,32},{32,40},{40,48},{48,56},{56,64},{64,7... | collective-permute-start | bytes 1572872 | tf_op jit(solution)/shard_map/ppermute | solution.py:17
  49.1 39.3 %collective-permute-start.6 = (bf16[16,256,64]{1,2,0:T(8,128)(2,1)S(1)}, bf16[16,256,64]{1,2,0:T(8,128)(2,1)S(1)}, u32[]{:S(2)}, u32[]{:S(2)}) collective-permute-start(bf16[16,256,64]{1,2,0:T(8,128)(2,1)S(1)} %collective-permute-done.5), channel_id=1, source_target_pairs={{0,8},{8,16},{16,24},{24,32},{32,40},{40,48},{48,56},{56,64},{64,7... | collective-permute-start | bytes 1572872 | tf_op jit(solution)/shard_map/ppermute | solution.py:17
  54.3 28.2 %collective-permute-start = (f32[16]{0:T(128)S(1)}, f32[16]{0:T(128)S(1)}, u32[]{:S(2)}, u32[]{:S(2)}) collective-permute-start(f32[16]{0:T(128)S(1)} %get-tuple-element.74), channel_id=1, source_target_pairs={{0,8},{8,16},{16,24},{24,32},{32,40},{40,48},{48,56},{56,64},{64,7... | collective-permute-start | bytes 200 | tf_op jit(solution)/shard_map/ppermute | solution.py:16
  82.4 5.9 %collective-permute-start.1 = (f32[16]{0:T(128)S(1)}, f32[16]{0:T(128)S(1)}, u32[]{:S(2)}, u32[]{:S(2)}) collective-permute-start(f32[16]{0:T(128)S(1)} %collective-permute-done), channel_id=1, source_target_pairs={{0,8},{8,16},{16,24},{24,32},{32,40},{40,48},{48,56},{56,64},{64,7... | collective-permute-start | bytes 200 | tf_op jit(solution)/shard_map/ppermute | solution.py:16
  88.6 23.7 %collective-permute-start.7 = (bf16[16,256,64]{1,2,0:T(8,128)(2,1)S(1)}, bf16[16,256,64]{1,2,0:T(8,128)(2,1)S(1)}, u32[]{:S(2)}, u32[]{:S(2)}) collective-permute-start(bf16[16,256,64]{1,2,0:T(8,128)(2,1)S(1)} %fusion.27), channel_id=1, source_target_pairs={{0,16},{8,24},{16,32},{24,40},{32,48},{40,56},{48,64},{56,72},{64,... | collective-permute-start | bytes 1572872 | tf_op jit(solution)/shard_map/ppermute | solution.py:17
  112.8 43.8 %collective-permute-start.8 = (bf16[16,256,64]{1,2,0:T(8,128)(2,1)S(1)}, bf16[16,256,64]{1,2,0:T(8,128)(2,1)S(1)}, u32[]{:S(2)}, u32[]{:S(2)}) collective-permute-start(bf16[16,256,64]{1,2,0:T(8,128)(2,1)S(1)} %fusion.31), channel_id=1, source_target_pairs={{0,32},{8,40},{16,48},{24,56},{32,64},{40,72},{48,80},{56,88},{64,... | collective-permute-start | bytes 1572872 | tf_op jit(solution)/shard_map/ppermute | solution.py:17
  116.3 40.2 %collective-permute-start.2 = (f32[16]{0:T(128)S(1)}, f32[16]{0:T(128)S(1)}, u32[]{:S(2)}, u32[]{:S(2)}) collective-permute-start(f32[16]{0:T(128)S(1)} %get-tuple-element.93), channel_id=1, source_target_pairs={{0,16},{8,24},{16,32},{24,40},{32,48},{40,56},{48,64},{56,72},{64,... | collective-permute-start | bytes 200 | tf_op jit(solution)/shard_map/ppermute | solution.py:16
  157.0 17.9 %collective-permute-start.9 = (bf16[16,256,64]{1,2,0:T(8,128)(2,1)S(1)}, bf16[16,256,64]{1,2,0:T(8,128)(2,1)S(1)}, u32[]{:S(2)}, u32[]{:S(2)}) collective-permute-start(bf16[16,256,64]{1,2,0:T(8,128)(2,1)S(1)} %fusion.28), channel_id=1, source_target_pairs={{0,64},{8,72},{16,80},{24,88},{32,96},{40,104},{48,112},{56,120},{... | collective-permute-start | bytes 1572872 | tf_op jit(solution)/shard_map/ppermute | solution.py:17
  162.6 4.7 %collective-permute-start.3 = (f32[16]{0:T(128)S(1)}, f32[16]{0:T(128)S(1)}, u32[]{:S(2)}, u32[]{:S(2)}) collective-permute-start(f32[16]{0:T(128)S(1)} %get-tuple-element.91), channel_id=1, source_target_pairs={{0,32},{8,40},{16,48},{24,56},{32,64},{40,72},{48,80},{56,88},{64,... | collective-permute-start | bytes 200 | tf_op jit(solution)/shard_map/ppermute | solution.py:16
  177.1 19.4 %collective-permute-start.10 = (bf16[16,256,64]{1,2,0:T(8,128)(2,1)}, bf16[16,256,64]{1,2,0:T(8,128)(2,1)}, u32[]{:S(2)}, u32[]{:S(2)}) collective-permute-start(bf16[16,256,64]{1,2,0:T(8,128)(2,1)} %fusion.30), channel_id=1, source_target_pairs={{0,128},{8,136},{16,144},{24,152},{32,160},{40,168},{48,176},{56,1... | collective-permute-start | bytes 1572872 | tf_op jit(solution)/shard_map/ppermute | solution.py:17
  190.3 6.2 %collective-permute-start.4 = (f32[16]{0:T(128)S(1)}, f32[16]{0:T(128)S(1)}, u32[]{:S(2)}, u32[]{:S(2)}) collective-permute-start(f32[16]{0:T(128)S(1)} %get-tuple-element.89), channel_id=1, source_target_pairs={{0,64},{8,72},{16,80},{24,88},{32,96},{40,104},{48,112},{56,120},{... | collective-permute-start | bytes 200 | tf_op jit(solution)/shard_map/ppermute | solution.py:16
  196.5 4.7 %copy-start.10 = (f32[16]{0:T(128)S(1)}, f32[16]{0:T(128)}, u32[]{:S(2)}) copy-start(f32[16]{0:T(128)} %param.19) | copy-start | bytes 196
  226.2 69.4 %copy-start.3 = (bf16[64,4096]{1,0:T(8,128)(2,1)S(1)}, bf16[64,4096]{1,0:T(8,128)(2,1)}, u32[]{:S(2)}) copy-start(bf16[64,4096]{1,0:T(8,128)(2,1)} %param.22) | copy-start | bytes 1572868
  226.2 72.9 %copy-start.8 = (f32[4096]{0:T(1024)S(1)}, f32[4096]{0:T(1024)}, u32[]{:S(2)}) copy-start(f32[4096]{0:T(1024)} %param.24) | copy-start | bytes 49156
  226.2 128.0 %all-gather.8.cloned.1.call-start = ((), (), s32[]{:S(2)}) async-start(), calls=%async_computation.4 | async-start | bytes 4718592 | tf_op jit(solution)/shard_map/all_gather | solution.py:123
  299.1 65.3 %copy-start.4 = (bf16[64,4096]{1,0:T(8,128)(2,1)}, bf16[64,4096]{1,0:T(8,128)(2,1)S(1)}, u32[]{:S(2)}) copy-start(bf16[64,4096]{1,0:T(8,128)(2,1)S(1)} %get-tuple-element.87) | copy-start | bytes 1572868
  354.2 10.2 %copy-start.1 = (bf16[512,1,256]{2,0,1:T(8,128)(2,1)S(1)}, bf16[512,1,256]{2,0,1:T(8,128)(2,1)}, u32[]{:S(2)}) copy-start(bf16[512,1,256]{2,0,1:T(8,128)(2,1)} %param.17) | copy-start | bytes 786436
  (3 other events, 3.4 us)
Sparse Core Ops, SparseCore 0:
  10.6 88.9 all-gather.3
  102.0 114.6 all-gather.5
  226.3 69.2 reduce-scatter.1
  300.2 53.9 all-gather.7

commit v2 on v1

--- a/solution.py
+++ b/solution.py
@@ -1,7 +1,7 @@
 import jax
 import jax.numpy as jnp
 from jax import lax
-from jax.sharding import PartitionSpec as P
+from jax.sharding import Mesh, PartitionSpec as P
 
 SPAN = 256
 
@@ -23,6 +23,15 @@
         acc = carry_combine(shifted(acc, distance), acc)
         distance *= 2
     return acc
+
+
+def gather_pairs(part, axis):
+    across = lax.all_gather(part, "chip", axis=0)
+    both = lax.all_gather(across, "core", axis=1)
+    both = jnp.moveaxis(both, (0, 1), (axis, axis + 1))
+    shape = list(part.shape)
+    shape[axis] = -1
+    return both.reshape(shape)
 
 
 def carry_combine(earlier, later):
@@ -87,7 +96,7 @@
     zero_state = jnp.zeros((head_count, state_width, head_width), jnp.float32)
     device_state, local_starts = lax.scan(advance, zero_state, (block_decay, block_state))
     device_decay = jnp.sum(block_decay, axis=0)
-    total_decay, incoming = shift_scan(device_decay, device_state, "seq")
+    total_decay, incoming = shift_scan(device_decay, device_state, ("chip", "core"))
     before_block = jnp.cumsum(block_decay, axis=0) - block_decay
     starts = local_starts + jnp.exp(before_block)[:, :, None, None] * incoming[None]
     c_heads = jnp.repeat(c_grouped, per_group, axis=2).astype(jnp.float32)
@@ -100,15 +109,15 @@
     grouped = gated.reshape(seq_rows, group_count, per_group * head_width)
     grouped = grouped * lax.rsqrt(jnp.mean(grouped * grouped, axis=-1, keepdims=True) + 1e-05)
     ssd_out = (grouped.reshape(seq_rows, channels) * norm_gain[None, :]).astype(jnp.bfloat16)
-    w_in_all = lax.all_gather(w_in, "seq", axis=0, tiled=True)
+    w_in_all = gather_pairs(w_in, 0)
     ssd_out, w_in_all = lax.optimization_barrier((ssd_out, w_in_all))
     partial_sum = jnp.dot(
         ssd_out,
-        lax.all_gather(w_out, "seq", axis=1, tiled=True),
+        gather_pairs(w_out, 1),
         preferred_element_type=jnp.float32,
     )
     mixer_out = lax.psum_scatter(
-        partial_sum.astype(jnp.bfloat16), "head", scatter_dimension=0, tiled=True
+        partial_sum.astype(jnp.bfloat16), ("zlo", "x"), scatter_dimension=0, tiled=True
     ).astype(jnp.float32)
     unit = refusal / jnp.sqrt(jnp.sum(refusal * refusal) + 1e-06)
     hidden = residual.astype(jnp.float32) + mixer_out
@@ -120,7 +129,7 @@
         * lax.rsqrt(jnp.mean(stream_float * stream_float, axis=-1, keepdims=True) + 1e-05)
         * stream_gain[None, :]
     ).astype(jnp.bfloat16)
-    all_rows = lax.all_gather(normed, "head", axis=0, tiled=True)
+    all_rows = lax.all_gather(normed, ("zlo", "x"), axis=0, tiled=True)
     next_float = jnp.dot(
         all_rows,
         w_in_all,
@@ -131,18 +140,22 @@
 
 def solution(mesh):
     in_specs = (
-        P("seq", "head"),
-        P("seq", "head"),
-        P("seq", "head", None),
-        P("seq", "head", None),
-        P("seq", "head"),
-        P("head"),
-        P("head"),
-        P("head", "seq"),
-        P(("seq", "head"), None),
+        P(("chip", "core"), ("zlo", "x")),
+        P(("chip", "core"), ("zlo", "x")),
+        P(("chip", "core"), ("zlo", "x"), None),
+        P(("chip", "core"), ("zlo", "x"), None),
+        P(("chip", "core"), ("zlo", "x")),
+        P(("zlo", "x")),
+        P(("zlo", "x")),
+        P(("zlo", "x"), ("chip", "core")),
+        P(("chip", "core", "zlo", "x"), None),
         P(),
         P(),
-        P("seq", "head"),
+        P(("chip", "core"), ("zlo", "x")),
     )
-    out_specs = (P(("seq", "head"), None), P("seq", "head"))
-    return jax.shard_map(body, mesh=mesh, in_specs=in_specs, out_specs=out_specs, check_vma=False)
+    out_specs = (P(("chip", "core", "zlo", "x"), None), P(("chip", "core"), ("zlo", "x")))
+    seq_size, head_size = mesh.devices.shape
+    split = Mesh(
+        mesh.devices.reshape(seq_size // 2, 2, 2, head_size // 2), ("chip", "core", "zlo", "x")
+    )
+    return jax.shard_map(body, mesh=split, in_specs=in_specs, out_specs=out_specs, check_vma=False)

time: 372 us -> 488 us (1.31)
  waiting for transfers between devices: 217 us -> 301 us
  starting transfers between devices: 58.7 us -> 80.8 us
  local copies, waits for them, and re-layouts: 25.5 us -> 35.3 us
    all_gather x3 -> x5, waiting for transfers between devices: 59.4 us -> 204 us  [the longest x2 150 us: gather_pairs(): across = lax.all_gather(part, 'chip', axis=0)]
    ppermute x5, waiting for transfers between devices: 59.5 us -> 15.9 us  [shifted(): lax.ppermute(a, axis, pairs)]
    ppermute x6, starting transfers between devices: 37.3 us -> 60.9 us  [shifted(): lax.ppermute(s.astype(jnp.bfloat16), axis, pairs).astype(jnp.float32)]
    reduce_scatter x1, waiting for transfers between devices: 67.4 us -> 54.9 us  [body(): lax.psum_scatter(partial_sum.astype(jnp.bfloat16), ('zlo', 'x'), scatter_...]
    transpose x0 -> x1, local copies, waits for them, and re-layouts: none -> 12.3 us  [gather_pairs(): both = jnp.moveaxis(both, (0, 1), (axis, axis + 1))]
  transfers between devices with their start and end apart: 15 -> 17, of which waited for: 10 -> 11; matrix products, arithmetic and copies ran while one was open for 14% -> 10% of each run, Pallas kernels for 0% -> 0%
where the time goes in v2:
time: 488 us; the launch traced here: 487 us
  waiting for transfers between devices  301 us (62%)
  starting transfers between devices  80.8 us (17%)
  matrix products  38.6 us (8%)
  local copies, waits for them, and re-layouts  35.3 us (7%)
  other arithmetic  16.6 us (3%)
  between operations  15.2 us (3%)
    all_gather x2, waiting for transfers between devices, gather_pairs(): across = lax.all_gather(part, 'chip', axis=0)  150 us
    ppermute x6, starting transfers between devices, shifted(): lax.ppermute(s.astype(jnp.bfloat16), axis, pairs).astype(jnp.float32)  60.9 us
    reduce_scatter x1, waiting for transfers between devices, body(): lax.psum_scatter(partial_sum.astype(jnp.bfloat16), ('zlo', 'x'), scatter_...  54.9 us
    all_gather x1, waiting for transfers between devices, body(): all_rows = lax.all_gather(normed, ('zlo', 'x'), axis=0, tiled=True)  54.1 us
    ppermute x6, waiting for transfers between devices, shifted(): lax.ppermute(s.astype(jnp.bfloat16), axis, pairs).astype(jnp.float32)  24.6 us
    ppermute x5, starting transfers between devices, shifted(): lax.ppermute(a, axis, pairs)  19.4 us
    ppermute x5, waiting for transfers between devices, shifted(): lax.ppermute(a, axis, pairs)  15.9 us
    transpose x1, local copies, waits for them, and re-layouts, gather_pairs(): both = jnp.moveaxis(both, (0, 1), (axis, axis + 1))  12.3 us
  transfers between devices with their start and end apart: 17, of which 11 were waited for; matrix products, arithmetic and copies ran while one was open for 10% of the time, Pallas kernels for 0%

profile of v2, /device:TPU:1, one launch (start us, length us, event | category | flops | bytes accessed | tf_op | source)
XLA Modules:
  0.0 487.1 jit_solution(14526635348454765277)
XLA Ops:
  8.7 80.3 %all-gather.12.cloned.1.call-done = bf16[2048,1024]{1,0:T(8,128)(2,1)} async-done(((bf16[128,1024]{1,0:T(8,128)(2,1)}), bf16[2048,1024]{1,0:T(8,128)(2,1)}) %all-gather.12.cloned.1.call-update) | async-done | bytes 4194320 | tf_op jit(solution)/shard_map/all_gather | solution.py:29
  97.8 69.4 %all-gather.16.cloned.1.call-done = bf16[16384,128]{1,0:T(8,128)(2,1)} async-done(((bf16[1024,128]{1,0:T(8,128)(2,1)}), bf16[16384,128]{1,0:T(8,128)(2,1)}) %all-gather.16.cloned.1.call-update) | async-done | bytes 4194320 | tf_op jit(solution)/shard_map/all_gather | solution.py:29
  167.3 5.1 %fusion.3 = f32[2,16,256,64]{3,2,1,0:T(8,128)} fusion(bf16[2,256,16,64]{1,3,2,0:T(8,128)(2,1)S(1)} %copy.51, f32[2,256,16]{1,2,0:T(8,128)S(1)} %get-tuple-element.95, f32[2,256,256]{2,1,0:T(8,128)} %convert_element_type.80), kind=kOutput, calls=%fused_computation.9 | convolution fusion | flops 272629760 | bytes 3702784 | tf_op jit(solution)/shard_map/klhn,klhp->khnp/dot_general | solution.py:87
  172.4 6.9 %while.13 = (s32[]{:T(128)}, f32[16,256,64]{2,1,0:T(8,128)S(1)}, f32[2,16,256,64]{3,2,1,0:T(8,128)}, f32[2,16]{1,0:T(2,128)S(1)}, f32[2,16,256,64]{3,2,1,0:T(8,128)}, /*index=5*/s32[]{:T(128)}, s32[]{:T(128)}) while((s32[]{:T(128)}, f32[16,256,64]{2,1,0:T(8,128)S(1)}, f32[2,16,256,64]{3,2,1,0:T(8,128)}, f32[2,16]{1,0:T(2,128)S(1)}, ...), condition=%wide.region_3.4_spmd.clone, body=%wide.region_2.3_spmd.clone.sunk | while | flops 1048579 | bytes 14680892 | solution.py:97
  180.5 7.6 %collective-permute-start.5 = (bf16[16,256,64]{1,2,0:T(8,128)(2,1)}, bf16[16,256,64]{1,2,0:T(8,128)(2,1)S(1)}, u32[]{:S(2)}, u32[]{:S(2)}) collective-permute-start(bf16[16,256,64]{1,2,0:T(8,128)(2,1)} %copy.54), channel_id=1, source_target_pairs={{0,8},{8,16},{16,24},{24,32},{32,40},{40,48},{48,56},{56,64},{64,7... | collective-permute-start | bytes 1572872 | tf_op jit(solution)/shard_map/ppermute | solution.py:17
  188.1 8.7 %collective-permute-done.5 = bf16[16,256,64]{1,2,0:T(8,128)(2,1)S(1)} collective-permute-done((bf16[16,256,64]{1,2,0:T(8,128)(2,1)}, bf16[16,256,64]{1,2,0:T(8,128)(2,1)S(1)}, u32[]{:S(2)}, u32[]{:S(2)}) %collective-permute-start.5) | collective-permute-done | bytes 524320 | tf_op jit(solution)/shard_map/ppermute | solution.py:17
  196.7 5.2 %collective-permute-start.6 = (bf16[16,256,64]{1,2,0:T(8,128)(2,1)S(1)}, bf16[16,256,64]{1,2,0:T(8,128)(2,1)S(1)}, u32[]{:S(2)}, u32[]{:S(2)}) collective-permute-start(bf16[16,256,64]{1,2,0:T(8,128)(2,1)S(1)} %collective-permute-done.5), channel_id=1, source_target_pairs={{0,8},{8,16},{16,24},{24,32},{32,40},{40,48},{48,56},{56,64},{64,7... | collective-permute-start | bytes 1572872 | tf_op jit(solution)/shard_map/ppermute | solution.py:17
  203.9 4.3 collective-permute-done
  208.1 5.4 %collective-permute-start.1 = (f32[16]{0:T(128)S(1)}, f32[16]{0:T(128)S(1)}, u32[]{:S(2)}, u32[]{:S(2)}) collective-permute-start(f32[16]{0:T(128)S(1)} %collective-permute-done), channel_id=1, source_target_pairs={{0,8},{8,16},{16,24},{24,32},{32,40},{40,48},{48,56},{56,64},{64,7... | collective-permute-start | bytes 200 | tf_op jit(solution)/shard_map/ppermute | solution.py:16
  214.4 11.7 %collective-permute-start.7 = (bf16[16,256,64]{1,2,0:T(8,128)(2,1)S(1)}, bf16[16,256,64]{1,2,0:T(8,128)(2,1)S(1)}, u32[]{:S(2)}, u32[]{:S(2)}) collective-permute-start(bf16[16,256,64]{1,2,0:T(8,128)(2,1)S(1)} %fusion.27), channel_id=1, source_target_pairs={{0,16},{8,24},{16,32},{24,40},{32,48},{40,56},{48,64},{56,72},{64,... | collective-permute-start | bytes 1572872 | tf_op jit(solution)/shard_map/ppermute | solution.py:17
  226.1 12.7 %collective-permute-done.7 = bf16[16,256,64]{1,2,0:T(8,128)(2,1)S(1)} collective-permute-done((bf16[16,256,64]{1,2,0:T(8,128)(2,1)S(1)}, bf16[16,256,64]{1,2,0:T(8,128)(2,1)S(1)}, u32[]{:S(2)}, u32[]{:S(2)}) %collective-permute-start.7) | collective-permute-done | bytes 524320 | tf_op jit(solution)/shard_map/ppermute | solution.py:17
  239.3 16.5 %collective-permute-start.8 = (bf16[16,256,64]{1,2,0:T(8,128)(2,1)S(1)}, bf16[16,256,64]{1,2,0:T(8,128)(2,1)S(1)}, u32[]{:S(2)}, u32[]{:S(2)}) collective-permute-start(bf16[16,256,64]{1,2,0:T(8,128)(2,1)S(1)} %fusion.31), channel_id=1, source_target_pairs={{0,32},{8,40},{16,48},{24,56},{32,64},{40,72},{48,80},{56,88},{64,... | collective-permute-start | bytes 1572872 | tf_op jit(solution)/shard_map/ppermute | solution.py:17
  255.8 4.7 collective-permute-start.2
  260.5 10.3 %collective-permute-done.2 = f32[16]{0:T(128)S(1)} collective-permute-done((f32[16]{0:T(128)S(1)}, f32[16]{0:T(128)S(1)}, u32[]{:S(2)}, u32[]{:S(2)}) %collective-permute-start.2) | collective-permute-done | bytes 96 | tf_op jit(solution)/shard_map/ppermute | solution.py:16
  271.3 11.5 %collective-permute-start.9 = (bf16[16,256,64]{1,2,0:T(8,128)(2,1)S(1)}, bf16[16,256,64]{1,2,0:T(8,128)(2,1)S(1)}, u32[]{:S(2)}, u32[]{:S(2)}) collective-permute-start(bf16[16,256,64]{1,2,0:T(8,128)(2,1)S(1)} %fusion.28), channel_id=1, source_target_pairs={{0,64},{8,72},{16,80},{24,88},{32,96},{40,104},{48,112},{56,120},{... | collective-permute-start | bytes 1572872 | tf_op jit(solution)/shard_map/ppermute | solution.py:17
  283.1 5.6 %collective-permute-start.3 = (f32[16]{0:T(128)S(1)}, f32[16]{0:T(128)S(1)}, u32[]{:S(2)}, u32[]{:S(2)}) collective-permute-start(f32[16]{0:T(128)S(1)} %get-tuple-element.91), channel_id=1, source_target_pairs={{0,32},{8,40},{16,48},{24,56},{32,64},{40,72},{48,80},{56,88},{64,... | collective-permute-start | bytes 200 | tf_op jit(solution)/shard_map/ppermute | solution.py:16
  295.4 8.4 %collective-permute-start.10 = (bf16[16,256,64]{1,2,0:T(8,128)(2,1)}, bf16[16,256,64]{1,2,0:T(8,128)(2,1)}, u32[]{:S(2)}, u32[]{:S(2)}) collective-permute-start(bf16[16,256,64]{1,2,0:T(8,128)(2,1)} %fusion.30), channel_id=1, source_target_pairs={{0,128},{8,136},{16,144},{24,152},{32,160},{40,168},{48,176},{56,1... | collective-permute-start | bytes 1572872 | tf_op jit(solution)/shard_map/ppermute | solution.py:17
  313.9 4.6 copy.60
  323.2 7.3 %multiply_reduce_fusion = (f32[2,256]{1,0:T(2,128)S(1)}, f32[2,256,16,64]{1,3,2,0:T(8,128)S(1)}) fusion(f32[2,256,16,64]{1,3,2,0:T(8,128)} %copy.60, bf16[2,256,16,64]{1,3,2,0:T(8,128)(2,1)S(1)} %copy.51, f32[16]{0:T(128)S(1)} %copy-done.15, f32[2,256,16]{1,2,0:T(8,128)S(1)} %get-tuple-element.94, bf16[2,256,256]{2,1,0:T(8,128)(2,1)S(1)} %bitcast.76, ...), kind=kOutput, calls=%fused_computation.25 | convolution fusion | flops 1617952256 | bytes 10782912 | tf_op jit(solution)/shard_map/klhn,khnp->klhp/dot_general | solution.py:103
  332.7 12.3 %copy.62 = bf16[1024,16,2,128]{0,3,2,1:T(8,128)(2,1)} copy(bf16[1024,16,2,128]{3,0,2,1:T(8,128)(2,1)} %bitcast.77) | data formatting | bytes 16777216 | tf_op jit(solution)/shard_map/transpose | solution.py:31
  345.0 9.6 %convolution_convert_fusion = bf16[512,4096]{1,0:T(8,128)(2,1)} fusion(bf16[512,1024]{0,1:T(8,128)(2,1)S(1)} %multiply_convert_fusion.4, bf16[1024,4096]{0,1:T(8,128)(2,1)} %bitcast.78), kind=kOutput, calls=%fused_computation.7 | convolution fusion | flops 4297064448 | bytes 13631488 | tf_op jit(solution)/shard_map/dot_general | solution.py:114
  356.7 54.9 %reduce-scatter.2.cloned.1.call-done = bf16[64,4096]{1,0:T(8,128)(2,1)} async-done(((bf16[512,4096]{1,0:T(8,128)(2,1)}), bf16[64,4096]{1,0:T(8,128)(2,1)}) %reduce-scatter.2.cloned.1.call-update) | async-done | bytes 524304 | tf_op jit(solution)/shard_map/reduce_scatter | solution.py:119
  416.0 54.1 %all-gather.10.cloned.1.call-done = bf16[512,4096]{1,0:T(8,128)(2,1)} async-done(((bf16[64,4096]{1,0:T(8,128)(2,1)}), bf16[512,4096]{1,0:T(8,128)(2,1)}) %all-gather.10.cloned.1.call-update) | async-done | bytes 4194320 | tf_op jit(solution)/shard_map/all_gather | solution.py:132
  470.1 10.1 %convolution_convert_fusion.1 = bf16[512,1024]{1,0:T(8,128)(2,1)} fusion(bf16[512,4096]{1,0:T(8,128)(2,1)} %all-gather.10.cloned.1.call-done, bf16[4096,1024]{1,0:T(8,128)(2,1)} %bitcast.88), kind=kOutput, calls=%fused_computation.29 | convolution fusion | flops 4295491584 | bytes 13631488 | tf_op jit(solution)/shard_map/dot_general | solution.py:133
  (104 shorter events, 51.6 us)
Async XLA Ops:
  7.2 275.6 %copy-start = (bf16[512,1,256]{2,0,1:T(8,128)(2,1)S(1)}, bf16[512,1,256]{2,0,1:T(8,128)(2,1)}, u32[]{:S(2)}) copy-start(bf16[512,1,256]{2,0,1:T(8,128)(2,1)} %param.17) | copy-start | bytes 786436
  7.2 81.9 %copy-start.9 = (f32[512,16]{0,1:T(8,128)S(1)}, f32[512,16]{0,1:T(8,128)}, u32[]{:S(2)}) copy-start(f32[512,16]{0,1:T(8,128)} %param.18) | copy-start | bytes 98308
  7.2 83.3 %copy-start.6 = (bf16[512,1024]{1,0:T(8,128)(2,1)S(1)}, bf16[512,1024]{1,0:T(8,128)(2,1)}, u32[]{:S(2)}) copy-start(bf16[512,1024]{1,0:T(8,128)(2,1)} %param.14) | copy-start | bytes 3145732
  7.2 81.8 %all-gather.12.cloned.1.call-start = ((), (), s32[]{:S(2)}) async-start(), calls=%async_computation.3 | async-start | bytes 4456448 | tf_op jit(solution)/shard_map/all_gather | solution.py:29
  7.9 159.3 %all-gather.16.cloned.1.call-start = ((), (), s32[]{:S(2)}) async-start(), calls=%async_computation.5 | async-start | bytes 4456448 | tf_op jit(solution)/shard_map/all_gather | solution.py:29
  8.7 324.0 %all-gather.14.cloned.1.call-start = ((), (), s32[]{:S(2)}) async-start(), calls=%async_computation.4 | async-start | bytes 12582912 | tf_op jit(solution)/shard_map/all_gather | solution.py:30
  89.0 243.7 %all-gather.18.cloned.1.call-start = ((), (), s32[]{:S(2)}) async-start(), calls=%async_computation.6 | async-start | bytes 12582912 | tf_op jit(solution)/shard_map/all_gather | solution.py:30
  167.2 244.3 %reduce-scatter.2.cloned.1.call-start = ((), (), s32[]{:S(2)}) async-start(), calls=%async_computation.1 | async-start | bytes 4718592 | tf_op jit(solution)/shard_map/reduce_scatter | solution.py:119
  180.5 102.3 %copy-start.7 = (bf16[512,1,256]{2,0,1:T(8,128)(2,1)S(1)}, bf16[512,1,256]{2,0,1:T(8,128)(2,1)}, u32[]{:S(2)}) copy-start(bf16[512,1,256]{2,0,1:T(8,128)(2,1)} %param.16) | copy-start | bytes 786436
  180.5 16.3 %collective-permute-start.5 = (bf16[16,256,64]{1,2,0:T(8,128)(2,1)}, bf16[16,256,64]{1,2,0:T(8,128)(2,1)S(1)}, u32[]{:S(2)}, u32[]{:S(2)}) collective-permute-start(bf16[16,256,64]{1,2,0:T(8,128)(2,1)} %copy.54), channel_id=1, source_target_pairs={{0,8},{8,16},{16,24},{24,32},{32,40},{40,48},{48,56},{56,64},{64,7... | collective-permute-start | bytes 1572872 | tf_op jit(solution)/shard_map/ppermute | solution.py:17
  196.7 17.4 %collective-permute-start.6 = (bf16[16,256,64]{1,2,0:T(8,128)(2,1)S(1)}, bf16[16,256,64]{1,2,0:T(8,128)(2,1)S(1)}, u32[]{:S(2)}, u32[]{:S(2)}) collective-permute-start(bf16[16,256,64]{1,2,0:T(8,128)(2,1)S(1)} %collective-permute-done.5), channel_id=1, source_target_pairs={{0,8},{8,16},{16,24},{24,32},{32,40},{40,48},{48,56},{56,64},{64,7... | collective-permute-start | bytes 1572872 | tf_op jit(solution)/shard_map/ppermute | solution.py:17
  201.9 6.2 %collective-permute-start = (f32[16]{0:T(128)S(1)}, f32[16]{0:T(128)S(1)}, u32[]{:S(2)}, u32[]{:S(2)}) collective-permute-start(f32[16]{0:T(128)S(1)} %get-tuple-element.74), channel_id=1, source_target_pairs={{0,8},{8,16},{16,24},{24,32},{32,40},{40,48},{48,56},{56,64},{64,7... | collective-permute-start | bytes 200 | tf_op jit(solution)/shard_map/ppermute | solution.py:16
  208.1 6.1 %collective-permute-start.1 = (f32[16]{0:T(128)S(1)}, f32[16]{0:T(128)S(1)}, u32[]{:S(2)}, u32[]{:S(2)}) collective-permute-start(f32[16]{0:T(128)S(1)} %collective-permute-done), channel_id=1, source_target_pairs={{0,8},{8,16},{16,24},{24,32},{32,40},{40,48},{48,56},{56,64},{64,7... | collective-permute-start | bytes 200 | tf_op jit(solution)/shard_map/ppermute | solution.py:16
  214.4 24.4 %collective-permute-start.7 = (bf16[16,256,64]{1,2,0:T(8,128)(2,1)S(1)}, bf16[16,256,64]{1,2,0:T(8,128)(2,1)S(1)}, u32[]{:S(2)}, u32[]{:S(2)}) collective-permute-start(bf16[16,256,64]{1,2,0:T(8,128)(2,1)S(1)} %fusion.27), channel_id=1, source_target_pairs={{0,16},{8,24},{16,32},{24,40},{32,48},{40,56},{48,64},{56,72},{64,... | collective-permute-start | bytes 1572872 | tf_op jit(solution)/shard_map/ppermute | solution.py:17
  239.3 31.5 %collective-permute-start.8 = (bf16[16,256,64]{1,2,0:T(8,128)(2,1)S(1)}, bf16[16,256,64]{1,2,0:T(8,128)(2,1)S(1)}, u32[]{:S(2)}, u32[]{:S(2)}) collective-permute-start(bf16[16,256,64]{1,2,0:T(8,128)(2,1)S(1)} %fusion.31), channel_id=1, source_target_pairs={{0,32},{8,40},{16,48},{24,56},{32,64},{40,72},{48,80},{56,88},{64,... | collective-permute-start | bytes 1572872 | tf_op jit(solution)/shard_map/ppermute | solution.py:17
  255.8 15.0 %collective-permute-start.2 = (f32[16]{0:T(128)S(1)}, f32[16]{0:T(128)S(1)}, u32[]{:S(2)}, u32[]{:S(2)}) collective-permute-start(f32[16]{0:T(128)S(1)} %get-tuple-element.93), channel_id=1, source_target_pairs={{0,16},{8,24},{16,32},{24,40},{32,48},{40,56},{48,64},{56,72},{64,... | collective-permute-start | bytes 200 | tf_op jit(solution)/shard_map/ppermute | solution.py:16
  271.3 21.9 %collective-permute-start.9 = (bf16[16,256,64]{1,2,0:T(8,128)(2,1)S(1)}, bf16[16,256,64]{1,2,0:T(8,128)(2,1)S(1)}, u32[]{:S(2)}, u32[]{:S(2)}) collective-permute-start(bf16[16,256,64]{1,2,0:T(8,128)(2,1)S(1)} %fusion.28), channel_id=1, source_target_pairs={{0,64},{8,72},{16,80},{24,88},{32,96},{40,104},{48,112},{56,120},{... | collective-permute-start | bytes 1572872 | tf_op jit(solution)/shard_map/ppermute | solution.py:17
  283.1 6.3 %collective-permute-start.3 = (f32[16]{0:T(128)S(1)}, f32[16]{0:T(128)S(1)}, u32[]{:S(2)}, u32[]{:S(2)}) collective-permute-start(f32[16]{0:T(128)S(1)} %get-tuple-element.91), channel_id=1, source_target_pairs={{0,32},{8,40},{16,48},{24,56},{32,64},{40,72},{48,80},{56,88},{64,... | collective-permute-start | bytes 200 | tf_op jit(solution)/shard_map/ppermute | solution.py:16
  295.4 23.1 %collective-permute-start.10 = (bf16[16,256,64]{1,2,0:T(8,128)(2,1)}, bf16[16,256,64]{1,2,0:T(8,128)(2,1)}, u32[]{:S(2)}, u32[]{:S(2)}) collective-permute-start(bf16[16,256,64]{1,2,0:T(8,128)(2,1)} %fusion.30), channel_id=1, source_target_pairs={{0,128},{8,136},{16,144},{24,152},{32,160},{40,168},{48,176},{56,1... | collective-permute-start | bytes 1572872 | tf_op jit(solution)/shard_map/ppermute | solution.py:17
  312.0 6.4 %collective-permute-start.4 = (f32[16]{0:T(128)S(1)}, f32[16]{0:T(128)S(1)}, u32[]{:S(2)}, u32[]{:S(2)}) collective-permute-start(f32[16]{0:T(128)S(1)} %copy-done.14), channel_id=1, source_target_pairs={{0,64},{8,72},{16,80},{24,88},{32,96},{40,104},{48,112},{56,120},{... | collective-permute-start | bytes 200 | tf_op jit(solution)/shard_map/ppermute | solution.py:16
  354.7 56.9 %copy-start.3 = (bf16[64,4096]{1,0:T(8,128)(2,1)S(1)}, bf16[64,4096]{1,0:T(8,128)(2,1)}, u32[]{:S(2)}) copy-start(bf16[64,4096]{1,0:T(8,128)(2,1)} %param.22) | copy-start | bytes 1572868
  354.7 60.4 %copy-start.10 = (f32[4096]{0:T(1024)S(1)}, f32[4096]{0:T(1024)}, u32[]{:S(2)}) copy-start(f32[4096]{0:T(1024)} %param.24) | copy-start | bytes 49156
  354.7 115.4 %all-gather.10.cloned.1.call-start = ((), (), s32[]{:S(2)}) async-start(), calls=%async_computation.2 | async-start | bytes 4718592 | tf_op jit(solution)/shard_map/all_gather | solution.py:132
  415.0 65.3 %copy-start.4 = (bf16[64,4096]{1,0:T(8,128)(2,1)}, bf16[64,4096]{1,0:T(8,128)(2,1)S(1)}, u32[]{:S(2)}) copy-start(bf16[64,4096]{1,0:T(8,128)(2,1)S(1)} %get-tuple-element.87) | copy-start | bytes 1572868
  (10 other events, 40.3 us)
Sparse Core Ops, SparseCore 0:
  10.5 78.4 all-gather.11
  91.4 75.7 all-gather.15
  169.0 26.9 all-gather.13
  197.7 26.4 all-gather.17
  354.8 56.6 reduce-scatter.1
  416.2 53.9 all-gather.9

commit v3 on v1

--- a/solution.py
+++ b/solution.py
@@ -30,7 +30,8 @@
     decay_later, state_later = later
     return (
         decay_early + decay_later,
-        jnp.exp(decay_later)[:, None, None] * state_early + state_later,
+        jnp.exp(decay_later).reshape((-1,) + (1,) * (state_later.ndim - 1)) * state_early
+        + state_later,
     )
 
 
@@ -87,7 +88,10 @@
     zero_state = jnp.zeros((head_count, state_width, head_width), jnp.float32)
     device_state, local_starts = lax.scan(advance, zero_state, (block_decay, block_state))
     device_decay = jnp.sum(block_decay, axis=0)
-    total_decay, incoming = shift_scan(device_decay, device_state, "seq")
+    total_decay, incoming = shift_scan(
+        device_decay, device_state.reshape(head_count, state_width * head_width), "seq"
+    )
+    incoming = incoming.reshape(head_count, state_width, head_width)
     before_block = jnp.cumsum(block_decay, axis=0) - block_decay
     starts = local_starts + jnp.exp(before_block)[:, :, None, None] * incoming[None]
     c_heads = jnp.repeat(c_grouped, per_group, axis=2).astype(jnp.float32)

time: 372 us -> 369 us (level)
  waiting for transfers between devices: 217 us -> 186 us
  starting transfers between devices: 58.7 us -> 83.8 us
    ppermute x5, waiting for transfers between devices: 59.5 us -> 29.4 us  [shifted(): lax.ppermute(a, axis, pairs)]
    ppermute x6, starting transfers between devices: 37.3 us -> 51.6 us  [shifted(): lax.ppermute(s.astype(jnp.bfloat16), axis, pairs).astype(jnp.float32)]
    ppermute x5, starting transfers between devices: 21.1 us -> 31.8 us  [shifted(): lax.ppermute(a, axis, pairs)]
    reduce_scatter x1, waiting for transfers between devices: 67.4 us -> 59 us  [body(): lax.psum_scatter(partial_sum.astype(jnp.bfloat16), 'head', scatter_dimens...]
    all_gather x1, waiting for transfers between devices: 5.35 us -> 12.1 us  [body(): lax.all_gather(w_out, 'seq', axis=1, tiled=True)]
  transfers between devices with their start and end apart: 15 -> 15, of which waited for: 10 -> 10; matrix products, arithmetic and copies ran while one was open for 14% -> 15% of each run, Pallas kernels for 0% -> 0%
where the time goes in v3:
time: 369 us; the launch traced here: 368 us
  waiting for transfers between devices  186 us (50%)
  starting transfers between devices  83.8 us (23%)
  matrix products  39.9 us (11%)
  local copies, waits for them, and re-layouts  26.8 us (7%)
  other arithmetic  16.1 us (4%)
  between operations  14.8 us (4%)
    reduce_scatter x1, waiting for transfers between devices, body(): lax.psum_scatter(partial_sum.astype(jnp.bfloat16), 'head', scatter_dimens...  59 us
    all_gather x1, waiting for transfers between devices, body(): all_rows = lax.all_gather(normed, 'head', axis=0, tiled=True)  54.1 us
    ppermute x6, starting transfers between devices, shifted(): lax.ppermute(s.astype(jnp.bfloat16), axis, pairs).astype(jnp.float32)  51.6 us
    ppermute x5, starting transfers between devices, shifted(): lax.ppermute(a, axis, pairs)  31.8 us
    ppermute x6, waiting for transfers between devices, shifted(): lax.ppermute(s.astype(jnp.bfloat16), axis, pairs).astype(jnp.float32)  31.1 us
    ppermute x5, waiting for transfers between devices, shifted(): lax.ppermute(a, axis, pairs)  29.4 us
    all_gather x1, waiting for transfers between devices, body(): lax.all_gather(w_out, 'seq', axis=1, tiled=True)  12.1 us
    dot_general x1, matrix products, body(): next_float = jnp.dot(all_rows, w_in_all, preferred_element_type=jnp.float32)  10.1 us
  transfers between devices with their start and end apart: 15, of which 10 were waited for; matrix products, arithmetic and copies ran while one was open for 15% of the time, Pallas kernels for 0%

profile of v3, /device:TPU:1, one launch (start us, length us, event | category | flops | bytes accessed | tf_op | source)
XLA Modules:
  0.0 367.9 jit_solution(4580815393495530185)
XLA Ops:
  19.3 5.1 %fusion.3 = f32[2,16,256,64]{3,2,1,0:T(8,128)} fusion(bf16[2,256,16,64]{1,3,2,0:T(8,128)(2,1)S(1)} %copy.37, f32[2,256,16]{1,2,0:T(8,128)S(1)} %get-tuple-element.90, f32[2,256,256]{2,1,0:T(8,128)} %convert_element_type.83), kind=kOutput, calls=%fused_computation.9 | convolution fusion | flops 272629760 | bytes 3702784 | tf_op jit(solution)/shard_map/klhn,klhp->khnp/dot_general | solution.py:79
  24.4 7.0 %while.13 = (s32[]{:T(128)}, f32[16,256,64]{2,1,0:T(8,128)S(1)}, f32[2,16,256,64]{3,2,1,0:T(8,128)}, f32[2,16]{1,0:T(2,128)S(1)}, f32[2,16,256,64]{3,2,1,0:T(8,128)}, /*index=5*/s32[]{:T(128)}, s32[]{:T(128)}) while((s32[]{:T(128)}, f32[16,256,64]{2,1,0:T(8,128)S(1)}, f32[2,16,256,64]{3,2,1,0:T(8,128)}, f32[2,16]{1,0:T(2,128)S(1)}, ...), condition=%wide.region_3.4_spmd.clone, body=%wide.region_2.3_spmd.clone.sunk | while | flops 1048579 | bytes 14680892 | solution.py:89
  32.4 6.3 %collective-permute-start.5 = (bf16[16,16384]{1,0:T(8,128)(2,1)S(1)}, bf16[16,16384]{1,0:T(8,128)(2,1)S(1)}, u32[]{:S(2)}, u32[]{:S(2)}) collective-permute-start(bf16[16,16384]{1,0:T(8,128)(2,1)S(1)} %convert_element_type.86), channel_id=1, source_target_pairs={{0,8},{8,16},{16,24},{24,32},{32,40},{40,48},{48,56},{56,64},{64,7... | collective-permute-start | bytes 1572872 | tf_op jit(solution)/shard_map/ppermute | solution.py:17
  38.8 11.5 %collective-permute-done.5 = bf16[16,16384]{1,0:T(8,128)(2,1)S(1)} collective-permute-done((bf16[16,16384]{1,0:T(8,128)(2,1)S(1)}, bf16[16,16384]{1,0:T(8,128)(2,1)S(1)}, u32[]{:S(2)}, u32[]{:S(2)}) %collective-permute-start.5) | collective-permute-done | bytes 524320 | tf_op jit(solution)/shard_map/ppermute | solution.py:17
  50.2 5.3 %collective-permute-start.6 = (bf16[16,16384]{1,0:T(8,128)(2,1)S(1)}, bf16[16,16384]{1,0:T(8,128)(2,1)S(1)}, u32[]{:S(2)}, u32[]{:S(2)}) collective-permute-start(bf16[16,16384]{1,0:T(8,128)(2,1)S(1)} %collective-permute-done.5), channel_id=1, source_target_pairs={{0,8},{8,16},{16,24},{24,32},{32,40},{40,48},{48,56},{56,64},{64,7... | collective-permute-start | bytes 1572872 | tf_op jit(solution)/shard_map/ppermute | solution.py:17
  58.7 23.5 %collective-permute-done = f32[16]{0:T(128)S(1)} collective-permute-done((f32[16]{0:T(128)S(1)}, f32[16]{0:T(128)S(1)}, u32[]{:S(2)}, u32[]{:S(2)}) %collective-permute-start) | collective-permute-done | bytes 96 | tf_op jit(solution)/shard_map/ppermute | solution.py:16
  82.3 6.7 %collective-permute-start.1 = (f32[16]{0:T(128)S(1)}, f32[16]{0:T(128)S(1)}, u32[]{:S(2)}, u32[]{:S(2)}) collective-permute-start(f32[16]{0:T(128)S(1)} %collective-permute-done), channel_id=1, source_target_pairs={{0,8},{8,16},{16,24},{24,32},{32,40},{40,48},{48,56},{56,64},{64,7... | collective-permute-start | bytes 200 | tf_op jit(solution)/shard_map/ppermute | solution.py:16
  89.9 7.6 %collective-permute-start.7 = (bf16[16,16384]{1,0:T(8,128)(2,1)S(1)}, bf16[16,16384]{1,0:T(8,128)(2,1)S(1)}, u32[]{:S(2)}, u32[]{:S(2)}) collective-permute-start(bf16[16,16384]{1,0:T(8,128)(2,1)S(1)} %fusion.27), channel_id=1, source_target_pairs={{0,16},{8,24},{16,32},{24,40},{32,48},{40,56},{48,64},{56,72},{64,... | collective-permute-start | bytes 1572872 | tf_op jit(solution)/shard_map/ppermute | solution.py:17
  97.6 15.2 %collective-permute-done.7 = bf16[16,16384]{1,0:T(8,128)(2,1)S(1)} collective-permute-done((bf16[16,16384]{1,0:T(8,128)(2,1)S(1)}, bf16[16,16384]{1,0:T(8,128)(2,1)S(1)}, u32[]{:S(2)}, u32[]{:S(2)}) %collective-permute-start.7) | collective-permute-done | bytes 524320 | tf_op jit(solution)/shard_map/ppermute | solution.py:17
  113.1 4.6 %collective-permute-start.8 = (bf16[16,16384]{1,0:T(8,128)(2,1)S(1)}, bf16[16,16384]{1,0:T(8,128)(2,1)S(1)}, u32[]{:S(2)}, u32[]{:S(2)}) collective-permute-start(bf16[16,16384]{1,0:T(8,128)(2,1)S(1)} %fusion.31), channel_id=1, source_target_pairs={{0,32},{8,40},{16,48},{24,56},{32,64},{40,72},{48,80},{56,88},{64,... | collective-permute-start | bytes 1572872 | tf_op jit(solution)/shard_map/ppermute | solution.py:17
  117.8 16.3 %collective-permute-start.2 = (f32[16]{0:T(128)S(1)}, f32[16]{0:T(128)S(1)}, u32[]{:S(2)}, u32[]{:S(2)}) collective-permute-start(f32[16]{0:T(128)S(1)} %get-tuple-element.88), channel_id=1, source_target_pairs={{0,16},{8,24},{16,32},{24,40},{32,48},{40,56},{48,64},{56,72},{64,... | collective-permute-start | bytes 200 | tf_op jit(solution)/shard_map/ppermute | solution.py:16
  134.1 4.4 %collective-permute-done.2 = f32[16]{0:T(128)S(1)} collective-permute-done((f32[16]{0:T(128)S(1)}, f32[16]{0:T(128)S(1)}, u32[]{:S(2)}, u32[]{:S(2)}) %collective-permute-start.2) | collective-permute-done | bytes 96 | tf_op jit(solution)/shard_map/ppermute | solution.py:16
  139.0 21.5 %collective-permute-start.9 = (bf16[16,16384]{1,0:T(8,128)(2,1)S(1)}, bf16[16,16384]{1,0:T(8,128)(2,1)S(1)}, u32[]{:S(2)}, u32[]{:S(2)}) collective-permute-start(bf16[16,16384]{1,0:T(8,128)(2,1)S(1)} %fusion.28), channel_id=1, source_target_pairs={{0,64},{8,72},{16,80},{24,88},{32,96},{40,104},{48,112},{56,120},{... | collective-permute-start | bytes 1572872 | tf_op jit(solution)/shard_map/ppermute | solution.py:17
  161.7 4.1 %collective-permute-start.3 = (f32[16]{0:T(128)S(1)}, f32[16]{0:T(128)S(1)}, u32[]{:S(2)}, u32[]{:S(2)}) collective-permute-start(f32[16]{0:T(128)S(1)} %get-tuple-element.86), channel_id=1, source_target_pairs={{0,32},{8,40},{16,48},{24,56},{32,64},{40,72},{48,80},{56,88},{64,... | collective-permute-start | bytes 200 | tf_op jit(solution)/shard_map/ppermute | solution.py:16
  166.5 4.4 %collective-permute-done.9 = bf16[16,16384]{1,0:T(8,128)(2,1)S(1)} collective-permute-done((bf16[16,16384]{1,0:T(8,128)(2,1)S(1)}, bf16[16,16384]{1,0:T(8,128)(2,1)S(1)}, u32[]{:S(2)}, u32[]{:S(2)}) %collective-permute-start.9) | collective-permute-done | bytes 524320 | tf_op jit(solution)/shard_map/ppermute | solution.py:17
  173.1 6.3 %collective-permute-start.10 = (bf16[16,16384]{1,0:T(8,128)(2,1)}, bf16[16,16384]{1,0:T(8,128)(2,1)}, u32[]{:S(2)}, u32[]{:S(2)}) collective-permute-start(bf16[16,16384]{1,0:T(8,128)(2,1)} %fusion.30), channel_id=1, source_target_pairs={{0,128},{8,136},{16,144},{24,152},{32,160},{40,168},{48,176},{56,1... | collective-permute-start | bytes 1572872 | tf_op jit(solution)/shard_map/ppermute | solution.py:17
  183.5 4.1 %reshape.166 = f32[2,256,16,64]{3,2,1,0:T(8,128)} reshape(bf16[512,1024]{1,0:T(8,128)(2,1)} %param.15) | data formatting | bytes 3145728 | tf_op jit(solution)/shard_map/convert_element_type | solution.py:102
  189.1 4.6 %copy.44 = f32[2,256,16,64]{1,3,2,0:T(8,128)} copy(f32[2,256,16,64]{3,2,1,0:T(8,128)} %reshape.166) | data formatting | bytes 4194304 | tf_op jit(solution)/shard_map/convert_element_type | solution.py:102
  200.0 7.9 %multiply_reduce_fusion = (f32[2,256]{1,0:T(2,128)S(1)}, f32[2,256,16,64]{1,3,2,0:T(8,128)S(1)}) fusion(f32[2,256,16,64]{1,3,2,0:T(8,128)} %copy.44, bf16[2,256,16,64]{1,3,2,0:T(8,128)(2,1)S(1)} %copy-done.4, f32[16]{0:T(128)S(1)} %copy-done.11, f32[2,256,16]{1,2,0:T(8,128)S(1)} %get-tuple-element.89, bf16[2,256,256]{2,1,0:T(8,128)(2,1)S(1)} %bitcast.69, ...), kind=kOutput, calls=%fused_computation.25 | convolution fusion | flops 1617952256 | bytes 10782912 | tf_op jit(solution)/shard_map/klhn,khnp->klhp/dot_general | solution.py:98
  210.1 12.1 %all-gather.6.cloned.1.call-done = bf16[1024,4096]{1,0:T(8,128)(2,1)} async-done(((bf16[1024,128]{1,0:T(8,128)(2,1)}), bf16[1024,4096]{1,0:T(8,128)(2,1)}) %all-gather.6.cloned.1.call-update) | async-done | bytes 8388624 | tf_op jit(solution)/shard_map/all_gather | solution.py:111
  222.1 9.5 %convolution_convert_fusion = bf16[512,4096]{1,0:T(8,128)(2,1)} fusion(bf16[512,1024]{0,1:T(8,128)(2,1)S(1)} %multiply_convert_fusion.4, bf16[1024,4096]{1,0:T(8,128)(2,1)} %all-gather.6.cloned.1.call-done), kind=kOutput, calls=%fused_computation.7 | convolution fusion | flops 4297064448 | bytes 13631488 | tf_op jit(solution)/shard_map/dot_general | solution.py:109
  233.6 59.0 %reduce-scatter.2.cloned.1.call-done = bf16[64,4096]{1,0:T(8,128)(2,1)} async-done(((bf16[512,4096]{1,0:T(8,128)(2,1)}), bf16[64,4096]{1,0:T(8,128)(2,1)}) %reduce-scatter.2.cloned.1.call-update) | async-done | bytes 524304 | tf_op jit(solution)/shard_map/reduce_scatter | solution.py:114
  297.1 54.1 %all-gather.8.cloned.1.call-done = bf16[512,4096]{1,0:T(8,128)(2,1)} async-done(((bf16[64,4096]{1,0:T(8,128)(2,1)}), bf16[512,4096]{1,0:T(8,128)(2,1)}) %all-gather.8.cloned.1.call-update) | async-done | bytes 4194320 | tf_op jit(solution)/shard_map/all_gather | solution.py:127
  351.2 10.1 %convolution_convert_fusion.1 = bf16[512,1024]{1,0:T(8,128)(2,1)} fusion(bf16[512,4096]{1,0:T(8,128)(2,1)} %all-gather.8.cloned.1.call-done, bf16[4096,1024]{1,0:T(8,128)(2,1)} %all-gather.4.cloned.1.call-done), kind=kOutput, calls=%fused_computation.29 | convolution fusion | flops 4295491584 | bytes 13631488 | tf_op jit(solution)/shard_map/dot_general | solution.py:128
  (90 shorter events, 48.7 us)
Async XLA Ops:
  7.2 153.3 %copy-start = (bf16[512,1,256]{2,0,1:T(8,128)(2,1)S(1)}, bf16[512,1,256]{2,0,1:T(8,128)(2,1)}, u32[]{:S(2)}) copy-start(bf16[512,1,256]{2,0,1:T(8,128)(2,1)} %param.17) | copy-start | bytes 786436
  7.2 202.9 %all-gather.4.cloned.1.call-start = ((), (), s32[]{:S(2)}) async-start(), calls=%async_computation.1 | async-start | bytes 8650752 | tf_op jit(solution)/shard_map/all_gather | solution.py:107
  7.9 214.2 %all-gather.6.cloned.1.call-start = ((), (), s32[]{:S(2)}) async-start(), calls=%async_computation.2 | async-start | bytes 8650752 | tf_op jit(solution)/shard_map/all_gather | solution.py:111
  16.9 7.5 %copy-start.3 = (bf16[2,256,16,64]{1,3,2,0:T(8,128)(2,1)}, bf16[2,256,16,64]{1,3,2,0:T(8,128)(2,1)S(1)}, u32[]{:S(2)}) copy-start(bf16[2,256,16,64]{1,3,2,0:T(8,128)(2,1)S(1)} %copy.37) | copy-start | bytes 3145732
  24.4 3.0 copy-start.2
  32.4 17.8 %collective-permute-start.5 = (bf16[16,16384]{1,0:T(8,128)(2,1)S(1)}, bf16[16,16384]{1,0:T(8,128)(2,1)S(1)}, u32[]{:S(2)}, u32[]{:S(2)}) collective-permute-start(bf16[16,16384]{1,0:T(8,128)(2,1)S(1)} %convert_element_type.86), channel_id=1, source_target_pairs={{0,8},{8,16},{16,24},{24,32},{32,40},{40,48},{48,56},{56,64},{64,7... | collective-permute-start | bytes 1572872 | tf_op jit(solution)/shard_map/ppermute | solution.py:17
  50.2 39.5 %collective-permute-start.6 = (bf16[16,16384]{1,0:T(8,128)(2,1)S(1)}, bf16[16,16384]{1,0:T(8,128)(2,1)S(1)}, u32[]{:S(2)}, u32[]{:S(2)}) collective-permute-start(bf16[16,16384]{1,0:T(8,128)(2,1)S(1)} %collective-permute-done.5), channel_id=1, source_target_pairs={{0,8},{8,16},{16,24},{24,32},{32,40},{40,48},{48,56},{56,64},{64,7... | collective-permute-start | bytes 1572872 | tf_op jit(solution)/shard_map/ppermute | solution.py:17
  55.5 26.7 %collective-permute-start = (f32[16]{0:T(128)S(1)}, f32[16]{0:T(128)S(1)}, u32[]{:S(2)}, u32[]{:S(2)}) collective-permute-start(f32[16]{0:T(128)S(1)} %get-tuple-element.69), channel_id=1, source_target_pairs={{0,8},{8,16},{16,24},{24,32},{32,40},{40,48},{48,56},{56,64},{64,7... | collective-permute-start | bytes 200 | tf_op jit(solution)/shard_map/ppermute | solution.py:16
  82.3 7.4 %collective-permute-start.1 = (f32[16]{0:T(128)S(1)}, f32[16]{0:T(128)S(1)}, u32[]{:S(2)}, u32[]{:S(2)}) collective-permute-start(f32[16]{0:T(128)S(1)} %collective-permute-done), channel_id=1, source_target_pairs={{0,8},{8,16},{16,24},{24,32},{32,40},{40,48},{48,56},{56,64},{64,7... | collective-permute-start | bytes 200 | tf_op jit(solution)/shard_map/ppermute | solution.py:16
  89.9 22.9 %collective-permute-start.7 = (bf16[16,16384]{1,0:T(8,128)(2,1)S(1)}, bf16[16,16384]{1,0:T(8,128)(2,1)S(1)}, u32[]{:S(2)}, u32[]{:S(2)}) collective-permute-start(bf16[16,16384]{1,0:T(8,128)(2,1)S(1)} %fusion.27), channel_id=1, source_target_pairs={{0,16},{8,24},{16,32},{24,40},{32,48},{40,56},{48,64},{56,72},{64,... | collective-permute-start | bytes 1572872 | tf_op jit(solution)/shard_map/ppermute | solution.py:17
  97.6 195.1 %reduce-scatter.2.cloned.1.call-start = ((), (), s32[]{:S(2)}) async-start(), calls=%async_computation.3 | async-start | bytes 4718592 | tf_op jit(solution)/shard_map/reduce_scatter | solution.py:114
  112.8 66.6 %copy-start.4 = (bf16[2,256,16,64]{1,3,2,0:T(8,128)(2,1)S(1)}, bf16[2,256,16,64]{1,3,2,0:T(8,128)(2,1)}, u32[]{:S(2)}) copy-start(bf16[2,256,16,64]{1,3,2,0:T(8,128)(2,1)} %copy-done.3) | copy-start | bytes 3145732
  113.1 25.4 %collective-permute-start.8 = (bf16[16,16384]{1,0:T(8,128)(2,1)S(1)}, bf16[16,16384]{1,0:T(8,128)(2,1)S(1)}, u32[]{:S(2)}, u32[]{:S(2)}) collective-permute-start(bf16[16,16384]{1,0:T(8,128)(2,1)S(1)} %fusion.31), channel_id=1, source_target_pairs={{0,32},{8,40},{16,48},{24,56},{32,64},{40,72},{48,80},{56,88},{64,... | collective-permute-start | bytes 1572872 | tf_op jit(solution)/shard_map/ppermute | solution.py:17
  117.8 20.7 %collective-permute-start.2 = (f32[16]{0:T(128)S(1)}, f32[16]{0:T(128)S(1)}, u32[]{:S(2)}, u32[]{:S(2)}) collective-permute-start(f32[16]{0:T(128)S(1)} %get-tuple-element.88), channel_id=1, source_target_pairs={{0,16},{8,24},{16,32},{24,40},{32,48},{40,56},{48,64},{56,72},{64,... | collective-permute-start | bytes 200 | tf_op jit(solution)/shard_map/ppermute | solution.py:16
  139.0 32.0 %collective-permute-start.9 = (bf16[16,16384]{1,0:T(8,128)(2,1)S(1)}, bf16[16,16384]{1,0:T(8,128)(2,1)S(1)}, u32[]{:S(2)}, u32[]{:S(2)}) collective-permute-start(bf16[16,16384]{1,0:T(8,128)(2,1)S(1)} %fusion.28), channel_id=1, source_target_pairs={{0,64},{8,72},{16,80},{24,88},{32,96},{40,104},{48,112},{56,120},{... | collective-permute-start | bytes 1572872 | tf_op jit(solution)/shard_map/ppermute | solution.py:17
  161.7 4.9 %collective-permute-start.3 = (f32[16]{0:T(128)S(1)}, f32[16]{0:T(128)S(1)}, u32[]{:S(2)}, u32[]{:S(2)}) collective-permute-start(f32[16]{0:T(128)S(1)} %get-tuple-element.86), channel_id=1, source_target_pairs={{0,32},{8,40},{16,48},{24,56},{32,64},{40,72},{48,80},{56,88},{64,... | collective-permute-start | bytes 200 | tf_op jit(solution)/shard_map/ppermute | solution.py:16
  173.1 20.7 %collective-permute-start.10 = (bf16[16,16384]{1,0:T(8,128)(2,1)}, bf16[16,16384]{1,0:T(8,128)(2,1)}, u32[]{:S(2)}, u32[]{:S(2)}) collective-permute-start(bf16[16,16384]{1,0:T(8,128)(2,1)} %fusion.30), channel_id=1, source_target_pairs={{0,128},{8,136},{16,144},{24,152},{32,160},{40,168},{48,176},{56,1... | collective-permute-start | bytes 1572872 | tf_op jit(solution)/shard_map/ppermute | solution.py:17
  187.7 6.1 %collective-permute-start.4 = (f32[16]{0:T(128)S(1)}, f32[16]{0:T(128)S(1)}, u32[]{:S(2)}, u32[]{:S(2)}) collective-permute-start(f32[16]{0:T(128)S(1)} %get-tuple-element.84), channel_id=1, source_target_pairs={{0,64},{8,72},{16,80},{24,88},{32,96},{40,104},{48,112},{56,120},{... | collective-permute-start | bytes 200 | tf_op jit(solution)/shard_map/ppermute | solution.py:16
  193.8 6.2 %copy-start.11 = (f32[16]{0:T(128)S(1)}, f32[16]{0:T(128)}, u32[]{:S(2)}) copy-start(f32[16]{0:T(128)} %param.19) | copy-start | bytes 196
  231.6 61.0 %copy-start.5 = (bf16[64,4096]{1,0:T(8,128)(2,1)S(1)}, bf16[64,4096]{1,0:T(8,128)(2,1)}, u32[]{:S(2)}) copy-start(bf16[64,4096]{1,0:T(8,128)(2,1)} %param.22) | copy-start | bytes 1572868
  231.6 64.5 %copy-start.9 = (f32[4096]{0:T(1024)S(1)}, f32[4096]{0:T(1024)}, u32[]{:S(2)}) copy-start(f32[4096]{0:T(1024)} %param.24) | copy-start | bytes 49156
  231.6 119.5 %all-gather.8.cloned.1.call-start = ((), (), s32[]{:S(2)}) async-start(), calls=%async_computation.4 | async-start | bytes 4718592 | tf_op jit(solution)/shard_map/all_gather | solution.py:127
  296.1 65.3 %copy-start.6 = (bf16[64,4096]{1,0:T(8,128)(2,1)}, bf16[64,4096]{1,0:T(8,128)(2,1)S(1)}, u32[]{:S(2)}) copy-start(bf16[64,4096]{1,0:T(8,128)(2,1)S(1)} %get-tuple-element.82) | copy-start | bytes 1572868
  351.2 10.2 %copy-start.1 = (bf16[512,1,256]{2,0,1:T(8,128)(2,1)S(1)}, bf16[512,1,256]{2,0,1:T(8,128)(2,1)}, u32[]{:S(2)}) copy-start(bf16[512,1,256]{2,0,1:T(8,128)(2,1)} %param.17) | copy-start | bytes 786436
  (4 other events, 6.3 us)
Sparse Core Ops, SparseCore 0:
  10.6 85.8 all-gather.3
  98.9 123.1 all-gather.5
  231.8 60.8 reduce-scatter.1
  297.2 53.8 all-gather.7

commit v4 on v3

--- a/solution.py
+++ b/solution.py
@@ -106,31 +106,39 @@
     ssd_out = (grouped.reshape(seq_rows, channels) * norm_gain[None, :]).astype(jnp.bfloat16)
     w_in_all = lax.all_gather(w_in, "seq", axis=0, tiled=True)
     ssd_out, w_in_all = lax.optimization_barrier((ssd_out, w_in_all))
-    partial_sum = jnp.dot(
-        ssd_out,
-        lax.all_gather(w_out, "seq", axis=1, tiled=True),
-        preferred_element_type=jnp.float32,
-    )
-    mixer_out = lax.psum_scatter(
-        partial_sum.astype(jnp.bfloat16), "head", scatter_dimension=0, tiled=True
-    ).astype(jnp.float32)
+    w_out_all = lax.all_gather(w_out, "seq", axis=1, tiled=True)
     unit = refusal / jnp.sqrt(jnp.sum(refusal * refusal) + 1e-06)
-    hidden = residual.astype(jnp.float32) + mixer_out
-    coef = jnp.dot(hidden, unit, precision=lax.Precision.HIGHEST)
-    stream = (hidden - coef[:, None] * unit[None, :]).astype(jnp.bfloat16)
-    stream_float = stream.astype(jnp.float32)
-    normed = (
-        stream_float
-        * lax.rsqrt(jnp.mean(stream_float * stream_float, axis=-1, keepdims=True) + 1e-05)
-        * stream_gain[None, :]
-    ).astype(jnp.bfloat16)
-    all_rows = lax.all_gather(normed, "head", axis=0, tiled=True)
-    next_float = jnp.dot(
-        all_rows,
-        w_in_all,
-        preferred_element_type=jnp.float32,
-    )
-    return (stream, next_float.astype(jnp.bfloat16))
+    head_devices = lax.axis_size("head")
+    chunks = 2
+    own_rows = residual.shape[0] // chunks
+    ssd_parts = ssd_out.reshape(head_devices, chunks, own_rows, channels)
+    streams, nexts = [], []
+    for chunk in range(chunks):
+        partial_sum = jnp.dot(
+            ssd_parts[:, chunk].reshape(-1, channels),
+            w_out_all,
+            preferred_element_type=jnp.float32,
+        )
+        mixer_out = lax.psum_scatter(
+            partial_sum.astype(jnp.bfloat16), "head", scatter_dimension=0, tiled=True
+        ).astype(jnp.float32)
+        rows = residual[chunk * own_rows:(chunk + 1) * own_rows]
+        hidden = rows.astype(jnp.float32) + mixer_out
+        coef = jnp.dot(hidden, unit, precision=lax.Precision.HIGHEST)
+        stream = (hidden - coef[:, None] * unit[None, :]).astype(jnp.bfloat16)
+        stream_float = stream.astype(jnp.float32)
+        normed = (
+            stream_float
+            * lax.rsqrt(jnp.mean(stream_float * stream_float, axis=-1, keepdims=True) + 1e-05)
+            * stream_gain[None, :]
+        ).astype(jnp.bfloat16)
+        all_rows = lax.all_gather(normed, "head", axis=0, tiled=True)
+        next_part = jnp.dot(all_rows, w_in_all, preferred_element_type=jnp.float32)
+        streams.append(stream)
+        nexts.append(next_part.astype(jnp.bfloat16).reshape(head_devices, own_rows, -1))
+    stream = jnp.concatenate(streams, axis=0)
+    next_out = jnp.stack(nexts, axis=1).reshape(seq_rows, -1)
+    return (stream, next_out)
 
 
 def solution(mesh):

time: 369 us -> 438 us (1.19)
  waiting for transfers between devices: 186 us -> 241 us
  matrix products: 39.9 us -> 46.5 us
    reduce_scatter x1 -> x2, waiting for transfers between devices: 59 us -> 86.9 us  [body(): lax.psum_scatter(partial_sum.astype(jnp.bfloat16), 'head', scatter_dimens...]
    all_gather x1 -> x2, waiting for transfers between devices: 54.1 us -> 81 us  [body(): all_rows = lax.all_gather(normed, 'head', axis=0, tiled=True)]
    dot_general x2 -> x4, matrix products: 19.6 us -> 26.8 us  [the longest x2 14.1 us: body(): jnp.dot(ssd_parts[:, chunk].reshape(-1, channels), w_out_all, preferred_e...]
  transfers between devices with their start and end apart: 15 -> 17, of which waited for: 10 -> 12; matrix products, arithmetic and copies ran while one was open for 15% -> 16% of each run, Pallas kernels for 0% -> 0%
where the time goes in v4:
time: 438 us; the launch traced here: 434 us
  waiting for transfers between devices  241 us (55%)
  starting transfers between devices  84.1 us (19%)
  matrix products  46.5 us (11%)
  local copies, waits for them, and re-layouts  29.4 us (7%)
  other arithmetic  17.1 us (4%)
  between operations  15.2 us (3%)
    reduce_scatter x2, waiting for transfers between devices, body(): lax.psum_scatter(partial_sum.astype(jnp.bfloat16), 'head', scatter_dimens...  86.9 us
    all_gather x2, waiting for transfers between devices, body(): all_rows = lax.all_gather(normed, 'head', axis=0, tiled=True)  81 us
    ppermute x6, starting transfers between devices, shifted(): lax.ppermute(s.astype(jnp.bfloat16), axis, pairs).astype(jnp.float32)  51.7 us
    ppermute x5, starting transfers between devices, shifted(): lax.ppermute(a, axis, pairs)  31.9 us
    ppermute x6, waiting for transfers between devices, shifted(): lax.ppermute(s.astype(jnp.bfloat16), axis, pairs).astype(jnp.float32)  31.8 us
    ppermute x5, waiting for transfers between devices, shifted(): lax.ppermute(a, axis, pairs)  29.4 us
    dot_general x2, matrix products, body(): jnp.dot(ssd_parts[:, chunk].reshape(-1, channels), w_out_all, preferred_e...  14.1 us
    dot_general x2, matrix products, body(): next_part = jnp.dot(all_rows, w_in_all, preferred_element_type=jnp.float32)  12.7 us
  transfers between devices with their start and end apart: 17, of which 12 were waited for; matrix products, arithmetic and copies ran while one was open for 16% of the time, Pallas kernels for 0%

profile of v4, /device:TPU:1, one launch (start us, length us, event | category | flops | bytes accessed | tf_op | source)
XLA Modules:
  0.0 433.6 jit_solution(4571550896217294559)
XLA Ops:
  19.3 5.1 %fusion.3 = f32[2,16,256,64]{3,2,1,0:T(8,128)} fusion(bf16[2,256,16,64]{1,3,2,0:T(8,128)(2,1)S(1)} %copy.39, f32[2,256,16]{1,2,0:T(8,128)S(1)} %get-tuple-element.96, f32[2,256,256]{2,1,0:T(8,128)} %convert_element_type.104), kind=kOutput, calls=%fused_computation.10 | convolution fusion | flops 272629760 | bytes 3702784 | tf_op jit(solution)/shard_map/klhn,klhp->khnp/dot_general | solution.py:79
  24.4 7.0 %while.13 = (s32[]{:T(128)}, f32[16,256,64]{2,1,0:T(8,128)S(1)}, f32[2,16,256,64]{3,2,1,0:T(8,128)}, f32[2,16]{1,0:T(2,128)S(1)}, f32[2,16,256,64]{3,2,1,0:T(8,128)}, /*index=5*/s32[]{:T(128)}, s32[]{:T(128)}) while((s32[]{:T(128)}, f32[16,256,64]{2,1,0:T(8,128)S(1)}, f32[2,16,256,64]{3,2,1,0:T(8,128)}, f32[2,16]{1,0:T(2,128)S(1)}, ...), condition=%wide.region_3.4_spmd.clone, body=%wide.region_2.3_spmd.clone.sunk | while | flops 1048579 | bytes 14680892 | solution.py:89
  32.5 6.3 %collective-permute-start.5 = (bf16[16,16384]{1,0:T(8,128)(2,1)S(1)}, bf16[16,16384]{1,0:T(8,128)(2,1)S(1)}, u32[]{:S(2)}, u32[]{:S(2)}) collective-permute-start(bf16[16,16384]{1,0:T(8,128)(2,1)S(1)} %convert_element_type.107), channel_id=1, source_target_pairs={{0,8},{8,16},{16,24},{24,32},{32,40},{40,48},{48,56},{56,64},{64,7... | collective-permute-start | bytes 1572872 | tf_op jit(solution)/shard_map/ppermute | solution.py:17
  38.8 11.5 %collective-permute-done.5 = bf16[16,16384]{1,0:T(8,128)(2,1)S(1)} collective-permute-done((bf16[16,16384]{1,0:T(8,128)(2,1)S(1)}, bf16[16,16384]{1,0:T(8,128)(2,1)S(1)}, u32[]{:S(2)}, u32[]{:S(2)}) %collective-permute-start.5) | collective-permute-done | bytes 524320 | tf_op jit(solution)/shard_map/ppermute | solution.py:17
  50.3 5.3 %collective-permute-start.6 = (bf16[16,16384]{1,0:T(8,128)(2,1)S(1)}, bf16[16,16384]{1,0:T(8,128)(2,1)S(1)}, u32[]{:S(2)}, u32[]{:S(2)}) collective-permute-start(bf16[16,16384]{1,0:T(8,128)(2,1)S(1)} %collective-permute-done.5), channel_id=1, source_target_pairs={{0,8},{8,16},{16,24},{24,32},{32,40},{40,48},{48,56},{56,64},{64,7... | collective-permute-start | bytes 1572872 | tf_op jit(solution)/shard_map/ppermute | solution.py:17
  58.7 23.6 %collective-permute-done = f32[16]{0:T(128)S(1)} collective-permute-done((f32[16]{0:T(128)S(1)}, f32[16]{0:T(128)S(1)}, u32[]{:S(2)}, u32[]{:S(2)}) %collective-permute-start) | collective-permute-done | bytes 96 | tf_op jit(solution)/shard_map/ppermute | solution.py:16
  82.3 6.8 %collective-permute-start.1 = (f32[16]{0:T(128)S(1)}, f32[16]{0:T(128)S(1)}, u32[]{:S(2)}, u32[]{:S(2)}) collective-permute-start(f32[16]{0:T(128)S(1)} %collective-permute-done), channel_id=1, source_target_pairs={{0,8},{8,16},{16,24},{24,32},{32,40},{40,48},{48,56},{56,64},{64,7... | collective-permute-start | bytes 200 | tf_op jit(solution)/shard_map/ppermute | solution.py:16
  90.0 7.6 %collective-permute-start.7 = (bf16[16,16384]{1,0:T(8,128)(2,1)S(1)}, bf16[16,16384]{1,0:T(8,128)(2,1)S(1)}, u32[]{:S(2)}, u32[]{:S(2)}) collective-permute-start(bf16[16,16384]{1,0:T(8,128)(2,1)S(1)} %fusion.24), channel_id=1, source_target_pairs={{0,16},{8,24},{16,32},{24,40},{32,48},{40,56},{48,64},{56,72},{64,... | collective-permute-start | bytes 1572872 | tf_op jit(solution)/shard_map/ppermute | solution.py:17
  97.7 15.1 %collective-permute-done.7 = bf16[16,16384]{1,0:T(8,128)(2,1)S(1)} collective-permute-done((bf16[16,16384]{1,0:T(8,128)(2,1)S(1)}, bf16[16,16384]{1,0:T(8,128)(2,1)S(1)}, u32[]{:S(2)}, u32[]{:S(2)}) %collective-permute-start.7) | collective-permute-done | bytes 524320 | tf_op jit(solution)/shard_map/ppermute | solution.py:17
  117.8 16.3 %collective-permute-start.2 = (f32[16]{0:T(128)S(1)}, f32[16]{0:T(128)S(1)}, u32[]{:S(2)}, u32[]{:S(2)}) collective-permute-start(f32[16]{0:T(128)S(1)} %get-tuple-element.90), channel_id=1, source_target_pairs={{0,16},{8,24},{16,32},{24,40},{32,48},{40,56},{48,64},{56,72},{64,... | collective-permute-start | bytes 200 | tf_op jit(solution)/shard_map/ppermute | solution.py:16
  139.0 21.5 %collective-permute-start.9 = (bf16[16,16384]{1,0:T(8,128)(2,1)S(1)}, bf16[16,16384]{1,0:T(8,128)(2,1)S(1)}, u32[]{:S(2)}, u32[]{:S(2)}) collective-permute-start(bf16[16,16384]{1,0:T(8,128)(2,1)S(1)} %fusion.25), channel_id=1, source_target_pairs={{0,64},{8,72},{16,80},{24,88},{32,96},{40,104},{48,112},{56,120},{... | collective-permute-start | bytes 1572872 | tf_op jit(solution)/shard_map/ppermute | solution.py:17
  165.7 5.2 %collective-permute-done.9 = bf16[16,16384]{1,0:T(8,128)(2,1)S(1)} collective-permute-done((bf16[16,16384]{1,0:T(8,128)(2,1)S(1)}, bf16[16,16384]{1,0:T(8,128)(2,1)S(1)}, u32[]{:S(2)}, u32[]{:S(2)}) %collective-permute-start.9) | collective-permute-done | bytes 524320 | tf_op jit(solution)/shard_map/ppermute | solution.py:17
  173.1 6.4 %collective-permute-start.10 = (bf16[16,16384]{1,0:T(8,128)(2,1)}, bf16[16,16384]{1,0:T(8,128)(2,1)}, u32[]{:S(2)}, u32[]{:S(2)}) collective-permute-start(bf16[16,16384]{1,0:T(8,128)(2,1)} %fusion.35), channel_id=1, source_target_pairs={{0,128},{8,136},{16,144},{24,152},{32,160},{40,168},{48,176},{56,1... | collective-permute-start | bytes 1572872 | tf_op jit(solution)/shard_map/ppermute | solution.py:17
  189.2 4.7 %copy.46 = f32[2,256,16,64]{1,3,2,0:T(8,128)} copy(f32[2,256,16,64]{3,2,1,0:T(8,128)} %reshape.185) | data formatting | bytes 4194304 | tf_op jit(solution)/shard_map/convert_element_type | solution.py:102
  200.2 7.3 %multiply_reduce_fusion = (f32[2,256]{1,0:T(2,128)S(1)}, f32[2,256,16,64]{1,3,2,0:T(8,128)S(1)}) fusion(f32[2,256,16,64]{1,3,2,0:T(8,128)S(1)} %copy-done.5, bf16[2,256,16,64]{1,3,2,0:T(8,128)(2,1)S(1)} %copy-done.4, f32[16]{0:T(128)S(1)} %copy-done.12, f32[2,256,16]{1,2,0:T(8,128)S(1)} %get-tuple-element.95, bf16[2,256,256]{2,1,0:T(8,128)(2,1)S(1)} %bitcast.83, ...), kind=kOutput, calls=%fused_computation.26 | convolution fusion | flops 1617952256 | bytes 10782912 | tf_op jit(solution)/shard_map/klhn,khnp->klhp/dot_general | solution.py:98
  210.8 10.9 %all-gather.7.cloned.1.call-done = bf16[1024,4096]{1,0:T(8,128)(2,1)} async-done(((bf16[1024,128]{1,0:T(8,128)(2,1)}), bf16[1024,4096]{1,0:T(8,128)(2,1)}) %all-gather.7.cloned.1.call-update) | async-done | bytes 8388624 | tf_op jit(solution)/shard_map/all_gather | solution.py:109
  221.7 7.1 %convolution_convert_fusion = bf16[256,4096]{1,0:T(8,128)(2,1)} fusion(bf16[256,1024]{1,0:T(8,128)(2,1)S(1)} %bitcast.92, bf16[1024,4096]{1,0:T(8,128)(2,1)} %all-gather.7.cloned.1.call-done), kind=kOutput, calls=%fused_computation.7 | convolution fusion | flops 2148532224 | bytes 11010048 | tf_op jit(solution)/shard_map/dot_general | solution.py:117
  229.1 7.0 %convolution_convert_fusion.1 = bf16[256,4096]{1,0:T(8,128)(2,1)} fusion(bf16[256,1024]{1,0:T(8,128)(2,1)S(1)} %bitcast.90, bf16[1024,4096]{1,0:T(8,128)(2,1)} %all-gather.7.cloned.1.call-done), kind=kOutput, calls=%fused_computation.8 | convolution fusion | flops 2148532224 | bytes 11010048 | tf_op jit(solution)/shard_map/dot_general | solution.py:117
  238.1 42.1 %reduce-scatter.5.cloned.1.call-done = bf16[32,4096]{1,0:T(8,128)(2,1)} async-done(((bf16[256,4096]{1,0:T(8,128)(2,1)}), bf16[32,4096]{1,0:T(8,128)(2,1)}) %reduce-scatter.5.cloned.1.call-update) | async-done | bytes 262160 | tf_op jit(solution)/shard_map/reduce_scatter | solution.py:122
  281.7 44.8 %reduce-scatter.3.cloned.1.call-done = bf16[32,4096]{1,0:T(8,128)(2,1)} async-done(((bf16[256,4096]{1,0:T(8,128)(2,1)}), bf16[32,4096]{1,0:T(8,128)(2,1)}) %reduce-scatter.3.cloned.1.call-update) | async-done | bytes 262160 | tf_op jit(solution)/shard_map/reduce_scatter | solution.py:122
  331.9 42.3 %all-gather.9.cloned.1.call-done = bf16[256,4096]{1,0:T(8,128)(2,1)} async-done(((bf16[32,4096]{1,0:T(8,128)(2,1)}), bf16[256,4096]{1,0:T(8,128)(2,1)}) %all-gather.9.cloned.1.call-update) | async-done | bytes 2097168 | tf_op jit(solution)/shard_map/all_gather | solution.py:135
  374.2 6.3 %convolution_convert_fusion.3 = bf16[256,1024]{1,0:T(8,128)(2,1)S(1)} fusion(bf16[256,4096]{1,0:T(8,128)(2,1)} %all-gather.9.cloned.1.call-done, bf16[4096,1024]{1,0:T(8,128)(2,1)} %all-gather.5.cloned.1.call-done), kind=kOutput, calls=%fused_computation.31 | convolution fusion | flops 2147745792 | bytes 11010048 | tf_op jit(solution)/shard_map/dot_general | solution.py:136
  380.6 38.7 %all-gather.11.cloned.1.call-done = bf16[256,4096]{1,0:T(8,128)(2,1)} async-done(((bf16[32,4096]{1,0:T(8,128)(2,1)}), bf16[256,4096]{1,0:T(8,128)(2,1)}) %all-gather.11.cloned.1.call-update) | async-done | bytes 2097168 | tf_op jit(solution)/shard_map/all_gather | solution.py:135
  419.2 6.3 %convolution_convert_fusion.2 = bf16[256,1024]{1,0:T(8,128)(2,1)S(1)} fusion(bf16[256,4096]{1,0:T(8,128)(2,1)} %all-gather.11.cloned.1.call-done, bf16[4096,1024]{1,0:T(8,128)(2,1)} %all-gather.5.cloned.1.call-done), kind=kOutput, calls=%fused_computation.30 | convolution fusion | flops 2147745792 | bytes 11010048 | tf_op jit(solution)/shard_map/dot_general | solution.py:136
  (106 shorter events, 70.3 us)
Async XLA Ops:
  7.2 153.3 %copy-start = (bf16[512,1,256]{2,0,1:T(8,128)(2,1)S(1)}, bf16[512,1,256]{2,0,1:T(8,128)(2,1)}, u32[]{:S(2)}) copy-start(bf16[512,1,256]{2,0,1:T(8,128)(2,1)} %param.17) | copy-start | bytes 786436
  7.2 203.0 %all-gather.5.cloned.1.call-start = ((), (), s32[]{:S(2)}) async-start(), calls=%async_computation.2 | async-start | bytes 8650752 | tf_op jit(solution)/shard_map/all_gather | solution.py:107
  7.9 213.8 %all-gather.7.cloned.1.call-start = ((), (), s32[]{:S(2)}) async-start(), calls=%async_computation.3 | async-start | bytes 8650752 | tf_op jit(solution)/shard_map/all_gather | solution.py:109
  16.9 7.5 %copy-start.3 = (bf16[2,256,16,64]{1,3,2,0:T(8,128)(2,1)}, bf16[2,256,16,64]{1,3,2,0:T(8,128)(2,1)S(1)}, u32[]{:S(2)}) copy-start(bf16[2,256,16,64]{1,3,2,0:T(8,128)(2,1)S(1)} %copy.39) | copy-start | bytes 3145732
  32.5 17.8 %collective-permute-start.5 = (bf16[16,16384]{1,0:T(8,128)(2,1)S(1)}, bf16[16,16384]{1,0:T(8,128)(2,1)S(1)}, u32[]{:S(2)}, u32[]{:S(2)}) collective-permute-start(bf16[16,16384]{1,0:T(8,128)(2,1)S(1)} %convert_element_type.107), channel_id=1, source_target_pairs={{0,8},{8,16},{16,24},{24,32},{32,40},{40,48},{48,56},{56,64},{64,7... | collective-permute-start | bytes 1572872 | tf_op jit(solution)/shard_map/ppermute | solution.py:17
  50.3 39.5 %collective-permute-start.6 = (bf16[16,16384]{1,0:T(8,128)(2,1)S(1)}, bf16[16,16384]{1,0:T(8,128)(2,1)S(1)}, u32[]{:S(2)}, u32[]{:S(2)}) collective-permute-start(bf16[16,16384]{1,0:T(8,128)(2,1)S(1)} %collective-permute-done.5), channel_id=1, source_target_pairs={{0,8},{8,16},{16,24},{24,32},{32,40},{40,48},{48,56},{56,64},{64,7... | collective-permute-start | bytes 1572872 | tf_op jit(solution)/shard_map/ppermute | solution.py:17
  55.5 26.7 %collective-permute-start = (f32[16]{0:T(128)S(1)}, f32[16]{0:T(128)S(1)}, u32[]{:S(2)}, u32[]{:S(2)}) collective-permute-start(f32[16]{0:T(128)S(1)} %get-tuple-element.69), channel_id=1, source_target_pairs={{0,8},{8,16},{16,24},{24,32},{32,40},{40,48},{48,56},{56,64},{64,7... | collective-permute-start | bytes 200 | tf_op jit(solution)/shard_map/ppermute | solution.py:16
  82.3 7.5 %collective-permute-start.1 = (f32[16]{0:T(128)S(1)}, f32[16]{0:T(128)S(1)}, u32[]{:S(2)}, u32[]{:S(2)}) collective-permute-start(f32[16]{0:T(128)S(1)} %collective-permute-done), channel_id=1, source_target_pairs={{0,8},{8,16},{16,24},{24,32},{32,40},{40,48},{48,56},{56,64},{64,7... | collective-permute-start | bytes 200 | tf_op jit(solution)/shard_map/ppermute | solution.py:16
  90.0 22.8 %collective-permute-start.7 = (bf16[16,16384]{1,0:T(8,128)(2,1)S(1)}, bf16[16,16384]{1,0:T(8,128)(2,1)S(1)}, u32[]{:S(2)}, u32[]{:S(2)}) collective-permute-start(bf16[16,16384]{1,0:T(8,128)(2,1)S(1)} %fusion.24), channel_id=1, source_target_pairs={{0,16},{8,24},{16,32},{24,40},{32,48},{40,56},{48,64},{56,72},{64,... | collective-permute-start | bytes 1572872 | tf_op jit(solution)/shard_map/ppermute | solution.py:17
  97.6 182.6 %reduce-scatter.5.cloned.1.call-start = ((), (), s32[]{:S(2)}) async-start(), calls=%async_computation.5 | async-start | bytes 2359296 | tf_op jit(solution)/shard_map/reduce_scatter | solution.py:122
  112.8 47.7 %copy-start.7 = (bf16[512,1,256]{2,0,1:T(8,128)(2,1)S(1)}, bf16[512,1,256]{2,0,1:T(8,128)(2,1)}, u32[]{:S(2)}) copy-start(bf16[512,1,256]{2,0,1:T(8,128)(2,1)} %param.16) | copy-start | bytes 786436
  113.1 25.4 %collective-permute-start.8 = (bf16[16,16384]{1,0:T(8,128)(2,1)S(1)}, bf16[16,16384]{1,0:T(8,128)(2,1)S(1)}, u32[]{:S(2)}, u32[]{:S(2)}) collective-permute-start(bf16[16,16384]{1,0:T(8,128)(2,1)S(1)} %fusion.36), channel_id=1, source_target_pairs={{0,32},{8,40},{16,48},{24,56},{32,64},{40,72},{48,80},{56,88},{64,... | collective-permute-start | bytes 1572872 | tf_op jit(solution)/shard_map/ppermute | solution.py:17
  117.8 20.7 %collective-permute-start.2 = (f32[16]{0:T(128)S(1)}, f32[16]{0:T(128)S(1)}, u32[]{:S(2)}, u32[]{:S(2)}) collective-permute-start(f32[16]{0:T(128)S(1)} %get-tuple-element.90), channel_id=1, source_target_pairs={{0,16},{8,24},{16,32},{24,40},{32,48},{40,56},{48,64},{56,72},{64,... | collective-permute-start | bytes 200 | tf_op jit(solution)/shard_map/ppermute | solution.py:16
  139.0 32.0 %collective-permute-start.9 = (bf16[16,16384]{1,0:T(8,128)(2,1)S(1)}, bf16[16,16384]{1,0:T(8,128)(2,1)S(1)}, u32[]{:S(2)}, u32[]{:S(2)}) collective-permute-start(bf16[16,16384]{1,0:T(8,128)(2,1)S(1)} %fusion.25), channel_id=1, source_target_pairs={{0,64},{8,72},{16,80},{24,88},{32,96},{40,104},{48,112},{56,120},{... | collective-permute-start | bytes 1572872 | tf_op jit(solution)/shard_map/ppermute | solution.py:17
  160.5 18.9 %copy-start.4 = (bf16[2,256,16,64]{1,3,2,0:T(8,128)(2,1)S(1)}, bf16[2,256,16,64]{1,3,2,0:T(8,128)(2,1)}, u32[]{:S(2)}) copy-start(bf16[2,256,16,64]{1,3,2,0:T(8,128)(2,1)} %copy-done.3) | copy-start | bytes 3145732
  160.8 5.0 %collective-permute-start.3 = (f32[16]{0:T(128)S(1)}, f32[16]{0:T(128)S(1)}, u32[]{:S(2)}, u32[]{:S(2)}) collective-permute-start(f32[16]{0:T(128)S(1)} %get-tuple-element.88), channel_id=1, source_target_pairs={{0,32},{8,40},{16,48},{24,56},{32,64},{40,72},{48,80},{56,88},{64,... | collective-permute-start | bytes 200 | tf_op jit(solution)/shard_map/ppermute | solution.py:16
  173.1 20.8 %collective-permute-start.10 = (bf16[16,16384]{1,0:T(8,128)(2,1)}, bf16[16,16384]{1,0:T(8,128)(2,1)}, u32[]{:S(2)}, u32[]{:S(2)}) collective-permute-start(bf16[16,16384]{1,0:T(8,128)(2,1)} %fusion.35), channel_id=1, source_target_pairs={{0,128},{8,136},{16,144},{24,152},{32,160},{40,168},{48,176},{56,1... | collective-permute-start | bytes 1572872 | tf_op jit(solution)/shard_map/ppermute | solution.py:17
  187.7 6.2 %collective-permute-start.4 = (f32[16]{0:T(128)S(1)}, f32[16]{0:T(128)S(1)}, u32[]{:S(2)}, u32[]{:S(2)}) collective-permute-start(f32[16]{0:T(128)S(1)} %get-tuple-element.86), channel_id=1, source_target_pairs={{0,64},{8,72},{16,80},{24,88},{32,96},{40,104},{48,112},{56,120},{... | collective-permute-start | bytes 200 | tf_op jit(solution)/shard_map/ppermute | solution.py:16
  196.7 3.6 copy-start.12
  228.8 97.8 %reduce-scatter.3.cloned.1.call-start = ((), (), s32[]{:S(2)}) async-start(), calls=%async_computation.4 | async-start | bytes 2359296 | tf_op jit(solution)/shard_map/reduce_scatter | solution.py:122
  236.1 44.1 %copy-start.8 = (bf16[64,4096]{1,0:T(8,128)(2,1)S(1)}, bf16[64,4096]{1,0:T(8,128)(2,1)}, u32[]{:S(2)}) copy-start(bf16[64,4096]{1,0:T(8,128)(2,1)} %param.22) | copy-start | bytes 1572868
  236.1 93.4 %copy-start.10 = (f32[4096]{0:T(1024)S(1)}, f32[4096]{0:T(1024)}, u32[]{:S(2)}) copy-start(f32[4096]{0:T(1024)} %param.24) | copy-start | bytes 49156
  236.1 138.1 %all-gather.9.cloned.1.call-start = ((), (), s32[]{:S(2)}) async-start(), calls=%async_computation.6 | async-start | bytes 2359296 | tf_op jit(solution)/shard_map/all_gather | solution.py:135
  330.5 88.7 %all-gather.11.cloned.1.call-start = ((), (), s32[]{:S(2)}) async-start(), calls=%async_computation.7 | async-start | bytes 2359296 | tf_op jit(solution)/shard_map/all_gather | solution.py:135
  (7 other events, 13.0 us)
Sparse Core Ops, SparseCore 0:
  10.6 85.8 all-gather.4
  98.9 122.7 all-gather.6
  228.9 51.2 reduce-scatter.4
  282.6 43.8 reduce-scatter.2
  330.6 43.5 all-gather.8
  375.9 43.3 all-gather.10

commit v5 on v3

--- a/solution.py
+++ b/solution.py
@@ -104,11 +104,13 @@
     grouped = gated.reshape(seq_rows, group_count, per_group * head_width)
     grouped = grouped * lax.rsqrt(jnp.mean(grouped * grouped, axis=-1, keepdims=True) + 1e-05)
     ssd_out = (grouped.reshape(seq_rows, channels) * norm_gain[None, :]).astype(jnp.bfloat16)
-    w_in_all = lax.all_gather(w_in, "seq", axis=0, tiled=True)
-    ssd_out, w_in_all = lax.optimization_barrier((ssd_out, w_in_all))
-    partial_sum = jnp.dot(
+    both = lax.all_gather(jnp.stack([w_out.T, w_in]), "seq", axis=1, tiled=True)
+    ssd_out, both = lax.optimization_barrier((ssd_out, both))
+    w_in_all = both[1]
+    partial_sum = lax.dot_general(
         ssd_out,
-        lax.all_gather(w_out, "seq", axis=1, tiled=True),
+        both[0],
+        (((1,), (1,)), ((), ())),
         preferred_element_type=jnp.float32,
     )
     mixer_out = lax.psum_scatter(

time: 369 us -> 391 us (1.060)
  waiting for transfers between devices: 186 us -> 219 us
  starting transfers between devices: 83.8 us -> 71.7 us
    ppermute x6, waiting for transfers between devices: 31.1 us -> 66.8 us  [shifted(): lax.ppermute(s.astype(jnp.bfloat16), axis, pairs).astype(jnp.float32)]
    all_gather x2 -> x1, waiting for transfers between devices: 12.1 us -> 0.02 us  [body(): both = lax.all_gather(jnp.stack([w_out.T, w_in]), 'seq', axis=1, tiled=True)]
    ppermute x5, waiting for transfers between devices: 29.4 us -> 41.1 us  [shifted(): lax.ppermute(a, axis, pairs)]
    ppermute x5, starting transfers between devices: 31.8 us -> 22.8 us  [shifted(): lax.ppermute(a, axis, pairs)]
  transfers between devices with their start and end apart: 15 -> 14, of which waited for: 10 -> 9; matrix products, arithmetic and copies ran while one was open for 15% -> 14% of each run, Pallas kernels for 0% -> 0%
where the time goes in v5:
time: 391 us; the launch traced here: 390 us
  waiting for transfers between devices  219 us (56%)
  starting transfers between devices  71.7 us (18%)
  matrix products  39.1 us (10%)
  local copies, waits for them, and re-layouts  28 us (7%)
  other arithmetic  18 us (5%)
  between operations  14.8 us (4%)
    ppermute x6, waiting for transfers between devices, shifted(): lax.ppermute(s.astype(jnp.bfloat16), axis, pairs).astype(jnp.float32)  66.8 us
    reduce_scatter x1, waiting for transfers between devices, body(): lax.psum_scatter(partial_sum.astype(jnp.bfloat16), 'head', scatter_dimens...  56.7 us
    all_gather x1, waiting for transfers between devices, body(): all_rows = lax.all_gather(normed, 'head', axis=0, tiled=True)  54.1 us
    ppermute x6, starting transfers between devices, shifted(): lax.ppermute(s.astype(jnp.bfloat16), axis, pairs).astype(jnp.float32)  48.6 us
    ppermute x5, waiting for transfers between devices, shifted(): lax.ppermute(a, axis, pairs)  41.1 us
    ppermute x5, starting transfers between devices, shifted(): lax.ppermute(a, axis, pairs)  22.8 us
    dot_general x1, matrix products, body(): next_float = jnp.dot(all_rows, w_in_all, preferred_element_type=jnp.float32)  10.1 us
    dot_general x1, matrix products, body(): lax.dot_general(ssd_out, both[0], (((1,), (1,)), ((), ())), preferred_ele...  9.65 us
  transfers between devices with their start and end apart: 14, of which 9 were waited for; matrix products, arithmetic and copies ran while one was open for 14% of the time, Pallas kernels for 0%

profile of v5, /device:TPU:1, one launch (start us, length us, event | category | flops | bytes accessed | tf_op | source)
XLA Modules:
  0.0 390.4 jit_solution(2981738312741864728)
XLA Ops:
  21.6 5.1 %fusion.12 = f32[2,16,256,64]{3,2,1,0:T(8,128)} fusion(bf16[2,256,16,64]{1,3,2,0:T(8,128)(2,1)S(1)} %copy.39, f32[2,256,16]{1,2,0:T(8,128)S(1)} %get-tuple-element.90, f32[2,256,256]{2,1,0:T(8,128)} %convert_element_type.83), kind=kOutput, calls=%fused_computation.15 | convolution fusion | flops 272629760 | bytes 3702784 | tf_op jit(solution)/shard_map/klhn,klhp->khnp/dot_general | solution.py:79
  26.7 7.2 %while.13 = (s32[]{:T(128)}, f32[16,256,64]{2,1,0:T(8,128)S(1)}, f32[2,16,256,64]{3,2,1,0:T(8,128)}, f32[2,16]{1,0:T(2,128)S(1)}, f32[2,16,256,64]{3,2,1,0:T(8,128)}, /*index=5*/s32[]{:T(128)}, s32[]{:T(128)}) while((s32[]{:T(128)}, f32[16,256,64]{2,1,0:T(8,128)S(1)}, f32[2,16,256,64]{3,2,1,0:T(8,128)}, f32[2,16]{1,0:T(2,128)S(1)}, ...), condition=%wide.region_3.4_spmd.clone, body=%wide.region_2.3_spmd.clone.sunk | while | flops 1048579 | bytes 14680892 | solution.py:89
  34.8 6.2 %collective-permute-start.5 = (bf16[16,16384]{1,0:T(8,128)(2,1)S(1)}, bf16[16,16384]{1,0:T(8,128)(2,1)S(1)}, u32[]{:S(2)}, u32[]{:S(2)}) collective-permute-start(bf16[16,16384]{1,0:T(8,128)(2,1)S(1)} %convert_element_type.86), channel_id=1, source_target_pairs={{0,8},{8,16},{16,24},{24,32},{32,40},{40,48},{48,56},{56,64},{64,7... | collective-permute-start | bytes 1572872 | tf_op jit(solution)/shard_map/ppermute | solution.py:17
  41.1 18.3 %collective-permute-done.5 = bf16[16,16384]{1,0:T(8,128)(2,1)S(1)} collective-permute-done((bf16[16,16384]{1,0:T(8,128)(2,1)S(1)}, bf16[16,16384]{1,0:T(8,128)(2,1)S(1)}, u32[]{:S(2)}, u32[]{:S(2)}) %collective-permute-start.5) | collective-permute-done | bytes 524320 | tf_op jit(solution)/shard_map/ppermute | solution.py:17
  59.3 5.3 %collective-permute-start.6 = (bf16[16,16384]{1,0:T(8,128)(2,1)S(1)}, bf16[16,16384]{1,0:T(8,128)(2,1)S(1)}, u32[]{:S(2)}, u32[]{:S(2)}) collective-permute-start(bf16[16,16384]{1,0:T(8,128)(2,1)S(1)} %collective-permute-done.5), channel_id=1, source_target_pairs={{0,8},{8,16},{16,24},{24,32},{32,40},{40,48},{48,56},{56,64},{64,7... | collective-permute-start | bytes 1572872 | tf_op jit(solution)/shard_map/ppermute | solution.py:17
  66.5 31.0 %collective-permute-done = f32[16]{0:T(128)S(1)} collective-permute-done((f32[16]{0:T(128)S(1)}, f32[16]{0:T(128)S(1)}, u32[]{:S(2)}, u32[]{:S(2)}) %collective-permute-start) | collective-permute-done | bytes 96 | tf_op jit(solution)/shard_map/ppermute | solution.py:16
  97.5 5.3 %collective-permute-start.1 = (f32[16]{0:T(128)S(1)}, f32[16]{0:T(128)S(1)}, u32[]{:S(2)}, u32[]{:S(2)}) collective-permute-start(f32[16]{0:T(128)S(1)} %collective-permute-done), channel_id=1, source_target_pairs={{0,8},{8,16},{16,24},{24,32},{32,40},{40,48},{48,56},{56,64},{64,7... | collective-permute-start | bytes 200 | tf_op jit(solution)/shard_map/ppermute | solution.py:16
  103.8 4.5 %collective-permute-start.7 = (bf16[16,16384]{1,0:T(8,128)(2,1)S(1)}, bf16[16,16384]{1,0:T(8,128)(2,1)S(1)}, u32[]{:S(2)}, u32[]{:S(2)}) collective-permute-start(bf16[16,16384]{1,0:T(8,128)(2,1)S(1)} %fusion.39), channel_id=1, source_target_pairs={{0,16},{8,24},{16,32},{24,40},{32,48},{40,56},{48,64},{56,72},{64,... | collective-permute-start | bytes 1572872 | tf_op jit(solution)/shard_map/ppermute | solution.py:17
  108.3 43.7 %collective-permute-done.7 = bf16[16,16384]{1,0:T(8,128)(2,1)S(1)} collective-permute-done((bf16[16,16384]{1,0:T(8,128)(2,1)S(1)}, bf16[16,16384]{1,0:T(8,128)(2,1)S(1)}, u32[]{:S(2)}, u32[]{:S(2)}) %collective-permute-start.7) | collective-permute-done | bytes 524320 | tf_op jit(solution)/shard_map/ppermute | solution.py:17
  152.3 7.6 %collective-permute-start.8 = (bf16[16,16384]{1,0:T(8,128)(2,1)S(1)}, bf16[16,16384]{1,0:T(8,128)(2,1)S(1)}, u32[]{:S(2)}, u32[]{:S(2)}) collective-permute-start(bf16[16,16384]{1,0:T(8,128)(2,1)S(1)} %fusion.43), channel_id=1, source_target_pairs={{0,32},{8,40},{16,48},{24,56},{32,64},{40,72},{48,80},{56,88},{64,... | collective-permute-start | bytes 1572872 | tf_op jit(solution)/shard_map/ppermute | solution.py:17
  159.9 8.0 %collective-permute-start.2 = (f32[16]{0:T(128)S(1)}, f32[16]{0:T(128)S(1)}, u32[]{:S(2)}, u32[]{:S(2)}) collective-permute-start(f32[16]{0:T(128)S(1)} %get-tuple-element.88), channel_id=1, source_target_pairs={{0,16},{8,24},{16,32},{24,40},{32,48},{40,56},{48,64},{56,72},{64,... | collective-permute-start | bytes 200 | tf_op jit(solution)/shard_map/ppermute | solution.py:16
  167.9 8.8 %collective-permute-done.2 = f32[16]{0:T(128)S(1)} collective-permute-done((f32[16]{0:T(128)S(1)}, f32[16]{0:T(128)S(1)}, u32[]{:S(2)}, u32[]{:S(2)}) %collective-permute-start.2) | collective-permute-done | bytes 96 | tf_op jit(solution)/shard_map/ppermute | solution.py:16
  177.1 19.4 %collective-permute-start.9 = (bf16[16,16384]{1,0:T(8,128)(2,1)S(1)}, bf16[16,16384]{1,0:T(8,128)(2,1)S(1)}, u32[]{:S(2)}, u32[]{:S(2)}) collective-permute-start(bf16[16,16384]{1,0:T(8,128)(2,1)S(1)} %fusion.40), channel_id=1, source_target_pairs={{0,64},{8,72},{16,80},{24,88},{32,96},{40,104},{48,112},{56,120},{... | collective-permute-start | bytes 1572872 | tf_op jit(solution)/shard_map/ppermute | solution.py:17
  196.8 4.5 %collective-permute-start.3 = (f32[16]{0:T(128)S(1)}, f32[16]{0:T(128)S(1)}, u32[]{:S(2)}, u32[]{:S(2)}) collective-permute-start(f32[16]{0:T(128)S(1)} %get-tuple-element.86), channel_id=1, source_target_pairs={{0,32},{8,40},{16,48},{24,56},{32,64},{40,72},{48,80},{56,88},{64,... | collective-permute-start | bytes 200 | tf_op jit(solution)/shard_map/ppermute | solution.py:16
  202.0 4.9 %collective-permute-done.9 = bf16[16,16384]{1,0:T(8,128)(2,1)S(1)} collective-permute-done((bf16[16,16384]{1,0:T(8,128)(2,1)S(1)}, bf16[16,16384]{1,0:T(8,128)(2,1)S(1)}, u32[]{:S(2)}, u32[]{:S(2)}) %collective-permute-start.9) | collective-permute-done | bytes 524320 | tf_op jit(solution)/shard_map/ppermute | solution.py:17
  209.0 5.6 %collective-permute-start.10 = (bf16[16,16384]{1,0:T(8,128)(2,1)}, bf16[16,16384]{1,0:T(8,128)(2,1)}, u32[]{:S(2)}, u32[]{:S(2)}) collective-permute-start(bf16[16,16384]{1,0:T(8,128)(2,1)} %fusion.42), channel_id=1, source_target_pairs={{0,128},{8,136},{16,144},{24,152},{32,160},{40,168},{48,176},{56,1... | collective-permute-start | bytes 1572872 | tf_op jit(solution)/shard_map/ppermute | solution.py:17
  214.6 4.1 %fusion.11 = f32[2,16,256,64]{2,3,1,0:T(8,128)} fusion(bf16[2,256,16,64]{1,3,2,0:T(8,128)(2,1)S(1)} %copy-done.4, f32[2,256,256]{2,1,0:T(8,128)S(1)} %fusion.47, f32[2,16,256]{2,1,0:T(8,128)S(1)} %copy_bitcast_fusion, pred[256,256]{1,0:T(8,128)(4,1)S(1)} %iota_compare_fusion), kind=kOutput, calls=%fused_computation.14 | convolution fusion | flops 278921216 | bytes 3768320 | tf_op jit(solution)/shard_map/khls,kshp->klhp/dot_general | solution.py:73
  218.7 4.1 %reshape.166 = f32[2,256,16,64]{3,2,1,0:T(8,128)} reshape(bf16[512,1024]{1,0:T(8,128)(2,1)} %param.15) | data formatting | bytes 3145728 | tf_op jit(solution)/shard_map/convert_element_type | solution.py:102
  225.9 4.6 %copy.46 = f32[2,256,16,64]{1,3,2,0:T(8,128)} copy(f32[2,256,16,64]{3,2,1,0:T(8,128)} %reshape.166) | data formatting | bytes 4194304 | tf_op jit(solution)/shard_map/convert_element_type | solution.py:102
  236.7 7.9 %multiply_reduce_fusion = (f32[2,256]{1,0:T(2,128)S(1)}, f32[2,256,16,64]{1,3,2,0:T(8,128)S(1)}) fusion(f32[2,256,16,64]{1,3,2,0:T(8,128)} %copy.46, bf16[2,256,16,64]{1,3,2,0:T(8,128)(2,1)S(1)} %copy-done.4, f32[16]{0:T(128)S(1)} %copy-done.12, f32[2,256,16]{1,2,0:T(8,128)S(1)} %get-tuple-element.89, bf16[2,256,256]{2,1,0:T(8,128)(2,1)S(1)} %bitcast.81, ...), kind=kOutput, calls=%fused_computation.31 | convolution fusion | flops 1617952256 | bytes 10782912 | tf_op jit(solution)/shard_map/klhn,khnp->klhp/dot_general | solution.py:98
  246.8 9.7 %fusion.8 = bf16[512,4096]{1,0:T(8,128)(2,1)} fusion(bf16[512,1024]{0,1:T(8,128)(2,1)S(1)} %multiply_convert_fusion.4, bf16[2,4096,1024]{2,1,0:T(8,128)(2,1)} %all-gather.3.cloned.1.call-done), kind=kOutput, calls=%fused_computation.13 | convolution fusion | flops 4297064448 | bytes 13631488 | tf_op jit(solution)/shard_map/dot_general | solution.py:110
  258.5 56.7 %reduce-scatter.2.cloned.1.call-done = bf16[64,4096]{1,0:T(8,128)(2,1)} async-done(((bf16[512,4096]{1,0:T(8,128)(2,1)}), bf16[64,4096]{1,0:T(8,128)(2,1)}) %reduce-scatter.2.cloned.1.call-update) | async-done | bytes 524304 | tf_op jit(solution)/shard_map/reduce_scatter | solution.py:116
  319.7 54.1 %all-gather.5.cloned.1.call-done = bf16[512,4096]{1,0:T(8,128)(2,1)} async-done(((bf16[64,4096]{1,0:T(8,128)(2,1)}), bf16[512,4096]{1,0:T(8,128)(2,1)}) %all-gather.5.cloned.1.call-update) | async-done | bytes 4194320 | tf_op jit(solution)/shard_map/all_gather | solution.py:129
  373.7 10.1 %fusion.29 = bf16[512,1024]{1,0:T(8,128)(2,1)} fusion(bf16[512,4096]{1,0:T(8,128)(2,1)} %all-gather.5.cloned.1.call-done, bf16[2,4096,1024]{2,1,0:T(8,128)(2,1)} %all-gather.3.cloned.1.call-done), kind=kOutput, calls=%fused_computation.35 | convolution fusion | flops 4295491584 | bytes 13631488 | tf_op jit(solution)/shard_map/dot_general | solution.py:130
  (91 shorter events, 46.4 us)
Async XLA Ops:
  7.2 189.3 %copy-start = (bf16[512,1,256]{2,0,1:T(8,128)(2,1)S(1)}, bf16[512,1,256]{2,0,1:T(8,128)(2,1)}, u32[]{:S(2)}) copy-start(bf16[512,1,256]{2,0,1:T(8,128)(2,1)} %param.17) | copy-start | bytes 786436
  7.2 239.6 %all-gather.3.cloned.1.call-start = ((), (), s32[]{:S(2)}) async-start(), calls=%async_computation.1 | async-start | bytes 17301504 | tf_op jit(solution)/shard_map/all_gather | solution.py:107
  10.2 305.0 %reduce-scatter.2.cloned.1.call-start = ((), (), s32[]{:S(2)}) async-start(), calls=%async_computation.2 | async-start | bytes 4718592 | tf_op jit(solution)/shard_map/reduce_scatter | solution.py:116
  19.2 7.5 %copy-start.3 = (bf16[2,256,16,64]{1,3,2,0:T(8,128)(2,1)}, bf16[2,256,16,64]{1,3,2,0:T(8,128)(2,1)S(1)}, u32[]{:S(2)}) copy-start(bf16[2,256,16,64]{1,3,2,0:T(8,128)(2,1)S(1)} %copy.39) | copy-start | bytes 3145732
  26.7 3.1 copy-start.2
  34.8 161.7 %copy-start.8 = (bf16[512,1,256]{2,0,1:T(8,128)(2,1)S(1)}, bf16[512,1,256]{2,0,1:T(8,128)(2,1)}, u32[]{:S(2)}) copy-start(bf16[512,1,256]{2,0,1:T(8,128)(2,1)} %param.16) | copy-start | bytes 786436
  34.8 24.5 %collective-permute-start.5 = (bf16[16,16384]{1,0:T(8,128)(2,1)S(1)}, bf16[16,16384]{1,0:T(8,128)(2,1)S(1)}, u32[]{:S(2)}, u32[]{:S(2)}) collective-permute-start(bf16[16,16384]{1,0:T(8,128)(2,1)S(1)} %convert_element_type.86), channel_id=1, source_target_pairs={{0,8},{8,16},{16,24},{24,32},{32,40},{40,48},{48,56},{56,64},{64,7... | collective-permute-start | bytes 1572872 | tf_op jit(solution)/shard_map/ppermute | solution.py:17
  59.3 44.2 %collective-permute-start.6 = (bf16[16,16384]{1,0:T(8,128)(2,1)S(1)}, bf16[16,16384]{1,0:T(8,128)(2,1)S(1)}, u32[]{:S(2)}, u32[]{:S(2)}) collective-permute-start(bf16[16,16384]{1,0:T(8,128)(2,1)S(1)} %collective-permute-done.5), channel_id=1, source_target_pairs={{0,8},{8,16},{16,24},{24,32},{32,40},{40,48},{48,56},{56,64},{64,7... | collective-permute-start | bytes 1572872 | tf_op jit(solution)/shard_map/ppermute | solution.py:17
  64.6 32.9 %collective-permute-start = (f32[16]{0:T(128)S(1)}, f32[16]{0:T(128)S(1)}, u32[]{:S(2)}, u32[]{:S(2)}) collective-permute-start(f32[16]{0:T(128)S(1)} %get-tuple-element.69), channel_id=1, source_target_pairs={{0,8},{8,16},{16,24},{24,32},{32,40},{40,48},{48,56},{56,64},{64,7... | collective-permute-start | bytes 200 | tf_op jit(solution)/shard_map/ppermute | solution.py:16
  97.5 6.0 %collective-permute-start.1 = (f32[16]{0:T(128)S(1)}, f32[16]{0:T(128)S(1)}, u32[]{:S(2)}, u32[]{:S(2)}) collective-permute-start(f32[16]{0:T(128)S(1)} %collective-permute-done), channel_id=1, source_target_pairs={{0,8},{8,16},{16,24},{24,32},{32,40},{40,48},{48,56},{56,64},{64,7... | collective-permute-start | bytes 200 | tf_op jit(solution)/shard_map/ppermute | solution.py:16
  103.8 48.2 %collective-permute-start.7 = (bf16[16,16384]{1,0:T(8,128)(2,1)S(1)}, bf16[16,16384]{1,0:T(8,128)(2,1)S(1)}, u32[]{:S(2)}, u32[]{:S(2)}) collective-permute-start(bf16[16,16384]{1,0:T(8,128)(2,1)S(1)} %fusion.39), channel_id=1, source_target_pairs={{0,16},{8,24},{16,32},{24,40},{32,48},{40,56},{48,64},{56,72},{64,... | collective-permute-start | bytes 1572872 | tf_op jit(solution)/shard_map/ppermute | solution.py:17
  152.0 62.6 %copy-start.4 = (bf16[2,256,16,64]{1,3,2,0:T(8,128)(2,1)S(1)}, bf16[2,256,16,64]{1,3,2,0:T(8,128)(2,1)}, u32[]{:S(2)}) copy-start(bf16[2,256,16,64]{1,3,2,0:T(8,128)(2,1)} %copy-done.3) | copy-start | bytes 3145732
  152.3 24.4 %collective-permute-start.8 = (bf16[16,16384]{1,0:T(8,128)(2,1)S(1)}, bf16[16,16384]{1,0:T(8,128)(2,1)S(1)}, u32[]{:S(2)}, u32[]{:S(2)}) collective-permute-start(bf16[16,16384]{1,0:T(8,128)(2,1)S(1)} %fusion.43), channel_id=1, source_target_pairs={{0,32},{8,40},{16,48},{24,56},{32,64},{40,72},{48,80},{56,88},{64,... | collective-permute-start | bytes 1572872 | tf_op jit(solution)/shard_map/ppermute | solution.py:17
  159.9 16.8 %collective-permute-start.2 = (f32[16]{0:T(128)S(1)}, f32[16]{0:T(128)S(1)}, u32[]{:S(2)}, u32[]{:S(2)}) collective-permute-start(f32[16]{0:T(128)S(1)} %get-tuple-element.88), channel_id=1, source_target_pairs={{0,16},{8,24},{16,32},{24,40},{32,48},{40,56},{48,64},{56,72},{64,... | collective-permute-start | bytes 200 | tf_op jit(solution)/shard_map/ppermute | solution.py:16
  177.1 29.8 %collective-permute-start.9 = (bf16[16,16384]{1,0:T(8,128)(2,1)S(1)}, bf16[16,16384]{1,0:T(8,128)(2,1)S(1)}, u32[]{:S(2)}, u32[]{:S(2)}) collective-permute-start(bf16[16,16384]{1,0:T(8,128)(2,1)S(1)} %fusion.40), channel_id=1, source_target_pairs={{0,64},{8,72},{16,80},{24,88},{32,96},{40,104},{48,112},{56,120},{... | collective-permute-start | bytes 1572872 | tf_op jit(solution)/shard_map/ppermute | solution.py:17
  196.8 5.2 %collective-permute-start.3 = (f32[16]{0:T(128)S(1)}, f32[16]{0:T(128)S(1)}, u32[]{:S(2)}, u32[]{:S(2)}) collective-permute-start(f32[16]{0:T(128)S(1)} %get-tuple-element.86), channel_id=1, source_target_pairs={{0,32},{8,40},{16,48},{24,56},{32,64},{40,72},{48,80},{56,88},{64,... | collective-permute-start | bytes 200 | tf_op jit(solution)/shard_map/ppermute | solution.py:16
  209.0 21.5 %collective-permute-start.10 = (bf16[16,16384]{1,0:T(8,128)(2,1)}, bf16[16,16384]{1,0:T(8,128)(2,1)}, u32[]{:S(2)}, u32[]{:S(2)}) collective-permute-start(bf16[16,16384]{1,0:T(8,128)(2,1)} %fusion.42), channel_id=1, source_target_pairs={{0,128},{8,136},{16,144},{24,152},{32,160},{40,168},{48,176},{56,1... | collective-permute-start | bytes 1572872 | tf_op jit(solution)/shard_map/ppermute | solution.py:17
  222.8 7.7 %collective-permute-start.4 = (f32[16]{0:T(128)S(1)}, f32[16]{0:T(128)S(1)}, u32[]{:S(2)}, u32[]{:S(2)}) collective-permute-start(f32[16]{0:T(128)S(1)} %get-tuple-element.84), channel_id=1, source_target_pairs={{0,64},{8,72},{16,80},{24,88},{32,96},{40,104},{48,112},{56,120},{... | collective-permute-start | bytes 200 | tf_op jit(solution)/shard_map/ppermute | solution.py:16
  230.5 6.2 %copy-start.12 = (f32[16]{0:T(128)S(1)}, f32[16]{0:T(128)}, u32[]{:S(2)}) copy-start(f32[16]{0:T(128)} %param.19) | copy-start | bytes 196
  256.5 58.7 %copy-start.5 = (bf16[64,4096]{1,0:T(8,128)(2,1)S(1)}, bf16[64,4096]{1,0:T(8,128)(2,1)}, u32[]{:S(2)}) copy-start(bf16[64,4096]{1,0:T(8,128)(2,1)} %param.22) | copy-start | bytes 1572868
  256.5 62.2 %copy-start.10 = (f32[4096]{0:T(1024)S(1)}, f32[4096]{0:T(1024)}, u32[]{:S(2)}) copy-start(f32[4096]{0:T(1024)} %param.24) | copy-start | bytes 49156
  256.5 117.2 %all-gather.5.cloned.1.call-start = ((), (), s32[]{:S(2)}) async-start(), calls=%async_computation.3 | async-start | bytes 4718592 | tf_op jit(solution)/shard_map/all_gather | solution.py:129
  318.6 65.3 %copy-start.6 = (bf16[64,4096]{1,0:T(8,128)(2,1)}, bf16[64,4096]{1,0:T(8,128)(2,1)S(1)}, u32[]{:S(2)}) copy-start(bf16[64,4096]{1,0:T(8,128)(2,1)S(1)} %get-tuple-element.82) | copy-start | bytes 1572868
  373.7 10.2 %copy-start.1 = (bf16[512,1,256]{2,0,1:T(8,128)(2,1)S(1)}, bf16[512,1,256]{2,0,1:T(8,128)(2,1)}, u32[]{:S(2)}) copy-start(bf16[512,1,256]{2,0,1:T(8,128)(2,1)} %param.17) | copy-start | bytes 786436
  (4 other events, 6.4 us)
Sparse Core Ops, SparseCore 0:
  10.7 161.2 all-gather.2
  256.6 58.5 reduce-scatter.1
  319.8 53.8 all-gather.4

commit v6 on v3

--- a/solution.py
+++ b/solution.py
@@ -88,6 +88,9 @@
     zero_state = jnp.zeros((head_count, state_width, head_width), jnp.float32)
     device_state, local_starts = lax.scan(advance, zero_state, (block_decay, block_state))
     device_decay = jnp.sum(block_decay, axis=0)
+    w_out_all = lax.all_gather(w_out, "seq", axis=1, tiled=True)
+    w_in_late, device_state = lax.optimization_barrier((w_in, device_state))
+    w_in_all = lax.all_gather(w_in_late, "seq", axis=0, tiled=True)
     total_decay, incoming = shift_scan(
         device_decay, device_state.reshape(head_count, state_width * head_width), "seq"
     )
@@ -104,15 +107,14 @@
     grouped = gated.reshape(seq_rows, group_count, per_group * head_width)
     grouped = grouped * lax.rsqrt(jnp.mean(grouped * grouped, axis=-1, keepdims=True) + 1e-05)
     ssd_out = (grouped.reshape(seq_rows, channels) * norm_gain[None, :]).astype(jnp.bfloat16)
-    w_in_all = lax.all_gather(w_in, "seq", axis=0, tiled=True)
-    ssd_out, w_in_all = lax.optimization_barrier((ssd_out, w_in_all))
     partial_sum = jnp.dot(
         ssd_out,
-        lax.all_gather(w_out, "seq", axis=1, tiled=True),
+        w_out_all,
         preferred_element_type=jnp.float32,
-    )
+    ).astype(jnp.bfloat16)
+    partial_sum, w_in_all = lax.optimization_barrier((partial_sum, w_in_all))
     mixer_out = lax.psum_scatter(
-        partial_sum.astype(jnp.bfloat16), "head", scatter_dimension=0, tiled=True
+        partial_sum, "head", scatter_dimension=0, tiled=True
     ).astype(jnp.float32)
     unit = refusal / jnp.sqrt(jnp.sum(refusal * refusal) + 1e-06)
     hidden = residual.astype(jnp.float32) + mixer_out

time: 369 us -> 390 us (1.057)
  waiting for transfers between devices: 186 us -> 206 us
    reduce_scatter x1, waiting for transfers between devices: 59 us -> 80.1 us  [body(): lax.psum_scatter(partial_sum, 'head', scatter_dimension=0, tiled=True)]
    ppermute x6, starting transfers between devices: 51.6 us -> 65 us  [shifted(): lax.ppermute(s.astype(jnp.bfloat16), axis, pairs).astype(jnp.float32)]
    ppermute x5, starting transfers between devices: 31.8 us -> 19.9 us  [shifted(): lax.ppermute(a, axis, pairs)]
    ppermute x5, waiting for transfers between devices: 29.4 us -> 22.9 us  [shifted(): lax.ppermute(a, axis, pairs)]
    ppermute x6, waiting for transfers between devices: 31.1 us -> 36.9 us  [shifted(): lax.ppermute(s.astype(jnp.bfloat16), axis, pairs).astype(jnp.float32)]
  transfers between devices with their start and end apart: 15 -> 15, of which waited for: 10 -> 10; matrix products, arithmetic and copies ran while one was open for 15% -> 17% of each run, Pallas kernels for 0% -> 0%
where the time goes in v6:
time: 390 us; the launch traced here: 389 us
  waiting for transfers between devices  206 us (53%)
  starting transfers between devices  85.4 us (22%)
  matrix products  40.7 us (10%)
  local copies, waits for them, and re-layouts  26.4 us (7%)
  other arithmetic  16.2 us (4%)
  between operations  14.8 us (4%)
    reduce_scatter x1, waiting for transfers between devices, body(): lax.psum_scatter(partial_sum, 'head', scatter_dimension=0, tiled=True)  80.1 us
    ppermute x6, starting transfers between devices, shifted(): lax.ppermute(s.astype(jnp.bfloat16), axis, pairs).astype(jnp.float32)  65 us
    all_gather x1, waiting for transfers between devices, body(): all_rows = lax.all_gather(normed, 'head', axis=0, tiled=True)  54.1 us
    ppermute x6, waiting for transfers between devices, shifted(): lax.ppermute(s.astype(jnp.bfloat16), axis, pairs).astype(jnp.float32)  36.9 us
    ppermute x5, waiting for transfers between devices, shifted(): lax.ppermute(a, axis, pairs)  22.9 us
    ppermute x5, starting transfers between devices, shifted(): lax.ppermute(a, axis, pairs)  19.9 us
    all_gather x1, waiting for transfers between devices, body(): w_in_all = lax.all_gather(w_in_late, 'seq', axis=0, tiled=True)  11.2 us
    dot_general x1, matrix products, body(): next_float = jnp.dot(all_rows, w_in_all, preferred_element_type=jnp.float32)  10.1 us
  transfers between devices with their start and end apart: 15, of which 10 were waited for; matrix products, arithmetic and copies ran while one was open for 17% of the time, Pallas kernels for 0%

profile of v6, /device:TPU:1, one launch (start us, length us, event | category | flops | bytes accessed | tf_op | source)
XLA Modules:
  0.0 389.3 jit_solution(605875987579394651)
XLA Ops:
  10.1 4.0 %reshape.165 = bf16[2,256,16,64]{3,2,1,0:T(8,128)(2,1)} reshape(bf16[512,1024]{1,0:T(8,128)(2,1)} %param.14) | data formatting | bytes 2097152 | tf_op jit(solution)/shard_map/reshape | solution.py:59
  19.3 5.1 %fusion.3 = f32[2,16,256,64]{3,2,1,0:T(8,128)} fusion(bf16[2,256,16,64]{1,3,2,0:T(8,128)(2,1)S(1)} %copy.37, f32[2,256,16]{1,2,0:T(8,128)S(1)} %get-tuple-element.94, f32[2,256,256]{2,1,0:T(8,128)} %convert_element_type.83), kind=kOutput, calls=%fused_computation.9 | convolution fusion | flops 272629760 | bytes 3702784 | tf_op jit(solution)/shard_map/klhn,klhp->khnp/dot_general | solution.py:79
  24.4 7.0 %while.13 = (s32[]{:T(128)}, f32[16,256,64]{2,1,0:T(8,128)S(1)}, f32[2,16,256,64]{3,2,1,0:T(8,128)}, f32[2,16]{1,0:T(2,128)S(1)}, f32[2,16,256,64]{3,2,1,0:T(8,128)}, /*index=5*/s32[]{:T(128)}, s32[]{:T(128)}) while((s32[]{:T(128)}, f32[16,256,64]{2,1,0:T(8,128)S(1)}, f32[2,16,256,64]{3,2,1,0:T(8,128)}, f32[2,16]{1,0:T(2,128)S(1)}, ...), condition=%wide.region_3.4_spmd.clone, body=%wide.region_2.3_spmd.clone.sunk | while | flops 1048579 | bytes 14680892 | solution.py:89
  32.4 6.3 %collective-permute-start.5 = (bf16[16,16384]{1,0:T(8,128)(2,1)S(1)}, bf16[16,16384]{1,0:T(8,128)(2,1)S(1)}, u32[]{:S(2)}, u32[]{:S(2)}) collective-permute-start(bf16[16,16384]{1,0:T(8,128)(2,1)S(1)} %convert_element_type.86), channel_id=1, source_target_pairs={{0,8},{8,16},{16,24},{24,32},{32,40},{40,48},{48,56},{56,64},{64,7... | collective-permute-start | bytes 1572872 | tf_op jit(solution)/shard_map/ppermute | solution.py:17
  38.7 11.5 %collective-permute-done.5 = bf16[16,16384]{1,0:T(8,128)(2,1)S(1)} collective-permute-done((bf16[16,16384]{1,0:T(8,128)(2,1)S(1)}, bf16[16,16384]{1,0:T(8,128)(2,1)S(1)}, u32[]{:S(2)}, u32[]{:S(2)}) %collective-permute-start.5) | collective-permute-done | bytes 524320 | tf_op jit(solution)/shard_map/ppermute | solution.py:17
  50.3 5.3 %collective-permute-start.6 = (bf16[16,16384]{1,0:T(8,128)(2,1)S(1)}, bf16[16,16384]{1,0:T(8,128)(2,1)S(1)}, u32[]{:S(2)}, u32[]{:S(2)}) collective-permute-start(bf16[16,16384]{1,0:T(8,128)(2,1)S(1)} %collective-permute-done.5), channel_id=1, source_target_pairs={{0,8},{8,16},{16,24},{24,32},{32,40},{40,48},{48,56},{56,64},{64,7... | collective-permute-start | bytes 1572872 | tf_op jit(solution)/shard_map/ppermute | solution.py:17
  57.5 10.2 %collective-permute-done = f32[16]{0:T(128)S(1)} collective-permute-done((f32[16]{0:T(128)S(1)}, f32[16]{0:T(128)S(1)}, u32[]{:S(2)}, u32[]{:S(2)}) %collective-permute-start) | collective-permute-done | bytes 96 | tf_op jit(solution)/shard_map/ppermute | solution.py:16
  67.6 5.3 %collective-permute-start.1 = (f32[16]{0:T(128)S(1)}, f32[16]{0:T(128)S(1)}, u32[]{:S(2)}, u32[]{:S(2)}) collective-permute-start(f32[16]{0:T(128)S(1)} %collective-permute-done), channel_id=1, source_target_pairs={{0,8},{8,16},{16,24},{24,32},{32,40},{40,48},{48,56},{56,64},{64,7... | collective-permute-start | bytes 200 | tf_op jit(solution)/shard_map/ppermute | solution.py:16
  73.9 29.3 %collective-permute-start.7 = (bf16[16,16384]{1,0:T(8,128)(2,1)S(1)}, bf16[16,16384]{1,0:T(8,128)(2,1)S(1)}, u32[]{:S(2)}, u32[]{:S(2)}) collective-permute-start(bf16[16,16384]{1,0:T(8,128)(2,1)S(1)} %fusion.29), channel_id=1, source_target_pairs={{0,16},{8,24},{16,32},{24,40},{32,48},{40,56},{48,64},{56,72},{64,... | collective-permute-start | bytes 1572872 | tf_op jit(solution)/shard_map/ppermute | solution.py:17
  103.3 25.3 %collective-permute-done.7 = bf16[16,16384]{1,0:T(8,128)(2,1)S(1)} collective-permute-done((bf16[16,16384]{1,0:T(8,128)(2,1)S(1)}, bf16[16,16384]{1,0:T(8,128)(2,1)S(1)}, u32[]{:S(2)}, u32[]{:S(2)}) %collective-permute-start.7) | collective-permute-done | bytes 524320 | tf_op jit(solution)/shard_map/ppermute | solution.py:17
  128.9 4.5 %collective-permute-start.8 = (bf16[16,16384]{1,0:T(8,128)(2,1)S(1)}, bf16[16,16384]{1,0:T(8,128)(2,1)S(1)}, u32[]{:S(2)}, u32[]{:S(2)}) collective-permute-start(bf16[16,16384]{1,0:T(8,128)(2,1)S(1)} %fusion.33), channel_id=1, source_target_pairs={{0,32},{8,40},{16,48},{24,56},{32,64},{40,72},{48,80},{56,88},{64,... | collective-permute-start | bytes 1572872 | tf_op jit(solution)/shard_map/ppermute | solution.py:17
  136.6 11.3 %collective-permute-done.2 = f32[16]{0:T(128)S(1)} collective-permute-done((f32[16]{0:T(128)S(1)}, f32[16]{0:T(128)S(1)}, u32[]{:S(2)}, u32[]{:S(2)}) %collective-permute-start.2) | collective-permute-done | bytes 96 | tf_op jit(solution)/shard_map/ppermute | solution.py:16
  148.4 12.9 %collective-permute-start.9 = (bf16[16,16384]{1,0:T(8,128)(2,1)S(1)}, bf16[16,16384]{1,0:T(8,128)(2,1)S(1)}, u32[]{:S(2)}, u32[]{:S(2)}) collective-permute-start(bf16[16,16384]{1,0:T(8,128)(2,1)S(1)} %fusion.30), channel_id=1, source_target_pairs={{0,64},{8,72},{16,80},{24,88},{32,96},{40,104},{48,112},{56,120},{... | collective-permute-start | bytes 1572872 | tf_op jit(solution)/shard_map/ppermute | solution.py:17
  162.6 5.8 %collective-permute-start.3 = (f32[16]{0:T(128)S(1)}, f32[16]{0:T(128)S(1)}, u32[]{:S(2)}, u32[]{:S(2)}) collective-permute-start(f32[16]{0:T(128)S(1)} %get-tuple-element.90), channel_id=1, source_target_pairs={{0,32},{8,40},{16,48},{24,56},{32,64},{40,72},{48,80},{56,88},{64,... | collective-permute-start | bytes 200 | tf_op jit(solution)/shard_map/ppermute | solution.py:16
  171.3 6.8 %collective-permute-start.10 = (bf16[16,16384]{1,0:T(8,128)(2,1)}, bf16[16,16384]{1,0:T(8,128)(2,1)}, u32[]{:S(2)}, u32[]{:S(2)}) collective-permute-start(bf16[16,16384]{1,0:T(8,128)(2,1)} %fusion.32), channel_id=1, source_target_pairs={{0,128},{8,136},{16,144},{24,152},{32,160},{40,168},{48,176},{56,1... | collective-permute-start | bytes 1572872 | tf_op jit(solution)/shard_map/ppermute | solution.py:17
  178.1 4.1 %fusion.2 = f32[2,16,256,64]{2,3,1,0:T(8,128)} fusion(bf16[2,256,16,64]{1,3,2,0:T(8,128)(2,1)S(1)} %copy-done.4, f32[2,256,256]{2,1,0:T(8,128)S(1)} %fusion.37, f32[2,16,256]{2,1,0:T(8,128)S(1)} %copy_bitcast_fusion, pred[256,256]{1,0:T(8,128)(4,1)S(1)} %iota_compare_fusion), kind=kOutput, calls=%fused_computation.8 | convolution fusion | flops 278921216 | bytes 3768320 | tf_op jit(solution)/shard_map/khls,kshp->klhp/dot_general | solution.py:73
  182.2 4.1 %reshape.166 = f32[2,256,16,64]{3,2,1,0:T(8,128)} reshape(bf16[512,1024]{1,0:T(8,128)(2,1)} %param.15) | data formatting | bytes 3145728 | tf_op jit(solution)/shard_map/convert_element_type | solution.py:105
  190.0 4.6 %copy.44 = f32[2,256,16,64]{1,3,2,0:T(8,128)} copy(f32[2,256,16,64]{3,2,1,0:T(8,128)} %reshape.166) | data formatting | bytes 4194304 | tf_op jit(solution)/shard_map/convert_element_type | solution.py:105
  201.1 8.1 %multiply_reduce_fusion = (f32[2,256]{1,0:T(2,128)S(1)}, f32[2,256,16,64]{1,3,2,0:T(8,128)S(1)}) fusion(f32[2,256,16,64]{1,3,2,0:T(8,128)} %copy.44, bf16[2,256,16,64]{1,3,2,0:T(8,128)(2,1)S(1)} %copy-done.4, f32[16]{0:T(128)S(1)} %copy-done.11, f32[2,256,16]{1,2,0:T(8,128)S(1)} %get-tuple-element.93, bf16[2,256,256]{2,1,0:T(8,128)(2,1)S(1)} %bitcast.68, ...), kind=kOutput, calls=%fused_computation.25 | convolution fusion | flops 1617952256 | bytes 10782912 | tf_op jit(solution)/shard_map/klhn,khnp->klhp/dot_general | solution.py:101
  211.2 10.0 %convolution_convert_fusion = bf16[512,4096]{1,0:T(8,128)(2,1)} fusion(bf16[1024,4096]{1,0:T(8,128)(2,1)} %all-gather.4.cloned.1.call-done, f32[512,1024]{0,1:T(8,128)S(1)} %bitcast.70, f32[1024]{0:T(1024)S(1)} %copy-done.10, f32[512]{0:T(512)S(1)} %bitcast.75), kind=kOutput, calls=%fused_computation.7 | convolution fusion | flops 4298637312 | bytes 14686208 | tf_op jit(solution)/shard_map/dot_general | solution.py:110
  221.2 11.2 %all-gather.6.cloned.1.call-done = bf16[4096,1024]{1,0:T(8,128)(2,1)} async-done(((bf16[128,1024]{1,0:T(8,128)(2,1)}), bf16[4096,1024]{1,0:T(8,128)(2,1)}) %all-gather.6.cloned.1.call-update) | async-done | bytes 8388624 | tf_op jit(solution)/shard_map/all_gather | solution.py:93
  233.9 80.1 %reduce-scatter.2.cloned.1.call-done = bf16[64,4096]{1,0:T(8,128)(2,1)} async-done(((bf16[512,4096]{1,0:T(8,128)(2,1)}), bf16[64,4096]{1,0:T(8,128)(2,1)}) %reduce-scatter.2.cloned.1.call-update) | async-done | bytes 524304 | tf_op jit(solution)/shard_map/reduce_scatter | solution.py:116
  318.5 54.1 %all-gather.8.cloned.1.call-done = bf16[512,4096]{1,0:T(8,128)(2,1)} async-done(((bf16[64,4096]{1,0:T(8,128)(2,1)}), bf16[512,4096]{1,0:T(8,128)(2,1)}) %all-gather.8.cloned.1.call-update) | async-done | bytes 4194320 | tf_op jit(solution)/shard_map/all_gather | solution.py:129
  372.6 10.1 %convolution_convert_fusion.1 = bf16[512,1024]{1,0:T(8,128)(2,1)} fusion(bf16[512,4096]{1,0:T(8,128)(2,1)} %all-gather.8.cloned.1.call-done, bf16[4096,1024]{1,0:T(8,128)(2,1)} %all-gather.6.cloned.1.call-done), kind=kOutput, calls=%fused_computation.29 | convolution fusion | flops 4295491584 | bytes 13631488 | tf_op jit(solution)/shard_map/dot_general | solution.py:130
  (89 shorter events, 44.5 us)
Async XLA Ops:
  7.2 154.2 %copy-start = (bf16[512,1,256]{2,0,1:T(8,128)(2,1)S(1)}, bf16[512,1,256]{2,0,1:T(8,128)(2,1)}, u32[]{:S(2)}) copy-start(bf16[512,1,256]{2,0,1:T(8,128)(2,1)} %param.17) | copy-start | bytes 786436
  7.2 204.0 %all-gather.4.cloned.1.call-start = ((), (), s32[]{:S(2)}) async-start(), calls=%async_computation.1 | async-start | bytes 8650752 | tf_op jit(solution)/shard_map/all_gather | solution.py:91
  7.9 224.4 %all-gather.6.cloned.1.call-start = ((), (), s32[]{:S(2)}) async-start(), calls=%async_computation.2 | async-start | bytes 8650752 | tf_op jit(solution)/shard_map/all_gather | solution.py:93
  16.9 7.5 %copy-start.3 = (bf16[2,256,16,64]{1,3,2,0:T(8,128)(2,1)}, bf16[2,256,16,64]{1,3,2,0:T(8,128)(2,1)S(1)}, u32[]{:S(2)}) copy-start(bf16[2,256,16,64]{1,3,2,0:T(8,128)(2,1)S(1)} %copy.37) | copy-start | bytes 3145732
  32.4 17.8 %collective-permute-start.5 = (bf16[16,16384]{1,0:T(8,128)(2,1)S(1)}, bf16[16,16384]{1,0:T(8,128)(2,1)S(1)}, u32[]{:S(2)}, u32[]{:S(2)}) collective-permute-start(bf16[16,16384]{1,0:T(8,128)(2,1)S(1)} %convert_element_type.86), channel_id=1, source_target_pairs={{0,8},{8,16},{16,24},{24,32},{32,40},{40,48},{48,56},{56,64},{64,7... | collective-permute-start | bytes 1572872 | tf_op jit(solution)/shard_map/ppermute | solution.py:17
  50.3 23.4 %collective-permute-start.6 = (bf16[16,16384]{1,0:T(8,128)(2,1)S(1)}, bf16[16,16384]{1,0:T(8,128)(2,1)S(1)}, u32[]{:S(2)}, u32[]{:S(2)}) collective-permute-start(bf16[16,16384]{1,0:T(8,128)(2,1)S(1)} %collective-permute-done.5), channel_id=1, source_target_pairs={{0,8},{8,16},{16,24},{24,32},{32,40},{40,48},{48,56},{56,64},{64,7... | collective-permute-start | bytes 1572872 | tf_op jit(solution)/shard_map/ppermute | solution.py:17
  55.6 12.1 %collective-permute-start = (f32[16]{0:T(128)S(1)}, f32[16]{0:T(128)S(1)}, u32[]{:S(2)}, u32[]{:S(2)}) collective-permute-start(f32[16]{0:T(128)S(1)} %get-tuple-element.73), channel_id=1, source_target_pairs={{0,8},{8,16},{16,24},{24,32},{32,40},{40,48},{48,56},{56,64},{64,7... | collective-permute-start | bytes 200 | tf_op jit(solution)/shard_map/ppermute | solution.py:16
  67.6 6.0 %collective-permute-start.1 = (f32[16]{0:T(128)S(1)}, f32[16]{0:T(128)S(1)}, u32[]{:S(2)}, u32[]{:S(2)}) collective-permute-start(f32[16]{0:T(128)S(1)} %collective-permute-done), channel_id=1, source_target_pairs={{0,8},{8,16},{16,24},{24,32},{32,40},{40,48},{48,56},{56,64},{64,7... | collective-permute-start | bytes 200 | tf_op jit(solution)/shard_map/ppermute | solution.py:16
  73.9 54.7 %collective-permute-start.7 = (bf16[16,16384]{1,0:T(8,128)(2,1)S(1)}, bf16[16,16384]{1,0:T(8,128)(2,1)S(1)}, u32[]{:S(2)}, u32[]{:S(2)}) collective-permute-start(bf16[16,16384]{1,0:T(8,128)(2,1)S(1)} %fusion.29), channel_id=1, source_target_pairs={{0,16},{8,24},{16,32},{24,40},{32,48},{40,56},{48,64},{56,72},{64,... | collective-permute-start | bytes 1572872 | tf_op jit(solution)/shard_map/ppermute | solution.py:17
  103.2 210.8 %reduce-scatter.2.cloned.1.call-start = ((), (), s32[]{:S(2)}) async-start(), calls=%async_computation.3 | async-start | bytes 4718592 | tf_op jit(solution)/shard_map/reduce_scatter | solution.py:116
  128.6 49.5 %copy-start.4 = (bf16[2,256,16,64]{1,3,2,0:T(8,128)(2,1)S(1)}, bf16[2,256,16,64]{1,3,2,0:T(8,128)(2,1)}, u32[]{:S(2)}) copy-start(bf16[2,256,16,64]{1,3,2,0:T(8,128)(2,1)} %copy-done.3) | copy-start | bytes 3145732
  128.9 19.1 %collective-permute-start.8 = (bf16[16,16384]{1,0:T(8,128)(2,1)S(1)}, bf16[16,16384]{1,0:T(8,128)(2,1)S(1)}, u32[]{:S(2)}, u32[]{:S(2)}) collective-permute-start(bf16[16,16384]{1,0:T(8,128)(2,1)S(1)} %fusion.33), channel_id=1, source_target_pairs={{0,32},{8,40},{16,48},{24,56},{32,64},{40,72},{48,80},{56,88},{64,... | collective-permute-start | bytes 1572872 | tf_op jit(solution)/shard_map/ppermute | solution.py:17
  133.4 14.6 %collective-permute-start.2 = (f32[16]{0:T(128)S(1)}, f32[16]{0:T(128)S(1)}, u32[]{:S(2)}, u32[]{:S(2)}) collective-permute-start(f32[16]{0:T(128)S(1)} %get-tuple-element.92), channel_id=1, source_target_pairs={{0,16},{8,24},{16,32},{24,40},{32,48},{40,56},{48,64},{56,72},{64,... | collective-permute-start | bytes 200 | tf_op jit(solution)/shard_map/ppermute | solution.py:16
  148.4 20.8 %collective-permute-start.9 = (bf16[16,16384]{1,0:T(8,128)(2,1)S(1)}, bf16[16,16384]{1,0:T(8,128)(2,1)S(1)}, u32[]{:S(2)}, u32[]{:S(2)}) collective-permute-start(bf16[16,16384]{1,0:T(8,128)(2,1)S(1)} %fusion.30), channel_id=1, source_target_pairs={{0,64},{8,72},{16,80},{24,88},{32,96},{40,104},{48,112},{56,120},{... | collective-permute-start | bytes 1572872 | tf_op jit(solution)/shard_map/ppermute | solution.py:17
  162.6 6.5 %collective-permute-start.3 = (f32[16]{0:T(128)S(1)}, f32[16]{0:T(128)S(1)}, u32[]{:S(2)}, u32[]{:S(2)}) collective-permute-start(f32[16]{0:T(128)S(1)} %get-tuple-element.90), channel_id=1, source_target_pairs={{0,32},{8,40},{16,48},{24,56},{32,64},{40,72},{48,80},{56,88},{64,... | collective-permute-start | bytes 200 | tf_op jit(solution)/shard_map/ppermute | solution.py:16
  171.3 23.3 %collective-permute-start.10 = (bf16[16,16384]{1,0:T(8,128)(2,1)}, bf16[16,16384]{1,0:T(8,128)(2,1)}, u32[]{:S(2)}, u32[]{:S(2)}) collective-permute-start(bf16[16,16384]{1,0:T(8,128)(2,1)} %fusion.32), channel_id=1, source_target_pairs={{0,128},{8,136},{16,144},{24,152},{32,160},{40,168},{48,176},{56,1... | collective-permute-start | bytes 1572872 | tf_op jit(solution)/shard_map/ppermute | solution.py:17
  186.4 8.3 %collective-permute-start.4 = (f32[16]{0:T(128)S(1)}, f32[16]{0:T(128)S(1)}, u32[]{:S(2)}, u32[]{:S(2)}) collective-permute-start(f32[16]{0:T(128)S(1)} %get-tuple-element.88), channel_id=1, source_target_pairs={{0,64},{8,72},{16,80},{24,88},{32,96},{40,104},{48,112},{56,120},{... | collective-permute-start | bytes 200 | tf_op jit(solution)/shard_map/ppermute | solution.py:16
  194.6 6.5 %copy-start.11 = (f32[16]{0:T(128)S(1)}, f32[16]{0:T(128)}, u32[]{:S(2)}) copy-start(f32[16]{0:T(128)} %param.19) | copy-start | bytes 196
  221.1 11.5 %copy-start.8 = (f32[4096]{0:T(1024)S(1)}, f32[4096]{0:T(1024)}, u32[]{:S(2)}) copy-start(f32[4096]{0:T(1024)} %param.23) | copy-start | bytes 49156
  221.2 92.9 %copy-start.5 = (bf16[64,4096]{1,0:T(8,128)(2,1)S(1)}, bf16[64,4096]{1,0:T(8,128)(2,1)}, u32[]{:S(2)}) copy-start(bf16[64,4096]{1,0:T(8,128)(2,1)} %param.22) | copy-start | bytes 1572868
  221.2 96.3 %copy-start.9 = (f32[4096]{0:T(1024)S(1)}, f32[4096]{0:T(1024)}, u32[]{:S(2)}) copy-start(f32[4096]{0:T(1024)} %param.24) | copy-start | bytes 49156
  232.3 140.2 %all-gather.8.cloned.1.call-start = ((), (), s32[]{:S(2)}) async-start(), calls=%async_computation.4 | async-start | bytes 4718592 | tf_op jit(solution)/shard_map/all_gather | solution.py:129
  317.5 65.3 %copy-start.6 = (bf16[64,4096]{1,0:T(8,128)(2,1)}, bf16[64,4096]{1,0:T(8,128)(2,1)S(1)}, u32[]{:S(2)}) copy-start(bf16[64,4096]{1,0:T(8,128)(2,1)S(1)} %get-tuple-element.86) | copy-start | bytes 1572868
  372.6 10.2 %copy-start.1 = (bf16[512,1,256]{2,0,1:T(8,128)(2,1)S(1)}, bf16[512,1,256]{2,0,1:T(8,128)(2,1)}, u32[]{:S(2)}) copy-start(bf16[512,1,256]{2,0,1:T(8,128)(2,1)} %param.17) | copy-start | bytes 786436
  (4 other events, 8.7 us)
Sparse Core Ops, SparseCore 0:
  10.5 116.6 all-gather.3
  129.7 102.5 all-gather.5
  234.9 79.0 reduce-scatter.1
  318.6 53.9 all-gather.7

commit v7 on v3

--- a/solution.py
+++ b/solution.py
@@ -111,20 +111,26 @@
         lax.all_gather(w_out, "seq", axis=1, tiled=True),
         preferred_element_type=jnp.float32,
     )
-    mixer_out = lax.psum_scatter(
-        partial_sum.astype(jnp.bfloat16), "head", scatter_dimension=0, tiled=True
-    ).astype(jnp.float32)
+    own_rows = residual.shape[0]
+    mine = lax.axis_index("head")
+    with_residual = lax.dynamic_update_slice_in_dim(
+        partial_sum,
+        lax.dynamic_slice_in_dim(partial_sum, mine * own_rows, own_rows)
+        + residual.astype(jnp.float32),
+        mine * own_rows,
+        axis=0,
+    )
+    hidden = lax.psum(with_residual.astype(jnp.bfloat16), "head").astype(jnp.float32)
     unit = refusal / jnp.sqrt(jnp.sum(refusal * refusal) + 1e-06)
-    hidden = residual.astype(jnp.float32) + mixer_out
     coef = jnp.dot(hidden, unit, precision=lax.Precision.HIGHEST)
-    stream = (hidden - coef[:, None] * unit[None, :]).astype(jnp.bfloat16)
-    stream_float = stream.astype(jnp.float32)
-    normed = (
+    stream_all = (hidden - coef[:, None] * unit[None, :]).astype(jnp.bfloat16)
+    stream_float = stream_all.astype(jnp.float32)
+    all_rows = (
         stream_float
         * lax.rsqrt(jnp.mean(stream_float * stream_float, axis=-1, keepdims=True) + 1e-05)
         * stream_gain[None, :]
     ).astype(jnp.bfloat16)
-    all_rows = lax.all_gather(normed, "head", axis=0, tiled=True)
+    stream = lax.dynamic_slice_in_dim(stream_all, mine * own_rows, own_rows)
     next_float = jnp.dot(
         all_rows,
         w_in_all,

time: 369 us -> 368 us (level)
  waiting for transfers between devices: 186 us -> 193 us
  starting transfers between devices: 83.8 us -> 77.4 us
  matrix products: 39.9 us -> 36.1 us
    psum x0 -> x1, waiting for transfers between devices: none -> 112 us  [body(): lax.psum(with_residual.astype(jnp.bfloat16), 'head').astype(jnp.float32)]
    reduce_scatter x1 -> x0, waiting for transfers between devices: 59 us -> none  [body(): lax.psum_scatter(partial_sum.astype(jnp.bfloat16), 'head', scatter_dimens...]
    all_gather x1 -> x0, waiting for transfers between devices: 54.1 us -> none  [body(): all_rows = lax.all_gather(normed, 'head', axis=0, tiled=True)]
    ppermute x5, waiting for transfers between devices: 29.4 us -> 35.8 us  [shifted(): lax.ppermute(a, axis, pairs)]
    ppermute x6, starting transfers between devices: 51.6 us -> 46.9 us  [shifted(): lax.ppermute(s.astype(jnp.bfloat16), axis, pairs).astype(jnp.float32)]
    dot_general x1, matrix products: 10.1 us -> 5.61 us  [body(): next_float = jnp.dot(all_rows, w_in_all, preferred_element_type=jnp.float32)]
  transfers between devices with their start and end apart: 15 -> 14, of which waited for: 10 -> 10; matrix products, arithmetic and copies ran while one was open for 15% -> 14% of each run, Pallas kernels for 0% -> 0%
where the time goes in v7:
time: 368 us; the launch traced here: 367 us
  waiting for transfers between devices  193 us (52%)
  starting transfers between devices  77.4 us (21%)
  matrix products  36.1 us (10%)
  local copies, waits for them, and re-layouts  27.3 us (7%)
  other arithmetic  18.4 us (5%)
  between operations  14.8 us (4%)
    psum x1, waiting for transfers between devices, body(): lax.psum(with_residual.astype(jnp.bfloat16), 'head').astype(jnp.float32)  112 us
    ppermute x6, starting transfers between devices, shifted(): lax.ppermute(s.astype(jnp.bfloat16), axis, pairs).astype(jnp.float32)  46.9 us
    ppermute x5, waiting for transfers between devices, shifted(): lax.ppermute(a, axis, pairs)  35.8 us
    ppermute x6, waiting for transfers between devices, shifted(): lax.ppermute(s.astype(jnp.bfloat16), axis, pairs).astype(jnp.float32)  31.3 us
    ppermute x5, starting transfers between devices, shifted(): lax.ppermute(a, axis, pairs)  30.3 us
    all_gather x1, waiting for transfers between devices, body(): lax.all_gather(w_out, 'seq', axis=1, tiled=True)  12.9 us
    convert_element_type x2, local copies, waits for them, and re-layouts, body(): gate_z.reshape(block_count, SPAN, head_count, head_width)  8.69 us
  transfers between devices with their start and end apart: 14, of which 10 were waited for; matrix products, arithmetic and copies ran while one was open for 14% of the time, Pallas kernels for 0%

profile of v7, /device:TPU:1, one launch (start us, length us, event | category | flops | bytes accessed | tf_op | source)
XLA Modules:
  0.0 366.9 jit_solution(14177775520396151558)
XLA Ops:
  19.3 5.1 %fusion.6 = f32[2,16,256,64]{3,2,1,0:T(8,128)} fusion(bf16[2,256,16,64]{1,3,2,0:T(8,128)(2,1)S(1)} %copy.37, f32[2,256,16]{1,2,0:T(8,128)S(1)} %get-tuple-element.90, f32[2,256,256]{2,1,0:T(8,128)} %convert_element_type.82), kind=kOutput, calls=%fused_computation.14 | convolution fusion | flops 272629760 | bytes 3702784 | tf_op jit(solution)/shard_map/klhn,klhp->khnp/dot_general | solution.py:79
  24.4 7.0 %while.13 = (s32[]{:T(128)}, f32[16,256,64]{2,1,0:T(8,128)S(1)}, f32[2,16,256,64]{3,2,1,0:T(8,128)}, f32[2,16]{1,0:T(2,128)S(1)}, f32[2,16,256,64]{3,2,1,0:T(8,128)}, /*index=5*/s32[]{:T(128)}, s32[]{:T(128)}) while((s32[]{:T(128)}, f32[16,256,64]{2,1,0:T(8,128)S(1)}, f32[2,16,256,64]{3,2,1,0:T(8,128)}, f32[2,16]{1,0:T(2,128)S(1)}, ...), condition=%wide.region_3.4_spmd.clone, body=%wide.region_2.3_spmd.clone.sunk | while | flops 1048579 | bytes 14680892 | solution.py:89
  32.4 6.3 %collective-permute-start.5 = (bf16[16,16384]{1,0:T(8,128)(2,1)S(1)}, bf16[16,16384]{1,0:T(8,128)(2,1)S(1)}, u32[]{:S(2)}, u32[]{:S(2)}) collective-permute-start(bf16[16,16384]{1,0:T(8,128)(2,1)S(1)} %convert_element_type.85), channel_id=1, source_target_pairs={{0,8},{8,16},{16,24},{24,32},{32,40},{40,48},{48,56},{56,64},{64,7... | collective-permute-start | bytes 1572872 | tf_op jit(solution)/shard_map/ppermute | solution.py:17
  38.7 11.5 %collective-permute-done.5 = bf16[16,16384]{1,0:T(8,128)(2,1)S(1)} collective-permute-done((bf16[16,16384]{1,0:T(8,128)(2,1)S(1)}, bf16[16,16384]{1,0:T(8,128)(2,1)S(1)}, u32[]{:S(2)}, u32[]{:S(2)}) %collective-permute-start.5) | collective-permute-done | bytes 524320 | tf_op jit(solution)/shard_map/ppermute | solution.py:17
  50.3 5.3 %collective-permute-start.6 = (bf16[16,16384]{1,0:T(8,128)(2,1)S(1)}, bf16[16,16384]{1,0:T(8,128)(2,1)S(1)}, u32[]{:S(2)}, u32[]{:S(2)}) collective-permute-start(bf16[16,16384]{1,0:T(8,128)(2,1)S(1)} %collective-permute-done.5), channel_id=1, source_target_pairs={{0,8},{8,16},{16,24},{24,32},{32,40},{40,48},{48,56},{56,64},{64,7... | collective-permute-start | bytes 1572872 | tf_op jit(solution)/shard_map/ppermute | solution.py:17
  58.7 25.4 %collective-permute-done = f32[16]{0:T(128)S(1)} collective-permute-done((f32[16]{0:T(128)S(1)}, f32[16]{0:T(128)S(1)}, u32[]{:S(2)}, u32[]{:S(2)}) %collective-permute-start) | collective-permute-done | bytes 96 | tf_op jit(solution)/shard_map/ppermute | solution.py:16
  84.1 6.7 %collective-permute-start.1 = (f32[16]{0:T(128)S(1)}, f32[16]{0:T(128)S(1)}, u32[]{:S(2)}, u32[]{:S(2)}) collective-permute-start(f32[16]{0:T(128)S(1)} %collective-permute-done), channel_id=1, source_target_pairs={{0,8},{8,16},{16,24},{24,32},{32,40},{40,48},{48,56},{56,64},{64,7... | collective-permute-start | bytes 200 | tf_op jit(solution)/shard_map/ppermute | solution.py:16
  91.7 6.5 %collective-permute-start.7 = (bf16[16,16384]{1,0:T(8,128)(2,1)S(1)}, bf16[16,16384]{1,0:T(8,128)(2,1)S(1)}, u32[]{:S(2)}, u32[]{:S(2)}) collective-permute-start(bf16[16,16384]{1,0:T(8,128)(2,1)S(1)} %fusion.34), channel_id=1, source_target_pairs={{0,16},{8,24},{16,32},{24,40},{32,48},{40,56},{48,64},{56,72},{64,... | collective-permute-start | bytes 1572872 | tf_op jit(solution)/shard_map/ppermute | solution.py:17
  98.3 14.3 %collective-permute-done.7 = bf16[16,16384]{1,0:T(8,128)(2,1)S(1)} collective-permute-done((bf16[16,16384]{1,0:T(8,128)(2,1)S(1)}, bf16[16,16384]{1,0:T(8,128)(2,1)S(1)}, u32[]{:S(2)}, u32[]{:S(2)}) %collective-permute-start.7) | collective-permute-done | bytes 524320 | tf_op jit(solution)/shard_map/ppermute | solution.py:17
  113.0 4.7 %collective-permute-start.8 = (bf16[16,16384]{1,0:T(8,128)(2,1)S(1)}, bf16[16,16384]{1,0:T(8,128)(2,1)S(1)}, u32[]{:S(2)}, u32[]{:S(2)}) collective-permute-start(bf16[16,16384]{1,0:T(8,128)(2,1)S(1)} %fusion.38), channel_id=1, source_target_pairs={{0,32},{8,40},{16,48},{24,56},{32,64},{40,72},{48,80},{56,88},{64,... | collective-permute-start | bytes 1572872 | tf_op jit(solution)/shard_map/ppermute | solution.py:17
  117.7 16.1 %collective-permute-start.2 = (f32[16]{0:T(128)S(1)}, f32[16]{0:T(128)S(1)}, u32[]{:S(2)}, u32[]{:S(2)}) collective-permute-start(f32[16]{0:T(128)S(1)} %get-tuple-element.88), channel_id=1, source_target_pairs={{0,16},{8,24},{16,32},{24,40},{32,48},{40,56},{48,64},{56,72},{64,... | collective-permute-start | bytes 200 | tf_op jit(solution)/shard_map/ppermute | solution.py:16
  133.9 8.5 %collective-permute-done.2 = f32[16]{0:T(128)S(1)} collective-permute-done((f32[16]{0:T(128)S(1)}, f32[16]{0:T(128)S(1)}, u32[]{:S(2)}, u32[]{:S(2)}) %collective-permute-start.2) | collective-permute-done | bytes 96 | tf_op jit(solution)/shard_map/ppermute | solution.py:16
  142.8 18.7 %collective-permute-start.9 = (bf16[16,16384]{1,0:T(8,128)(2,1)S(1)}, bf16[16,16384]{1,0:T(8,128)(2,1)S(1)}, u32[]{:S(2)}, u32[]{:S(2)}) collective-permute-start(bf16[16,16384]{1,0:T(8,128)(2,1)S(1)} %fusion.35), channel_id=1, source_target_pairs={{0,64},{8,72},{16,80},{24,88},{32,96},{40,104},{48,112},{56,120},{... | collective-permute-start | bytes 1572872 | tf_op jit(solution)/shard_map/ppermute | solution.py:17
  166.4 5.5 %collective-permute-done.9 = bf16[16,16384]{1,0:T(8,128)(2,1)S(1)} collective-permute-done((bf16[16,16384]{1,0:T(8,128)(2,1)S(1)}, bf16[16,16384]{1,0:T(8,128)(2,1)S(1)}, u32[]{:S(2)}, u32[]{:S(2)}) %collective-permute-start.9) | collective-permute-done | bytes 524320 | tf_op jit(solution)/shard_map/ppermute | solution.py:17
  174.0 5.4 %collective-permute-start.10 = (bf16[16,16384]{1,0:T(8,128)(2,1)}, bf16[16,16384]{1,0:T(8,128)(2,1)}, u32[]{:S(2)}, u32[]{:S(2)}) collective-permute-start(bf16[16,16384]{1,0:T(8,128)(2,1)} %fusion.37), channel_id=1, source_target_pairs={{0,128},{8,136},{16,144},{24,152},{32,160},{40,168},{48,176},{56,1... | collective-permute-start | bytes 1572872 | tf_op jit(solution)/shard_map/ppermute | solution.py:17
  179.4 4.1 %fusion.5 = f32[2,16,256,64]{2,3,1,0:T(8,128)} fusion(bf16[2,256,16,64]{1,3,2,0:T(8,128)(2,1)S(1)} %copy-done.5, f32[2,256,256]{2,1,0:T(8,128)S(1)} %fusion.42, f32[2,16,256]{2,1,0:T(8,128)S(1)} %copy_bitcast_fusion, pred[256,256]{1,0:T(8,128)(4,1)S(1)} %iota_compare_fusion), kind=kOutput, calls=%fused_computation.13 | convolution fusion | flops 278921216 | bytes 3768320 | tf_op jit(solution)/shard_map/khls,kshp->klhp/dot_general | solution.py:73
  183.5 4.1 %reshape.166 = f32[2,256,16,64]{3,2,1,0:T(8,128)} reshape(bf16[512,1024]{1,0:T(8,128)(2,1)} %param.15) | data formatting | bytes 3145728 | tf_op jit(solution)/shard_map/convert_element_type | solution.py:102
  187.6 4.6 %copy.44 = f32[2,256,16,64]{1,3,2,0:T(8,128)} copy(f32[2,256,16,64]{3,2,1,0:T(8,128)} %reshape.166) | data formatting | bytes 4194304 | tf_op jit(solution)/shard_map/convert_element_type | solution.py:102
  199.1 7.3 %multiply_reduce_fusion = (f32[2,256]{1,0:T(2,128)S(1)}, f32[2,256,16,64]{1,3,2,0:T(8,128)S(1)}) fusion(f32[2,256,16,64]{1,3,2,0:T(8,128)} %copy.44, bf16[2,256,16,64]{1,3,2,0:T(8,128)(2,1)S(1)} %copy-done.5, f32[16]{0:T(128)S(1)} %copy-done.12, f32[2,256,16]{1,2,0:T(8,128)S(1)} %get-tuple-element.89, bf16[2,256,256]{2,1,0:T(8,128)(2,1)S(1)} %bitcast.68, ...), kind=kOutput, calls=%fused_computation.33 | convolution fusion | flops 1617952256 | bytes 10782912 | tf_op jit(solution)/shard_map/klhn,khnp->klhp/dot_general | solution.py:98
  208.6 12.9 %all-gather.5.cloned.1.call-done = bf16[1024,4096]{1,0:T(8,128)(2,1)} async-done(((bf16[1024,128]{1,0:T(8,128)(2,1)}), bf16[1024,4096]{1,0:T(8,128)(2,1)}) %all-gather.5.cloned.1.call-update) | async-done | bytes 8388624 | tf_op jit(solution)/shard_map/all_gather | solution.py:111
  221.4 7.1 %fusion.43 = f32[512,4096]{1,0:T(8,128)S(1)} fusion(bf16[512,1024]{0,1:T(8,128)(2,1)S(1)} %multiply_convert_fusion.4, bf16[1024,4096]{1,0:T(8,128)(2,1)} %all-gather.5.cloned.1.call-done), kind=kOutput, calls=%fused_computation.70 | convolution fusion | flops 4294967296 | bytes 17825792 | tf_op jit(solution)/shard_map/dot_general | solution.py:109
  233.4 112.1 %all-reduce.2.cloned.1.call-done = bf16[512,4096]{1,0:T(8,128)(2,1)} async-done(((bf16[512,4096]{1,0:T(8,128)(2,1)}), bf16[512,4096]{1,0:T(8,128)(2,1)}) %all-reduce.2.cloned.1.call-update) | async-done | bytes 4194320 | tf_op jit(solution)/shard_map/psum | solution.py:123
  345.5 5.7 %fusion.44 = f32[1,512]{1,0:T(1,128)S(1)} fusion(bf16[512,4096]{1,0:T(8,128)(2,1)} %all-reduce.2.cloned.1.call-done, f32[4096,1]{0,1:T(1,128)S(1)} %bitcast.73), kind=kOutput, calls=%fused_computation.71 | convolution fusion | flops 25165824 | bytes 4212736 | tf_op jit(solution)/shard_map/dot_general | solution.py:125
  354.7 5.6 %fusion.27 = bf16[512,1024]{1,0:T(8,128)(2,1)} fusion(bf16[4096,1024]{1,0:T(8,128)(2,1)S(1)} %copy-done.10, bf16[512,4096]{1,0:T(8,128)(2,1)S(1)} %get-tuple-element.82, f32[4096]{0:T(1024)S(1)} %copy-done.11, f32[512]{0:T(512)S(1)} %add_rsqrt_fusion), kind=kOutput, calls=%fused_computation.37 | convolution fusion | flops 4303880192 | bytes 13649920 | tf_op jit(solution)/shard_map/dot_general | solution.py:134
  (91 shorter events, 48.5 us)
Async XLA Ops:
  7.2 154.4 %copy-start = (bf16[512,1,256]{2,0,1:T(8,128)(2,1)S(1)}, bf16[512,1,256]{2,0,1:T(8,128)(2,1)}, u32[]{:S(2)}) copy-start(bf16[512,1,256]{2,0,1:T(8,128)(2,1)} %param.17) | copy-start | bytes 786436
  7.2 201.4 %all-gather.3.cloned.1.call-start = ((), (), s32[]{:S(2)}) async-start(), calls=%async_computation | async-start | bytes 8650752 | tf_op jit(solution)/shard_map/all_gather | solution.py:107
  7.9 213.5 %all-gather.5.cloned.1.call-start = ((), (), s32[]{:S(2)}) async-start(), calls=%async_computation.1 | async-start | bytes 8650752 | tf_op jit(solution)/shard_map/all_gather | solution.py:111
  16.9 7.5 %copy-start.4 = (bf16[2,256,16,64]{1,3,2,0:T(8,128)(2,1)}, bf16[2,256,16,64]{1,3,2,0:T(8,128)(2,1)S(1)}, u32[]{:S(2)}) copy-start(bf16[2,256,16,64]{1,3,2,0:T(8,128)(2,1)S(1)} %copy.37) | copy-start | bytes 3145732
  24.4 3.0 copy-start.2
  32.4 17.8 %collective-permute-start.5 = (bf16[16,16384]{1,0:T(8,128)(2,1)S(1)}, bf16[16,16384]{1,0:T(8,128)(2,1)S(1)}, u32[]{:S(2)}, u32[]{:S(2)}) collective-permute-start(bf16[16,16384]{1,0:T(8,128)(2,1)S(1)} %convert_element_type.85), channel_id=1, source_target_pairs={{0,8},{8,16},{16,24},{24,32},{32,40},{40,48},{48,56},{56,64},{64,7... | collective-permute-start | bytes 1572872 | tf_op jit(solution)/shard_map/ppermute | solution.py:17
  50.3 41.2 %collective-permute-start.6 = (bf16[16,16384]{1,0:T(8,128)(2,1)S(1)}, bf16[16,16384]{1,0:T(8,128)(2,1)S(1)}, u32[]{:S(2)}, u32[]{:S(2)}) collective-permute-start(bf16[16,16384]{1,0:T(8,128)(2,1)S(1)} %collective-permute-done.5), channel_id=1, source_target_pairs={{0,8},{8,16},{16,24},{24,32},{32,40},{40,48},{48,56},{56,64},{64,7... | collective-permute-start | bytes 1572872 | tf_op jit(solution)/shard_map/ppermute | solution.py:17
  55.6 28.6 %collective-permute-start = (f32[16]{0:T(128)S(1)}, f32[16]{0:T(128)S(1)}, u32[]{:S(2)}, u32[]{:S(2)}) collective-permute-start(f32[16]{0:T(128)S(1)} %get-tuple-element.69), channel_id=1, source_target_pairs={{0,8},{8,16},{16,24},{24,32},{32,40},{40,48},{48,56},{56,64},{64,7... | collective-permute-start | bytes 200 | tf_op jit(solution)/shard_map/ppermute | solution.py:16
  84.1 7.4 %collective-permute-start.1 = (f32[16]{0:T(128)S(1)}, f32[16]{0:T(128)S(1)}, u32[]{:S(2)}, u32[]{:S(2)}) collective-permute-start(f32[16]{0:T(128)S(1)} %collective-permute-done), channel_id=1, source_target_pairs={{0,8},{8,16},{16,24},{24,32},{32,40},{40,48},{48,56},{56,64},{64,7... | collective-permute-start | bytes 200 | tf_op jit(solution)/shard_map/ppermute | solution.py:16
  91.7 20.9 %collective-permute-start.7 = (bf16[16,16384]{1,0:T(8,128)(2,1)S(1)}, bf16[16,16384]{1,0:T(8,128)(2,1)S(1)}, u32[]{:S(2)}, u32[]{:S(2)}) collective-permute-start(bf16[16,16384]{1,0:T(8,128)(2,1)S(1)} %fusion.34), channel_id=1, source_target_pairs={{0,16},{8,24},{16,32},{24,40},{32,48},{40,56},{48,64},{56,72},{64,... | collective-permute-start | bytes 1572872 | tf_op jit(solution)/shard_map/ppermute | solution.py:17
  98.3 247.2 %all-reduce.2.cloned.1.call-start = ((), (), s32[]{:S(2)}) async-start(), calls=%async_computation.2 | async-start | bytes 8388608 | tf_op jit(solution)/shard_map/psum | solution.py:123
  112.6 66.7 %copy-start.5 = (bf16[2,256,16,64]{1,3,2,0:T(8,128)(2,1)S(1)}, bf16[2,256,16,64]{1,3,2,0:T(8,128)(2,1)}, u32[]{:S(2)}) copy-start(bf16[2,256,16,64]{1,3,2,0:T(8,128)(2,1)} %copy-done.4) | copy-start | bytes 3145732
  113.0 29.4 %collective-permute-start.8 = (bf16[16,16384]{1,0:T(8,128)(2,1)S(1)}, bf16[16,16384]{1,0:T(8,128)(2,1)S(1)}, u32[]{:S(2)}, u32[]{:S(2)}) collective-permute-start(bf16[16,16384]{1,0:T(8,128)(2,1)S(1)} %fusion.38), channel_id=1, source_target_pairs={{0,32},{8,40},{16,48},{24,56},{32,64},{40,72},{48,80},{56,88},{64,... | collective-permute-start | bytes 1572872 | tf_op jit(solution)/shard_map/ppermute | solution.py:17
  117.7 24.6 %collective-permute-start.2 = (f32[16]{0:T(128)S(1)}, f32[16]{0:T(128)S(1)}, u32[]{:S(2)}, u32[]{:S(2)}) collective-permute-start(f32[16]{0:T(128)S(1)} %get-tuple-element.88), channel_id=1, source_target_pairs={{0,16},{8,24},{16,32},{24,40},{32,48},{40,56},{48,64},{56,72},{64,... | collective-permute-start | bytes 200 | tf_op jit(solution)/shard_map/ppermute | solution.py:16
  142.8 29.1 %collective-permute-start.9 = (bf16[16,16384]{1,0:T(8,128)(2,1)S(1)}, bf16[16,16384]{1,0:T(8,128)(2,1)S(1)}, u32[]{:S(2)}, u32[]{:S(2)}) collective-permute-start(bf16[16,16384]{1,0:T(8,128)(2,1)S(1)} %fusion.35), channel_id=1, source_target_pairs={{0,64},{8,72},{16,80},{24,88},{32,96},{40,104},{48,112},{56,120},{... | collective-permute-start | bytes 1572872 | tf_op jit(solution)/shard_map/ppermute | solution.py:17
  162.7 3.6 collective-permute-start.3
  174.0 20.2 %collective-permute-start.10 = (bf16[16,16384]{1,0:T(8,128)(2,1)}, bf16[16,16384]{1,0:T(8,128)(2,1)}, u32[]{:S(2)}, u32[]{:S(2)}) collective-permute-start(bf16[16,16384]{1,0:T(8,128)(2,1)} %fusion.37), channel_id=1, source_target_pairs={{0,128},{8,136},{16,144},{24,152},{32,160},{40,168},{48,176},{56,1... | collective-permute-start | bytes 1572872 | tf_op jit(solution)/shard_map/ppermute | solution.py:17
  192.2 6.9 %copy-start.12 = (f32[16]{0:T(128)S(1)}, f32[16]{0:T(128)}, u32[]{:S(2)}) copy-start(f32[16]{0:T(128)} %param.19) | copy-start | bytes 196
  192.2 2.0 collective-permute-start.4
  208.5 20.0 %copy-start.7 = (bf16[64,4096]{1,0:T(8,128)(2,1)S(1)}, bf16[64,4096]{1,0:T(8,128)(2,1)}, u32[]{:S(2)}) copy-start(bf16[64,4096]{1,0:T(8,128)(2,1)} %param.22) | copy-start | bytes 1572868
  345.5 5.7 %copy-start.3 = (bf16[512,4096]{1,0:T(8,128)(2,1)S(1)}, bf16[512,4096]{1,0:T(8,128)(2,1)}, u32[]{:S(2)}) copy-start(bf16[512,4096]{1,0:T(8,128)(2,1)} %all-reduce.2.cloned.1.call-done) | copy-start | bytes 12582916
  351.1 3.6 copy-start.10
  351.1 3.6 copy-start.11
  354.7 5.6 %copy-start.1 = (bf16[512,1,256]{2,0,1:T(8,128)(2,1)S(1)}, bf16[512,1,256]{2,0,1:T(8,128)(2,1)}, u32[]{:S(2)}) copy-start(bf16[512,1,256]{2,0,1:T(8,128)(2,1)} %param.17) | copy-start | bytes 786436
  (4 other events, 6.3 us)
Sparse Core Ops, SparseCore 0:
  10.6 86.6 all-gather.2
  99.8 121.6 all-gather.4
  231.5 113.9 all-reduce.1

commit v8 on v7

--- a/solution.py
+++ b/solution.py
@@ -81,12 +81,14 @@
     )
     block_decay = cum_heads[:, :, -1]
 
-    def advance(carried_state, pair):
-        decay_here, state_here = pair
-        return (jnp.exp(decay_here)[:, None, None] * carried_state + state_here, carried_state)
-
-    zero_state = jnp.zeros((head_count, state_width, head_width), jnp.float32)
-    device_state, local_starts = lax.scan(advance, zero_state, (block_decay, block_state))
+    device_state = jnp.zeros((head_count, state_width, head_width), jnp.float32)
+    starts_list = []
+    for block in range(block_count):
+        starts_list.append(device_state)
+        device_state = (
+            jnp.exp(block_decay[block])[:, None, None] * device_state + block_state[block]
+        )
+    local_starts = jnp.stack(starts_list)
     device_decay = jnp.sum(block_decay, axis=0)
     total_decay, incoming = shift_scan(
         device_decay, device_state.reshape(head_count, state_width * head_width), "seq"
@@ -106,21 +108,21 @@
     ssd_out = (grouped.reshape(seq_rows, channels) * norm_gain[None, :]).astype(jnp.bfloat16)
     w_in_all = lax.all_gather(w_in, "seq", axis=0, tiled=True)
     ssd_out, w_in_all = lax.optimization_barrier((ssd_out, w_in_all))
+    own_rows = residual.shape[0]
+    mine = lax.axis_index("head")
+    residual_rows = lax.dynamic_update_slice_in_dim(
+        jnp.zeros((seq_rows, residual.shape[1]), jnp.float32),
+        residual.astype(jnp.float32),
+        mine * own_rows,
+        axis=0,
+    )
     partial_sum = jnp.dot(
         ssd_out,
         lax.all_gather(w_out, "seq", axis=1, tiled=True),
         preferred_element_type=jnp.float32,
     )
-    own_rows = residual.shape[0]
-    mine = lax.axis_index("head")
-    with_residual = lax.dynamic_update_slice_in_dim(
-        partial_sum,
-        lax.dynamic_slice_in_dim(partial_sum, mine * own_rows, own_rows)
-        + residual.astype(jnp.float32),
-        mine * own_rows,
-        axis=0,
-    )
-    hidden = lax.psum(with_residual.astype(jnp.bfloat16), "head").astype(jnp.float32)
+    with_residual = (partial_sum + residual_rows).astype(jnp.bfloat16)
+    hidden = lax.psum(with_residual, "head").astype(jnp.float32)
     unit = refusal / jnp.sqrt(jnp.sum(refusal * refusal) + 1e-06)
     coef = jnp.dot(hidden, unit, precision=lax.Precision.HIGHEST)
     stream_all = (hidden - coef[:, None] * unit[None, :]).astype(jnp.bfloat16)

time: 368 us -> 366 us (level)
  matrix products: 36.1 us -> 29.5 us
  waiting for transfers between devices: 193 us -> 199 us
    ppermute x6, starting transfers between devices: 46.9 us -> 67.8 us  [shifted(): lax.ppermute(s.astype(jnp.bfloat16), axis, pairs).astype(jnp.float32)]
    ppermute x5, starting transfers between devices: 30.3 us -> 13 us  [shifted(): lax.ppermute(a, axis, pairs)]
    ppermute x5, waiting for transfers between devices: 35.8 us -> 42.3 us  [shifted(): lax.ppermute(a, axis, pairs)]
    psum x1, waiting for transfers between devices: 112 us -> 106 us  [body(): hidden = lax.psum(with_residual, 'head').astype(jnp.float32)]
    ppermute x6, waiting for transfers between devices: 31.3 us -> 36.8 us  [shifted(): lax.ppermute(s.astype(jnp.bfloat16), axis, pairs).astype(jnp.float32)]
  transfers between devices with their start and end apart: 14 -> 14, of which waited for: 10 -> 10; matrix products, arithmetic and copies ran while one was open for 14% -> 12% of each run, Pallas kernels for 0% -> 0%
where the time goes in v8:
time: 366 us; the launch traced here: 365 us
  waiting for transfers between devices  199 us (54%)
  starting transfers between devices  80.9 us (22%)
  matrix products  29.5 us (8%)
  local copies, waits for them, and re-layouts  24.7 us (7%)
  other arithmetic  16.3 us (4%)
  between operations  14.8 us (4%)
    psum x1, waiting for transfers between devices, body(): hidden = lax.psum(with_residual, 'head').astype(jnp.float32)  106 us
    ppermute x6, starting transfers between devices, shifted(): lax.ppermute(s.astype(jnp.bfloat16), axis, pairs).astype(jnp.float32)  67.8 us
    ppermute x5, waiting for transfers between devices, shifted(): lax.ppermute(a, axis, pairs)  42.3 us
    ppermute x6, waiting for transfers between devices, shifted(): lax.ppermute(s.astype(jnp.bfloat16), axis, pairs).astype(jnp.float32)  36.8 us
    ppermute x5, starting transfers between devices, shifted(): lax.ppermute(a, axis, pairs)  13 us
    all_gather x1, waiting for transfers between devices, body(): lax.all_gather(w_out, 'seq', axis=1, tiled=True)  12.6 us
    convert_element_type x2, local copies, waits for them, and re-layouts, body(): gate_z.reshape(block_count, SPAN, head_count, head_width)  8.72 us
  transfers between devices with their start and end apart: 14, of which 10 were waited for; matrix products, arithmetic and copies ran while one was open for 12% of the time, Pallas kernels for 0%

profile of v8, /device:TPU:1, one launch (start us, length us, event | category | flops | bytes accessed | tf_op | source)
XLA Modules:
  0.0 365.0 jit_solution(16787752407167788907)
XLA Ops:
  10.1 3.0 reshape.178
  26.5 6.3 %collective-permute-start.5 = (bf16[16,16384]{1,0:T(8,128)(2,1)S(1)}, bf16[16,16384]{1,0:T(8,128)(2,1)S(1)}, u32[]{:S(2)}, u32[]{:S(2)}) collective-permute-start(bf16[16,16384]{1,0:T(8,128)(2,1)S(1)} %add_convert_fusion), channel_id=1, source_target_pairs={{0,8},{8,16},{16,24},{24,32},{32,40},{40,48},{48,56},{56,64},{64,7... | collective-permute-start | bytes 1572872 | tf_op jit(solution)/shard_map/ppermute | solution.py:17
  32.9 15.5 %collective-permute-done.5 = bf16[16,16384]{1,0:T(8,128)(2,1)S(1)} collective-permute-done((bf16[16,16384]{1,0:T(8,128)(2,1)S(1)}, bf16[16,16384]{1,0:T(8,128)(2,1)S(1)}, u32[]{:S(2)}, u32[]{:S(2)}) %collective-permute-start.5) | collective-permute-done | bytes 524320 | tf_op jit(solution)/shard_map/ppermute | solution.py:17
  48.4 6.2 %collective-permute-start.6 = (bf16[16,16384]{1,0:T(8,128)(2,1)S(1)}, bf16[16,16384]{1,0:T(8,128)(2,1)S(1)}, u32[]{:S(2)}, u32[]{:S(2)}) collective-permute-start(bf16[16,16384]{1,0:T(8,128)(2,1)S(1)} %collective-permute-done.5), channel_id=1, source_target_pairs={{0,8},{8,16},{16,24},{24,32},{32,40},{40,48},{48,56},{56,64},{64,7... | collective-permute-start | bytes 1572872 | tf_op jit(solution)/shard_map/ppermute | solution.py:17
  54.6 2.5 collective-permute-start
  57.1 31.9 %collective-permute-done = f32[16]{0:T(128)S(1)} collective-permute-done((f32[16]{0:T(128)S(1)}, f32[16]{0:T(128)S(1)}, u32[]{:S(2)}, u32[]{:S(2)}) %collective-permute-start) | collective-permute-done | bytes 96 | tf_op jit(solution)/shard_map/ppermute | solution.py:16
  89.0 5.4 %collective-permute-start.1 = (f32[16]{0:T(128)S(1)}, f32[16]{0:T(128)S(1)}, u32[]{:S(2)}, u32[]{:S(2)}) collective-permute-start(f32[16]{0:T(128)S(1)} %collective-permute-done), channel_id=1, source_target_pairs={{0,8},{8,16},{16,24},{24,32},{32,40},{40,48},{48,56},{56,64},{64,7... | collective-permute-start | bytes 200 | tf_op jit(solution)/shard_map/ppermute | solution.py:16
  95.4 14.9 %collective-permute-start.7 = (bf16[16,16384]{1,0:T(8,128)(2,1)S(1)}, bf16[16,16384]{1,0:T(8,128)(2,1)S(1)}, u32[]{:S(2)}, u32[]{:S(2)}) collective-permute-start(bf16[16,16384]{1,0:T(8,128)(2,1)S(1)} %fusion.29), channel_id=1, source_target_pairs={{0,16},{8,24},{16,32},{24,40},{32,48},{40,56},{48,64},{56,72},{64,... | collective-permute-start | bytes 1572872 | tf_op jit(solution)/shard_map/ppermute | solution.py:17
  110.4 12.5 %collective-permute-done.7 = bf16[16,16384]{1,0:T(8,128)(2,1)S(1)} collective-permute-done((bf16[16,16384]{1,0:T(8,128)(2,1)S(1)}, bf16[16,16384]{1,0:T(8,128)(2,1)S(1)}, u32[]{:S(2)}, u32[]{:S(2)}) %collective-permute-start.7) | collective-permute-done | bytes 524320 | tf_op jit(solution)/shard_map/ppermute | solution.py:17
  123.2 8.5 %collective-permute-start.8 = (bf16[16,16384]{1,0:T(8,128)(2,1)S(1)}, bf16[16,16384]{1,0:T(8,128)(2,1)S(1)}, u32[]{:S(2)}, u32[]{:S(2)}) collective-permute-start(bf16[16,16384]{1,0:T(8,128)(2,1)S(1)} %fusion.37), channel_id=1, source_target_pairs={{0,32},{8,40},{16,48},{24,56},{32,64},{40,72},{48,80},{56,88},{64,... | collective-permute-start | bytes 1572872 | tf_op jit(solution)/shard_map/ppermute | solution.py:17
  134.1 8.4 %collective-permute-done.2 = f32[16]{0:T(128)S(1)} collective-permute-done((f32[16]{0:T(128)S(1)}, f32[16]{0:T(128)S(1)}, u32[]{:S(2)}, u32[]{:S(2)}) %collective-permute-start.2) | collective-permute-done | bytes 96 | tf_op jit(solution)/shard_map/ppermute | solution.py:16
  142.9 26.6 %collective-permute-start.9 = (bf16[16,16384]{1,0:T(8,128)(2,1)S(1)}, bf16[16,16384]{1,0:T(8,128)(2,1)S(1)}, u32[]{:S(2)}, u32[]{:S(2)}) collective-permute-start(bf16[16,16384]{1,0:T(8,128)(2,1)S(1)} %fusion.30), channel_id=1, source_target_pairs={{0,64},{8,72},{16,80},{24,88},{32,96},{40,104},{48,112},{56,120},{... | collective-permute-start | bytes 1572872 | tf_op jit(solution)/shard_map/ppermute | solution.py:17
  171.6 8.8 %collective-permute-done.9 = bf16[16,16384]{1,0:T(8,128)(2,1)S(1)} collective-permute-done((bf16[16,16384]{1,0:T(8,128)(2,1)S(1)}, bf16[16,16384]{1,0:T(8,128)(2,1)S(1)}, u32[]{:S(2)}, u32[]{:S(2)}) %collective-permute-start.9) | collective-permute-done | bytes 524320 | tf_op jit(solution)/shard_map/ppermute | solution.py:17
  181.7 5.3 %collective-permute-start.10 = (bf16[16,16384]{1,0:T(8,128)(2,1)}, bf16[16,16384]{1,0:T(8,128)(2,1)}, u32[]{:S(2)}, u32[]{:S(2)}) collective-permute-start(bf16[16,16384]{1,0:T(8,128)(2,1)} %fusion.36), channel_id=1, source_target_pairs={{0,128},{8,136},{16,144},{24,152},{32,160},{40,168},{48,176},{56,1... | collective-permute-start | bytes 1572872 | tf_op jit(solution)/shard_map/ppermute | solution.py:17
  187.1 4.1 %reshape.179 = f32[2,256,16,64]{3,2,1,0:T(8,128)} reshape(bf16[512,1024]{1,0:T(8,128)(2,1)} %param.13) | data formatting | bytes 3145728 | tf_op jit(solution)/shard_map/convert_element_type | solution.py:104
  191.2 4.6 %copy.44 = f32[2,256,16,64]{1,3,2,0:T(8,128)} copy(f32[2,256,16,64]{3,2,1,0:T(8,128)} %reshape.179) | data formatting | bytes 4194304 | tf_op jit(solution)/shard_map/convert_element_type | solution.py:104
  202.2 5.3 %fusion.19 = f32[2,16,64,256]{3,2,1,0:T(8,128)S(1)} fusion(bf16[2,256,256]{2,1,0:T(8,128)(2,1)S(1)} %bitcast.60, f32[1,16,256,64]{2,3,1,0:T(8,128)} %get-tuple-element.19, f32[16,256,64]{1,2,0:T(8,128)S(1)} %copy.40, f32[2,16]{1,0:T(2,128)S(1)} %subtract_exponential_fusion), kind=kOutput, calls=%fused_computation.26 | convolution fusion | flops 1611661312 | bytes 4456576 | tf_op jit(solution)/shard_map/klhn,khnp->klhp/dot_general | solution.py:100
  207.5 3.0 multiply_reduce_fusion
  212.8 12.6 %all-gather.5.cloned.1.call-done = bf16[1024,4096]{1,0:T(8,128)(2,1)} async-done(((bf16[1024,128]{1,0:T(8,128)(2,1)}), bf16[1024,4096]{1,0:T(8,128)(2,1)}) %all-gather.5.cloned.1.call-update) | async-done | bytes 8388624 | tf_op jit(solution)/shard_map/all_gather | solution.py:121
  225.4 7.1 %fusion.43 = f32[512,4096]{1,0:T(8,128)S(1)} fusion(bf16[512,1024]{0,1:T(8,128)(2,1)S(1)} %multiply_convert_fusion.4, bf16[1024,4096]{1,0:T(8,128)(2,1)} %all-gather.5.cloned.1.call-done), kind=kOutput, calls=%fused_computation.75 | convolution fusion | flops 4294967296 | bytes 17825792 | tf_op jit(solution)/shard_map/dot_general | solution.py:119
  232.7 2.6 convert_element_type.97
  237.3 106.3 %all-reduce.3.cloned.1.call-done = bf16[512,4096]{1,0:T(8,128)(2,1)} async-done(((bf16[512,4096]{1,0:T(8,128)(2,1)}), bf16[512,4096]{1,0:T(8,128)(2,1)}) %all-reduce.3.cloned.1.call-update) | async-done | bytes 4194320 | tf_op jit(solution)/shard_map/psum | solution.py:125
  343.6 5.7 %fusion.44 = f32[1,512]{1,0:T(1,128)S(1)} fusion(bf16[512,4096]{1,0:T(8,128)(2,1)} %all-reduce.3.cloned.1.call-done, f32[4096,1]{0,1:T(1,128)S(1)} %bitcast.65), kind=kOutput, calls=%fused_computation.76 | convolution fusion | flops 25165824 | bytes 4212736 | tf_op jit(solution)/shard_map/dot_general | solution.py:127
  352.9 5.6 %fusion.24 = bf16[512,1024]{1,0:T(8,128)(2,1)} fusion(bf16[4096,1024]{1,0:T(8,128)(2,1)S(1)} %copy-done.13, bf16[512,4096]{1,0:T(8,128)(2,1)S(1)} %get-tuple-element.11, f32[4096]{0:T(1024)S(1)} %copy-done.14, f32[512]{0:T(512)S(1)} %add_rsqrt_fusion), kind=kOutput, calls=%fused_computation.31 | convolution fusion | flops 4303880192 | bytes 13649920 | tf_op jit(solution)/shard_map/dot_general | solution.py:136
  (92 shorter events, 37.3 us)
Async XLA Ops:
  7.2 188.6 %copy-start = (bf16[512,1,256]{2,0,1:T(8,128)(2,1)S(1)}, bf16[512,1,256]{2,0,1:T(8,128)(2,1)}, u32[]{:S(2)}) copy-start(bf16[512,1,256]{2,0,1:T(8,128)(2,1)} %param.15) | copy-start | bytes 786436
  7.2 205.6 %all-gather.3.cloned.1.call-start = ((), (), s32[]{:S(2)}) async-start(), calls=%async_computation | async-start | bytes 8650752 | tf_op jit(solution)/shard_map/all_gather | solution.py:109
  7.9 217.4 %all-gather.5.cloned.1.call-start = ((), (), s32[]{:S(2)}) async-start(), calls=%async_computation.1 | async-start | bytes 8650752 | tf_op jit(solution)/shard_map/all_gather | solution.py:121
  14.7 5.6 %copy-start.5 = (bf16[2,256,16,64]{1,3,2,0:T(8,128)(2,1)}, bf16[2,256,16,64]{1,3,2,0:T(8,128)(2,1)S(1)}, u32[]{:S(2)}) copy-start(bf16[2,256,16,64]{1,3,2,0:T(8,128)(2,1)S(1)} %copy.36) | copy-start | bytes 3145732
  26.5 21.8 %collective-permute-start.5 = (bf16[16,16384]{1,0:T(8,128)(2,1)S(1)}, bf16[16,16384]{1,0:T(8,128)(2,1)S(1)}, u32[]{:S(2)}, u32[]{:S(2)}) collective-permute-start(bf16[16,16384]{1,0:T(8,128)(2,1)S(1)} %add_convert_fusion), channel_id=1, source_target_pairs={{0,8},{8,16},{16,24},{24,32},{32,40},{40,48},{48,56},{56,64},{64,7... | collective-permute-start | bytes 1572872 | tf_op jit(solution)/shard_map/ppermute | solution.py:17
  48.4 46.8 %collective-permute-start.6 = (bf16[16,16384]{1,0:T(8,128)(2,1)S(1)}, bf16[16,16384]{1,0:T(8,128)(2,1)S(1)}, u32[]{:S(2)}, u32[]{:S(2)}) collective-permute-start(bf16[16,16384]{1,0:T(8,128)(2,1)S(1)} %collective-permute-done.5), channel_id=1, source_target_pairs={{0,8},{8,16},{16,24},{24,32},{32,40},{40,48},{48,56},{56,64},{64,7... | collective-permute-start | bytes 1572872 | tf_op jit(solution)/shard_map/ppermute | solution.py:17
  54.6 34.5 %collective-permute-start = (f32[16]{0:T(128)S(1)}, f32[16]{0:T(128)S(1)}, u32[]{:S(2)}, u32[]{:S(2)}) collective-permute-start(f32[16]{0:T(128)S(1)} %get-tuple-element.6), channel_id=1, source_target_pairs={{0,8},{8,16},{16,24},{24,32},{32,40},{40,48},{48,56},{56,64},{64,7... | collective-permute-start | bytes 200 | tf_op jit(solution)/shard_map/ppermute | solution.py:16
  89.0 6.1 %collective-permute-start.1 = (f32[16]{0:T(128)S(1)}, f32[16]{0:T(128)S(1)}, u32[]{:S(2)}, u32[]{:S(2)}) collective-permute-start(f32[16]{0:T(128)S(1)} %collective-permute-done), channel_id=1, source_target_pairs={{0,8},{8,16},{16,24},{24,32},{32,40},{40,48},{48,56},{56,64},{64,7... | collective-permute-start | bytes 200 | tf_op jit(solution)/shard_map/ppermute | solution.py:16
  95.4 27.5 %collective-permute-start.7 = (bf16[16,16384]{1,0:T(8,128)(2,1)S(1)}, bf16[16,16384]{1,0:T(8,128)(2,1)S(1)}, u32[]{:S(2)}, u32[]{:S(2)}) collective-permute-start(bf16[16,16384]{1,0:T(8,128)(2,1)S(1)} %fusion.29), channel_id=1, source_target_pairs={{0,16},{8,24},{16,32},{24,40},{32,48},{40,56},{48,64},{56,72},{64,... | collective-permute-start | bytes 1572872 | tf_op jit(solution)/shard_map/ppermute | solution.py:17
  110.3 233.3 %all-reduce.3.cloned.1.call-start = ((), (), s32[]{:S(2)}) async-start(), calls=%async_computation.2 | async-start | bytes 8388608 | tf_op jit(solution)/shard_map/psum | solution.py:125
  123.2 19.3 %collective-permute-start.8 = (bf16[16,16384]{1,0:T(8,128)(2,1)S(1)}, bf16[16,16384]{1,0:T(8,128)(2,1)S(1)}, u32[]{:S(2)}, u32[]{:S(2)}) collective-permute-start(bf16[16,16384]{1,0:T(8,128)(2,1)S(1)} %fusion.37), channel_id=1, source_target_pairs={{0,32},{8,40},{16,48},{24,56},{32,64},{40,72},{48,80},{56,88},{64,... | collective-permute-start | bytes 1572872 | tf_op jit(solution)/shard_map/ppermute | solution.py:17
  131.8 10.7 %collective-permute-start.2 = (f32[16]{0:T(128)S(1)}, f32[16]{0:T(128)S(1)}, u32[]{:S(2)}, u32[]{:S(2)}) collective-permute-start(f32[16]{0:T(128)S(1)} %get-tuple-element.17), channel_id=1, source_target_pairs={{0,16},{8,24},{16,32},{24,40},{32,48},{40,56},{48,64},{56,72},{64,... | collective-permute-start | bytes 200 | tf_op jit(solution)/shard_map/ppermute | solution.py:16
  142.9 37.5 %collective-permute-start.9 = (bf16[16,16384]{1,0:T(8,128)(2,1)S(1)}, bf16[16,16384]{1,0:T(8,128)(2,1)S(1)}, u32[]{:S(2)}, u32[]{:S(2)}) collective-permute-start(bf16[16,16384]{1,0:T(8,128)(2,1)S(1)} %fusion.30), channel_id=1, source_target_pairs={{0,64},{8,72},{16,80},{24,88},{32,96},{40,104},{48,112},{56,120},{... | collective-permute-start | bytes 1572872 | tf_op jit(solution)/shard_map/ppermute | solution.py:17
  169.6 2.0 collective-permute-start.3
  180.4 10.8 %copy-start.4 = (bf16[16,16384]{1,0:T(8,128)(2,1)}, bf16[16,16384]{1,0:T(8,128)(2,1)S(1)}, u32[]{:S(2)}) copy-start(bf16[16,16384]{1,0:T(8,128)(2,1)S(1)} %collective-permute-done.9) | copy-start | bytes 1572868
  181.7 17.1 %collective-permute-start.10 = (bf16[16,16384]{1,0:T(8,128)(2,1)}, bf16[16,16384]{1,0:T(8,128)(2,1)}, u32[]{:S(2)}, u32[]{:S(2)}) collective-permute-start(bf16[16,16384]{1,0:T(8,128)(2,1)} %fusion.36), channel_id=1, source_target_pairs={{0,128},{8,136},{16,144},{24,152},{32,160},{40,168},{48,176},{56,1... | collective-permute-start | bytes 1572872 | tf_op jit(solution)/shard_map/ppermute | solution.py:17
  196.9 2.0 collective-permute-start.4
  201.5 6.0 %copy-start.11 = (f32[2,256,16]{1,2,0:T(8,128)S(1)}, f32[2,256,16]{1,2,0:T(8,128)}, u32[]{:S(2)}) copy-start(f32[2,256,16]{1,2,0:T(8,128)} %get-tuple-element.21) | copy-start | bytes 98308
  201.5 6.0 %copy-start.15 = (f32[16]{0:T(128)S(1)}, f32[16]{0:T(128)}, u32[]{:S(2)}) copy-start(f32[16]{0:T(128)} %param.17) | copy-start | bytes 196
  202.1 5.4 %copy-start.3 = (f32[2,256,16,64]{1,3,2,0:T(8,128)S(1)}, f32[2,256,16,64]{1,3,2,0:T(8,128)}, u32[]{:S(2)}) copy-start(f32[2,256,16,64]{1,3,2,0:T(8,128)} %copy.44) | copy-start | bytes 6291460
  202.1 5.4 %copy-start.6 = (bf16[2,256,16,64]{1,3,2,0:T(8,128)(2,1)S(1)}, bf16[2,256,16,64]{1,3,2,0:T(8,128)(2,1)}, u32[]{:S(2)}) copy-start(bf16[2,256,16,64]{1,3,2,0:T(8,128)(2,1)} %copy-done.5) | copy-start | bytes 3145732
  212.7 19.8 %copy-start.9 = (bf16[64,4096]{1,0:T(8,128)(2,1)S(1)}, bf16[64,4096]{1,0:T(8,128)(2,1)}, u32[]{:S(2)}) copy-start(bf16[64,4096]{1,0:T(8,128)(2,1)} %param.20) | copy-start | bytes 1572868
  343.6 5.7 %copy-start.2 = (bf16[512,4096]{1,0:T(8,128)(2,1)S(1)}, bf16[512,4096]{1,0:T(8,128)(2,1)}, u32[]{:S(2)}) copy-start(bf16[512,4096]{1,0:T(8,128)(2,1)} %all-reduce.3.cloned.1.call-done) | copy-start | bytes 12582916
  352.9 5.6 %copy-start.1 = (bf16[512,1,256]{2,0,1:T(8,128)(2,1)S(1)}, bf16[512,1,256]{2,0,1:T(8,128)(2,1)}, u32[]{:S(2)}) copy-start(bf16[512,1,256]{2,0,1:T(8,128)(2,1)} %param.15) | copy-start | bytes 786436
  (6 other events, 19.7 us)
Sparse Core Ops, SparseCore 0:
  10.6 103.8 all-gather.2
  116.9 108.4 all-gather.4
  235.4 108.1 all-reduce.2

commit v9 on v8

--- a/solution.py
+++ b/solution.py
@@ -12,9 +12,16 @@
     def shifted(parts, distance):
         pairs = [(i, i + distance) for i in range(devices - distance)]
         a, s = parts
+        high = a.astype(jnp.bfloat16)
+        low = (a - high.astype(jnp.float32)).astype(jnp.bfloat16)
+        tail = jnp.zeros((s.shape[0], 128), jnp.bfloat16)
+        tail = tail.at[:, 0].set(high).at[:, 1].set(low)
+        packed = jnp.concatenate([s.astype(jnp.bfloat16), tail], axis=1)
+        got = lax.ppermute(packed, axis, pairs)
+        width = s.shape[1]
         return (
-            lax.ppermute(a, axis, pairs),
-            lax.ppermute(s.astype(jnp.bfloat16), axis, pairs).astype(jnp.float32),
+            got[:, width].astype(jnp.float32) + got[:, width + 1].astype(jnp.float32),
+            got[:, :width].astype(jnp.float32),
         )
 
     acc = shifted((decay, state), 1)

time: 366 us -> 393 us (1.074)
  waiting for transfers between devices: 199 us -> 242 us
  starting transfers between devices: 80.9 us -> 53.6 us
  other arithmetic: 16.3 us -> 26.1 us
    all_gather x1, waiting for transfers between devices: 12.6 us -> 41 us  [body(): lax.all_gather(w_out, 'seq', axis=1, tiled=True)]
    ppermute x11 -> x6, starting transfers between devices: 80.8 us -> 53.5 us  [shifted(): got = lax.ppermute(packed, axis, pairs)]
    ppermute x11 -> x6, waiting for transfers between devices: 79.1 us -> 94.6 us  [shifted(): got = lax.ppermute(packed, axis, pairs)]
    another operation x3 -> x12, other arithmetic: 1.25 us -> 10.4 us
  transfers between devices with their start and end apart: 14 -> 9, of which waited for: 10 -> 7; matrix products, arithmetic and copies ran while one was open for 12% -> 9% of each run, Pallas kernels for 0% -> 0%
where the time goes in v9:
time: 393 us; the launch traced here: 392 us
  waiting for transfers between devices  242 us (62%)
  starting transfers between devices  53.6 us (14%)
  matrix products  29.5 us (8%)
  other arithmetic  26.1 us (7%)
  local copies, waits for them, and re-layouts  26 us (7%)
  between operations  14.9 us (4%)
    psum x1, waiting for transfers between devices, body(): hidden = lax.psum(with_residual, 'head').astype(jnp.float32)  106 us
    ppermute x6, waiting for transfers between devices, shifted(): got = lax.ppermute(packed, axis, pairs)  94.6 us
    ppermute x6, starting transfers between devices, shifted(): got = lax.ppermute(packed, axis, pairs)  53.5 us
    all_gather x1, waiting for transfers between devices, body(): lax.all_gather(w_out, 'seq', axis=1, tiled=True)  41 us
    another operation x12, other arithmetic  10.4 us
    convert_element_type x2, local copies, waits for them, and re-layouts, body(): gate_z.reshape(block_count, SPAN, head_count, head_width)  8.71 us
  transfers between devices with their start and end apart: 9, of which 7 were waited for; matrix products, arithmetic and copies ran while one was open for 9% of the time, Pallas kernels for 0%

profile of v9, /device:TPU:1, one launch (start us, length us, event | category | flops | bytes accessed | tf_op | source)
XLA Modules:
  0.0 392.1 jit_solution(3471142113388535046)
XLA Ops:
  11.9 2.9 reshape.464
  22.3 1.8 copy.42
  28.7 6.3 %collective-permute-start = (bf16[16,16512]{1,0:T(8,128)(2,1)S(1)}, bf16[16,16512]{1,0:T(8,128)(2,1)S(1)}, u32[]{:S(2)}, u32[]{:S(2)}) collective-permute-start(bf16[16,16512]{1,0:T(8,128)(2,1)S(1)} %pad_maximum_fusion), channel_id=1, source_target_pairs={{0,8},{8,16},{16,24},{24,32},{32,40},{40,48},{48,56},{56,64},{64,7... | collective-permute-start | bytes 1585160 | tf_op jit(solution)/shard_map/ppermute | solution.py:20
  35.1 7.1 %collective-permute-done = bf16[16,16512]{1,0:T(8,128)(2,1)S(1)} collective-permute-done((bf16[16,16512]{1,0:T(8,128)(2,1)S(1)}, bf16[16,16512]{1,0:T(8,128)(2,1)S(1)}, u32[]{:S(2)}, u32[]{:S(2)}) %collective-permute-start) | collective-permute-done | bytes 528416 | tf_op jit(solution)/shard_map/ppermute | solution.py:20
  43.8 5.3 %collective-permute-start.1 = (bf16[16,16512]{1,0:T(8,128)(2,1)S(1)}, bf16[16,16512]{1,0:T(8,128)(2,1)S(1)}, u32[]{:S(2)}, u32[]{:S(2)}) collective-permute-start(bf16[16,16512]{1,0:T(8,128)(2,1)S(1)} %pad_maximum_fusion.1), channel_id=1, source_target_pairs={{0,8},{8,16},{16,24},{24,32},{32,40},{40,48},{48,56},{56,64},{64,7... | collective-permute-start | bytes 1585160 | tf_op jit(solution)/shard_map/ppermute | solution.py:20
  49.1 13.7 %collective-permute-done.1 = bf16[16,16512]{1,0:T(8,128)(2,1)S(1)} collective-permute-done((bf16[16,16512]{1,0:T(8,128)(2,1)S(1)}, bf16[16,16512]{1,0:T(8,128)(2,1)S(1)}, u32[]{:S(2)}, u32[]{:S(2)}) %collective-permute-start.1) | collective-permute-done | bytes 528416 | tf_op jit(solution)/shard_map/ppermute | solution.py:20
  64.7 14.2 %collective-permute-start.2 = (bf16[16,16512]{1,0:T(8,128)(2,1)S(1)}, bf16[16,16512]{1,0:T(8,128)(2,1)S(1)}, u32[]{:S(2)}, u32[]{:S(2)}) collective-permute-start(bf16[16,16512]{1,0:T(8,128)(2,1)S(1)} %pad_maximum_fusion.2), channel_id=1, source_target_pairs={{0,16},{8,24},{16,32},{24,40},{32,48},{40,56},{48,64},{56,72},{64,... | collective-permute-start | bytes 1585160 | tf_op jit(solution)/shard_map/ppermute | solution.py:20
  78.9 43.2 %collective-permute-done.2 = bf16[16,16512]{1,0:T(8,128)(2,1)S(1)} collective-permute-done((bf16[16,16512]{1,0:T(8,128)(2,1)S(1)}, bf16[16,16512]{1,0:T(8,128)(2,1)S(1)}, u32[]{:S(2)}, u32[]{:S(2)}) %collective-permute-start.2) | collective-permute-done | bytes 528416 | tf_op jit(solution)/shard_map/ppermute | solution.py:20
  124.1 13.5 %collective-permute-start.3 = (bf16[16,16512]{1,0:T(8,128)(2,1)S(1)}, bf16[16,16512]{1,0:T(8,128)(2,1)S(1)}, u32[]{:S(2)}, u32[]{:S(2)}) collective-permute-start(bf16[16,16512]{1,0:T(8,128)(2,1)S(1)} %pad_maximum_fusion.3), channel_id=1, source_target_pairs={{0,32},{8,40},{16,48},{24,56},{32,64},{40,72},{48,80},{56,88},{64,... | collective-permute-start | bytes 1585160 | tf_op jit(solution)/shard_map/ppermute | solution.py:20
  137.6 19.0 %collective-permute-done.3 = bf16[16,16512]{1,0:T(8,128)(2,1)S(1)} collective-permute-done((bf16[16,16512]{1,0:T(8,128)(2,1)S(1)}, bf16[16,16512]{1,0:T(8,128)(2,1)S(1)}, u32[]{:S(2)}, u32[]{:S(2)}) %collective-permute-start.3) | collective-permute-done | bytes 528416 | tf_op jit(solution)/shard_map/ppermute | solution.py:20
  158.6 8.8 %collective-permute-start.4 = (bf16[16,16512]{1,0:T(8,128)(2,1)S(1)}, bf16[16,16512]{1,0:T(8,128)(2,1)S(1)}, u32[]{:S(2)}, u32[]{:S(2)}) collective-permute-start(bf16[16,16512]{1,0:T(8,128)(2,1)S(1)} %pad_maximum_fusion.4), channel_id=1, source_target_pairs={{0,64},{8,72},{16,80},{24,88},{32,96},{40,104},{48,112},{56,120},{... | collective-permute-start | bytes 1585160 | tf_op jit(solution)/shard_map/ppermute | solution.py:20
  167.4 11.6 %collective-permute-done.4 = bf16[16,16512]{1,0:T(8,128)(2,1)S(1)} collective-permute-done((bf16[16,16512]{1,0:T(8,128)(2,1)S(1)}, bf16[16,16512]{1,0:T(8,128)(2,1)S(1)}, u32[]{:S(2)}, u32[]{:S(2)}) %collective-permute-start.4) | collective-permute-done | bytes 528416 | tf_op jit(solution)/shard_map/ppermute | solution.py:20
  181.8 5.4 %collective-permute-start.5 = (bf16[16,16512]{1,0:T(8,128)(2,1)S(1)}, bf16[16,16512]{1,0:T(8,128)(2,1)}, u32[]{:S(2)}, u32[]{:S(2)}) collective-permute-start(bf16[16,16512]{1,0:T(8,128)(2,1)S(1)} %pad_maximum_fusion.5), channel_id=1, source_target_pairs={{0,128},{8,136},{16,144},{24,152},{32,160},{40,168},{48,176},{56,1... | collective-permute-start | bytes 1585160 | tf_op jit(solution)/shard_map/ppermute | solution.py:20
  187.2 4.1 %reshape.465 = f32[2,256,16,64]{3,2,1,0:T(8,128)} reshape(bf16[512,1024]{1,0:T(8,128)(2,1)} %param.37) | data formatting | bytes 3145728 | tf_op jit(solution)/shard_map/convert_element_type | solution.py:111
  191.3 4.6 %copy.49 = f32[2,256,16,64]{1,3,2,0:T(8,128)} copy(f32[2,256,16,64]{3,2,1,0:T(8,128)} %reshape.465) | data formatting | bytes 4194304 | tf_op jit(solution)/shard_map/convert_element_type | solution.py:111
  200.3 5.3 %fusion.19 = f32[2,16,64,256]{3,2,1,0:T(8,128)S(1)} fusion(bf16[2,256,256]{2,1,0:T(8,128)(2,1)S(1)} %bitcast.61, f32[1,16,256,64]{2,3,1,0:T(8,128)} %get-tuple-element.165, f32[16,256,64]{1,2,0:T(8,128)S(1)} %copy.45, f32[2,16]{1,0:T(2,128)S(1)} %subtract_exponential_fusion), kind=kOutput, calls=%fused_computation.26 | convolution fusion | flops 1611661312 | bytes 4456576 | tf_op jit(solution)/shard_map/klhn,khnp->klhp/dot_general | solution.py:107
  205.7 3.1 multiply_reduce_fusion
  211.4 41.0 %all-gather.5.cloned.1.call-done = bf16[1024,4096]{1,0:T(8,128)(2,1)} async-done(((bf16[1024,128]{1,0:T(8,128)(2,1)}), bf16[1024,4096]{1,0:T(8,128)(2,1)}) %all-gather.5.cloned.1.call-update) | async-done | bytes 8388624 | tf_op jit(solution)/shard_map/all_gather | solution.py:128
  252.4 7.1 %fusion.48 = f32[512,4096]{1,0:T(8,128)S(1)} fusion(bf16[512,1024]{0,1:T(8,128)(2,1)S(1)} %multiply_convert_fusion.4, bf16[1024,4096]{1,0:T(8,128)(2,1)} %all-gather.5.cloned.1.call-done), kind=kOutput, calls=%fused_computation.109 | convolution fusion | flops 4294967296 | bytes 17825792 | tf_op jit(solution)/shard_map/dot_general | solution.py:126
  259.8 2.6 convert_element_type.337
  264.4 106.3 %all-reduce.9.cloned.1.call-done = bf16[512,4096]{1,0:T(8,128)(2,1)} async-done(((bf16[512,4096]{1,0:T(8,128)(2,1)}), bf16[512,4096]{1,0:T(8,128)(2,1)}) %all-reduce.9.cloned.1.call-update) | async-done | bytes 4194320 | tf_op jit(solution)/shard_map/psum | solution.py:132
  370.7 5.7 %fusion.49 = f32[1,512]{1,0:T(1,128)S(1)} fusion(bf16[512,4096]{1,0:T(8,128)(2,1)} %all-reduce.9.cloned.1.call-done, f32[4096,1]{0,1:T(1,128)S(1)} %bitcast.66), kind=kOutput, calls=%fused_computation.110 | convolution fusion | flops 25165824 | bytes 4212736 | tf_op jit(solution)/shard_map/dot_general | solution.py:134
  376.4 1.9 fusion
  380.0 5.6 %fusion.24 = bf16[512,1024]{1,0:T(8,128)(2,1)} fusion(bf16[4096,1024]{1,0:T(8,128)(2,1)S(1)} %copy-done.13, bf16[512,4096]{1,0:T(8,128)(2,1)S(1)} %get-tuple-element.157, f32[4096]{0:T(1024)S(1)} %copy-done.14, f32[512]{0:T(512)S(1)} %add_rsqrt_fusion), kind=kOutput, calls=%fused_computation.31 | convolution fusion | flops 4303880192 | bytes 13649920 | tf_op jit(solution)/shard_map/dot_general | solution.py:143
  (110 shorter events, 37.0 us)
Async XLA Ops:
  7.2 188.8 %copy-start = (bf16[512,1,256]{2,0,1:T(8,128)(2,1)S(1)}, bf16[512,1,256]{2,0,1:T(8,128)(2,1)}, u32[]{:S(2)}) copy-start(bf16[512,1,256]{2,0,1:T(8,128)(2,1)} %param.39) | copy-start | bytes 786436
  7.2 204.2 %all-gather.3.cloned.1.call-start = ((), (), s32[]{:S(2)}) async-start(), calls=%async_computation | async-start | bytes 8650752 | tf_op jit(solution)/shard_map/all_gather | solution.py:116
  16.6 2.8 copy-start.5
  28.7 13.5 %collective-permute-start = (bf16[16,16512]{1,0:T(8,128)(2,1)S(1)}, bf16[16,16512]{1,0:T(8,128)(2,1)S(1)}, u32[]{:S(2)}, u32[]{:S(2)}) collective-permute-start(bf16[16,16512]{1,0:T(8,128)(2,1)S(1)} %pad_maximum_fusion), channel_id=1, source_target_pairs={{0,8},{8,16},{16,24},{24,32},{32,40},{40,48},{48,56},{56,64},{64,7... | collective-permute-start | bytes 1585160 | tf_op jit(solution)/shard_map/ppermute | solution.py:20
  35.0 217.4 %all-gather.5.cloned.1.call-start = ((), (), s32[]{:S(2)}) async-start(), calls=%async_computation.1 | async-start | bytes 8650752 | tf_op jit(solution)/shard_map/all_gather | solution.py:128
  43.8 19.1 %collective-permute-start.1 = (bf16[16,16512]{1,0:T(8,128)(2,1)S(1)}, bf16[16,16512]{1,0:T(8,128)(2,1)S(1)}, u32[]{:S(2)}, u32[]{:S(2)}) collective-permute-start(bf16[16,16512]{1,0:T(8,128)(2,1)S(1)} %pad_maximum_fusion.1), channel_id=1, source_target_pairs={{0,8},{8,16},{16,24},{24,32},{32,40},{40,48},{48,56},{56,64},{64,7... | collective-permute-start | bytes 1585160 | tf_op jit(solution)/shard_map/ppermute | solution.py:20
  64.7 57.4 %collective-permute-start.2 = (bf16[16,16512]{1,0:T(8,128)(2,1)S(1)}, bf16[16,16512]{1,0:T(8,128)(2,1)S(1)}, u32[]{:S(2)}, u32[]{:S(2)}) collective-permute-start(bf16[16,16512]{1,0:T(8,128)(2,1)S(1)} %pad_maximum_fusion.2), channel_id=1, source_target_pairs={{0,16},{8,24},{16,32},{24,40},{32,48},{40,56},{48,64},{56,72},{64,... | collective-permute-start | bytes 1585160 | tf_op jit(solution)/shard_map/ppermute | solution.py:20
  124.1 32.5 %collective-permute-start.3 = (bf16[16,16512]{1,0:T(8,128)(2,1)S(1)}, bf16[16,16512]{1,0:T(8,128)(2,1)S(1)}, u32[]{:S(2)}, u32[]{:S(2)}) collective-permute-start(bf16[16,16512]{1,0:T(8,128)(2,1)S(1)} %pad_maximum_fusion.3), channel_id=1, source_target_pairs={{0,32},{8,40},{16,48},{24,56},{32,64},{40,72},{48,80},{56,88},{64,... | collective-permute-start | bytes 1585160 | tf_op jit(solution)/shard_map/ppermute | solution.py:20
  137.6 233.1 %all-reduce.9.cloned.1.call-start = ((), (), s32[]{:S(2)}) async-start(), calls=%async_computation.2 | async-start | bytes 8388608 | tf_op jit(solution)/shard_map/psum | solution.py:132
  158.6 20.4 %collective-permute-start.4 = (bf16[16,16512]{1,0:T(8,128)(2,1)S(1)}, bf16[16,16512]{1,0:T(8,128)(2,1)S(1)}, u32[]{:S(2)}, u32[]{:S(2)}) collective-permute-start(bf16[16,16512]{1,0:T(8,128)(2,1)S(1)} %pad_maximum_fusion.4), channel_id=1, source_target_pairs={{0,64},{8,72},{16,80},{24,88},{32,96},{40,104},{48,112},{56,120},{... | collective-permute-start | bytes 1585160 | tf_op jit(solution)/shard_map/ppermute | solution.py:20
  179.0 2.8 copy-start.3
  181.8 15.2 %collective-permute-start.5 = (bf16[16,16512]{1,0:T(8,128)(2,1)S(1)}, bf16[16,16512]{1,0:T(8,128)(2,1)}, u32[]{:S(2)}, u32[]{:S(2)}) collective-permute-start(bf16[16,16512]{1,0:T(8,128)(2,1)S(1)} %pad_maximum_fusion.5), channel_id=1, source_target_pairs={{0,128},{8,136},{16,144},{24,152},{32,160},{40,168},{48,176},{56,1... | collective-permute-start | bytes 1585160 | tf_op jit(solution)/shard_map/ppermute | solution.py:20
  191.3 4.6 %copy-start.7 = (bf16[512,1,256]{2,0,1:T(8,128)(2,1)S(1)}, bf16[512,1,256]{2,0,1:T(8,128)(2,1)}, u32[]{:S(2)}) copy-start(bf16[512,1,256]{2,0,1:T(8,128)(2,1)} %param.38) | copy-start | bytes 786436
  200.3 5.4 %copy-start.4 = (f32[2,256,16,64]{1,3,2,0:T(8,128)S(1)}, f32[2,256,16,64]{1,3,2,0:T(8,128)}, u32[]{:S(2)}) copy-start(f32[2,256,16,64]{1,3,2,0:T(8,128)} %copy.49) | copy-start | bytes 6291460
  200.3 5.4 %copy-start.6 = (bf16[2,256,16,64]{1,3,2,0:T(8,128)(2,1)S(1)}, bf16[2,256,16,64]{1,3,2,0:T(8,128)(2,1)}, u32[]{:S(2)}) copy-start(bf16[2,256,16,64]{1,3,2,0:T(8,128)(2,1)} %copy-done.5) | copy-start | bytes 3145732
  200.3 5.4 %copy-start.8 = (f32[2,256,256]{2,1,0:T(8,128)S(1)}, f32[2,256,256]{2,1,0:T(8,128)}, u32[]{:S(2)}) copy-start(f32[2,256,256]{2,1,0:T(8,128)} %fusion.47) | copy-start | bytes 1572868
  200.3 5.4 %copy-start.11 = (f32[2,256,16]{1,2,0:T(8,128)S(1)}, f32[2,256,16]{1,2,0:T(8,128)}, u32[]{:S(2)}) copy-start(f32[2,256,16]{1,2,0:T(8,128)} %get-tuple-element.172) | copy-start | bytes 98308
  200.3 5.4 %copy-start.15 = (f32[16]{0:T(128)S(1)}, f32[16]{0:T(128)}, u32[]{:S(2)}) copy-start(f32[16]{0:T(128)} %param.41) | copy-start | bytes 196
  211.4 48.2 %copy-start.9 = (bf16[64,4096]{1,0:T(8,128)(2,1)S(1)}, bf16[64,4096]{1,0:T(8,128)(2,1)}, u32[]{:S(2)}) copy-start(bf16[64,4096]{1,0:T(8,128)(2,1)} %param.44) | copy-start | bytes 1572868
  262.4 0.7 copy-start.10
  370.7 5.7 %copy-start.2 = (bf16[512,4096]{1,0:T(8,128)(2,1)S(1)}, bf16[512,4096]{1,0:T(8,128)(2,1)}, u32[]{:S(2)}) copy-start(bf16[512,4096]{1,0:T(8,128)(2,1)} %all-reduce.9.cloned.1.call-done) | copy-start | bytes 12582916
  376.4 3.6 copy-start.13
  376.4 3.6 copy-start.14
  380.0 5.6 %copy-start.1 = (bf16[512,1,256]{2,0,1:T(8,128)(2,1)S(1)}, bf16[512,1,256]{2,0,1:T(8,128)(2,1)}, u32[]{:S(2)}) copy-start(bf16[512,1,256]{2,0,1:T(8,128)(2,1)} %param.39) | copy-start | bytes 786436
  (1 other events, 0.7 us)
Sparse Core Ops, SparseCore 0:
  35.1 106.7 all-gather.2
  144.4 108.0 all-gather.4
  262.5 108.1 all-reduce.8

commit v10 on v8

--- a/solution.py
+++ b/solution.py
@@ -62,6 +62,9 @@
     scores = jnp.einsum("klgn,ksgn->kgls", c_grouped, b_grouped, preferred_element_type=jnp.float32)
     scores = jnp.repeat(scores, per_group, axis=1)
     cum = jnp.cumsum(log_retain.reshape(block_count, SPAN, head_count), axis=1)
+    w_out_all = lax.all_gather(w_out, "seq", axis=1, tiled=True)
+    w_in_early, cum = lax.optimization_barrier((w_in, cum))
+    w_in_all = lax.all_gather(w_in_early, "seq", axis=0, tiled=True)
     cum_heads = jnp.transpose(cum, (0, 2, 1))
     later_pos = lax.broadcasted_iota(jnp.int32, (SPAN, SPAN), 0)
     earlier_pos = lax.broadcasted_iota(jnp.int32, (SPAN, SPAN), 1)
@@ -106,8 +109,6 @@
     grouped = gated.reshape(seq_rows, group_count, per_group * head_width)
     grouped = grouped * lax.rsqrt(jnp.mean(grouped * grouped, axis=-1, keepdims=True) + 1e-05)
     ssd_out = (grouped.reshape(seq_rows, channels) * norm_gain[None, :]).astype(jnp.bfloat16)
-    w_in_all = lax.all_gather(w_in, "seq", axis=0, tiled=True)
-    ssd_out, w_in_all = lax.optimization_barrier((ssd_out, w_in_all))
     own_rows = residual.shape[0]
     mine = lax.axis_index("head")
     residual_rows = lax.dynamic_update_slice_in_dim(
@@ -118,10 +119,11 @@
     )
     partial_sum = jnp.dot(
         ssd_out,
-        lax.all_gather(w_out, "seq", axis=1, tiled=True),
+        w_out_all,
         preferred_element_type=jnp.float32,
     )
     with_residual = (partial_sum + residual_rows).astype(jnp.bfloat16)
+    with_residual, w_in_all = lax.optimization_barrier((with_residual, w_in_all))
     hidden = lax.psum(with_residual, "head").astype(jnp.float32)
     unit = refusal / jnp.sqrt(jnp.sum(refusal * refusal) + 1e-06)
     coef = jnp.dot(hidden, unit, precision=lax.Precision.HIGHEST)

time: 366 us -> 392 us (1.071)
  starting transfers between devices: 80.9 us -> 115 us
  waiting for transfers between devices: 199 us -> 190 us
    ppermute x5, waiting for transfers between devices: 42.3 us -> 9.74 us  [shifted(): lax.ppermute(a, axis, pairs)]
    ppermute x6, starting transfers between devices: 67.8 us -> 97 us  [shifted(): lax.ppermute(s.astype(jnp.bfloat16), axis, pairs).astype(jnp.float32)]
    psum x1, waiting for transfers between devices: 106 us -> 131 us  [body(): hidden = lax.psum(with_residual, 'head').astype(jnp.float32)]
    ppermute x5, starting transfers between devices: 13 us -> 18.1 us  [shifted(): lax.ppermute(a, axis, pairs)]
  transfers between devices with their start and end apart: 14 -> 14, of which waited for: 10 -> 10; matrix products, arithmetic and copies ran while one was open for 12% -> 14% of each run, Pallas kernels for 0% -> 0%
where the time goes in v10:
time: 392 us; the launch traced here: 391 us
  waiting for transfers between devices  190 us (48%)
  starting transfers between devices  115 us (29%)
  matrix products  30 us (8%)
  local copies, waits for them, and re-layouts  24 us (6%)
  other arithmetic  16.7 us (4%)
  between operations  14.9 us (4%)
    psum x1, waiting for transfers between devices, body(): hidden = lax.psum(with_residual, 'head').astype(jnp.float32)  131 us
    ppermute x6, starting transfers between devices, shifted(): lax.ppermute(s.astype(jnp.bfloat16), axis, pairs).astype(jnp.float32)  97 us
    ppermute x6, waiting for transfers between devices, shifted(): lax.ppermute(s.astype(jnp.bfloat16), axis, pairs).astype(jnp.float32)  33.3 us
    ppermute x5, starting transfers between devices, shifted(): lax.ppermute(a, axis, pairs)  18.1 us
    all_gather x1, waiting for transfers between devices, body(): w_in_all = lax.all_gather(w_in_early, 'seq', axis=0, tiled=True)  15.2 us
    ppermute x5, waiting for transfers between devices, shifted(): lax.ppermute(a, axis, pairs)  9.74 us
    convert_element_type x2, local copies, waits for them, and re-layouts, body(): gate_z.reshape(block_count, SPAN, head_count, head_width)  8.74 us
  transfers between devices with their start and end apart: 14, of which 10 were waited for; matrix products, arithmetic and copies ran while one was open for 14% of the time, Pallas kernels for 0%

profile of v10, /device:TPU:1, one launch (start us, length us, event | category | flops | bytes accessed | tf_op | source)
XLA Modules:
  0.0 391.1 jit_solution(349736526655312717)
XLA Ops:
  10.1 3.0 reshape.159
  26.0 6.3 %collective-permute-start.5 = (bf16[16,16384]{1,0:T(8,128)(2,1)S(1)}, bf16[16,16384]{1,0:T(8,128)(2,1)S(1)}, u32[]{:S(2)}, u32[]{:S(2)}) collective-permute-start(bf16[16,16384]{1,0:T(8,128)(2,1)S(1)} %add_convert_fusion), channel_id=1, source_target_pairs={{0,8},{8,16},{16,24},{24,32},{32,40},{40,48},{48,56},{56,64},{64,7... | collective-permute-start | bytes 1572872 | tf_op jit(solution)/shard_map/ppermute | solution.py:17
  32.3 9.4 %collective-permute-done.5 = bf16[16,16384]{1,0:T(8,128)(2,1)S(1)} collective-permute-done((bf16[16,16384]{1,0:T(8,128)(2,1)S(1)}, bf16[16,16384]{1,0:T(8,128)(2,1)S(1)}, u32[]{:S(2)}, u32[]{:S(2)}) %collective-permute-start.5) | collective-permute-done | bytes 524320 | tf_op jit(solution)/shard_map/ppermute | solution.py:17
  41.7 5.3 %collective-permute-start.6 = (bf16[16,16384]{1,0:T(8,128)(2,1)S(1)}, bf16[16,16384]{1,0:T(8,128)(2,1)S(1)}, u32[]{:S(2)}, u32[]{:S(2)}) collective-permute-start(bf16[16,16384]{1,0:T(8,128)(2,1)S(1)} %collective-permute-done.5), channel_id=1, source_target_pairs={{0,8},{8,16},{16,24},{24,32},{32,40},{40,48},{48,56},{56,64},{64,7... | collective-permute-start | bytes 1572872 | tf_op jit(solution)/shard_map/ppermute | solution.py:17
  47.0 4.0 %collective-permute-start = (f32[16]{0:T(128)S(1)}, f32[16]{0:T(128)S(1)}, u32[]{:S(2)}, u32[]{:S(2)}) collective-permute-start(f32[16]{0:T(128)S(1)} %get-tuple-element.10), channel_id=1, source_target_pairs={{0,8},{8,16},{16,24},{24,32},{32,40},{40,48},{48,56},{56,64},{64,7... | collective-permute-start | bytes 200 | tf_op jit(solution)/shard_map/ppermute | solution.py:16
  51.0 6.1 %collective-permute-done = f32[16]{0:T(128)S(1)} collective-permute-done((f32[16]{0:T(128)S(1)}, f32[16]{0:T(128)S(1)}, u32[]{:S(2)}, u32[]{:S(2)}) %collective-permute-start) | collective-permute-done | bytes 96 | tf_op jit(solution)/shard_map/ppermute | solution.py:16
  57.1 6.7 %collective-permute-start.1 = (f32[16]{0:T(128)S(1)}, f32[16]{0:T(128)S(1)}, u32[]{:S(2)}, u32[]{:S(2)}) collective-permute-start(f32[16]{0:T(128)S(1)} %collective-permute-done), channel_id=1, source_target_pairs={{0,8},{8,16},{16,24},{24,32},{32,40},{40,48},{48,56},{56,64},{64,7... | collective-permute-start | bytes 200 | tf_op jit(solution)/shard_map/ppermute | solution.py:16
  64.7 54.3 %collective-permute-start.7 = (bf16[16,16384]{1,0:T(8,128)(2,1)S(1)}, bf16[16,16384]{1,0:T(8,128)(2,1)S(1)}, u32[]{:S(2)}, u32[]{:S(2)}) collective-permute-start(bf16[16,16384]{1,0:T(8,128)(2,1)S(1)} %fusion.32), channel_id=1, source_target_pairs={{0,16},{8,24},{16,32},{24,40},{32,48},{40,56},{48,64},{56,72},{64,... | collective-permute-start | bytes 1572872 | tf_op jit(solution)/shard_map/ppermute | solution.py:17
  119.1 13.7 %collective-permute-done.7 = bf16[16,16384]{1,0:T(8,128)(2,1)S(1)} collective-permute-done((bf16[16,16384]{1,0:T(8,128)(2,1)S(1)}, bf16[16,16384]{1,0:T(8,128)(2,1)S(1)}, u32[]{:S(2)}, u32[]{:S(2)}) %collective-permute-start.7) | collective-permute-done | bytes 524320 | tf_op jit(solution)/shard_map/ppermute | solution.py:17
  134.5 4.7 %collective-permute-start.2 = (f32[16]{0:T(128)S(1)}, f32[16]{0:T(128)S(1)}, u32[]{:S(2)}, u32[]{:S(2)}) collective-permute-start(f32[16]{0:T(128)S(1)} %get-tuple-element.21), channel_id=1, source_target_pairs={{0,16},{8,24},{16,32},{24,40},{32,48},{40,56},{48,64},{56,72},{64,... | collective-permute-start | bytes 200 | tf_op jit(solution)/shard_map/ppermute | solution.py:16
  139.2 2.3 collective-permute-done.2
  141.9 24.0 %collective-permute-start.9 = (bf16[16,16384]{1,0:T(8,128)(2,1)S(1)}, bf16[16,16384]{1,0:T(8,128)(2,1)S(1)}, u32[]{:S(2)}, u32[]{:S(2)}) collective-permute-start(bf16[16,16384]{1,0:T(8,128)(2,1)S(1)} %fusion.33), channel_id=1, source_target_pairs={{0,64},{8,72},{16,80},{24,88},{32,96},{40,104},{48,112},{56,120},{... | collective-permute-start | bytes 1572872 | tf_op jit(solution)/shard_map/ppermute | solution.py:17
  168.5 10.2 %collective-permute-done.9 = bf16[16,16384]{1,0:T(8,128)(2,1)S(1)} collective-permute-done((bf16[16,16384]{1,0:T(8,128)(2,1)S(1)}, bf16[16,16384]{1,0:T(8,128)(2,1)S(1)}, u32[]{:S(2)}, u32[]{:S(2)}) %collective-permute-start.9) | collective-permute-done | bytes 524320 | tf_op jit(solution)/shard_map/ppermute | solution.py:17
  180.1 5.8 %collective-permute-start.10 = (bf16[16,16384]{1,0:T(8,128)(2,1)}, bf16[16,16384]{1,0:T(8,128)(2,1)}, u32[]{:S(2)}, u32[]{:S(2)}) collective-permute-start(bf16[16,16384]{1,0:T(8,128)(2,1)} %fusion.39), channel_id=1, source_target_pairs={{0,128},{8,136},{16,144},{24,152},{32,160},{40,168},{48,176},{56,1... | collective-permute-start | bytes 1572872 | tf_op jit(solution)/shard_map/ppermute | solution.py:17
  185.9 4.1 %reshape.160 = f32[2,256,16,64]{3,2,1,0:T(8,128)} reshape(bf16[512,1024]{1,0:T(8,128)(2,1)} %param.13) | data formatting | bytes 3145728 | tf_op jit(solution)/shard_map/convert_element_type | solution.py:107
  190.0 4.6 %copy.44 = f32[2,256,16,64]{1,3,2,0:T(8,128)} copy(f32[2,256,16,64]{3,2,1,0:T(8,128)} %reshape.160) | data formatting | bytes 4194304 | tf_op jit(solution)/shard_map/convert_element_type | solution.py:107
  201.0 5.3 %fusion.19 = f32[2,16,64,256]{3,2,1,0:T(8,128)S(1)} fusion(bf16[2,256,256]{2,1,0:T(8,128)(2,1)S(1)} %bitcast.53, f32[1,16,256,64]{2,3,1,0:T(8,128)} %get-tuple-element.23, f32[16,256,64]{1,2,0:T(8,128)S(1)} %copy.40, f32[2,16]{1,0:T(2,128)S(1)} %copy-done.12), kind=kOutput, calls=%fused_computation.26 | convolution fusion | flops 1611661312 | bytes 4456576 | tf_op jit(solution)/shard_map/klhn,khnp->klhp/dot_general | solution.py:103
  206.4 3.0 multiply_reduce_fusion
  211.3 7.6 %fusion.27 = f32[512,4096]{1,0:T(8,128)S(1)} fusion(bf16[1024,4096]{1,0:T(8,128)(2,1)} %all-gather.3.cloned.1.call-done, f32[512,1024]{0,1:T(8,128)S(1)} %bitcast.54, f32[1024]{0:T(1024)S(1)} %copy-done.11, f32[512]{0:T(512)S(1)} %bitcast.63), kind=kOutput, calls=%fused_computation.32 | convolution fusion | flops 4296540160 | bytes 18880512 | tf_op jit(solution)/shard_map/dot_general | solution.py:120
  219.2 2.6 convert_element_type.97
  221.7 15.2 %all-gather.5.cloned.1.call-done = bf16[4096,1024]{1,0:T(8,128)(2,1)} async-done(((bf16[128,1024]{1,0:T(8,128)(2,1)}), bf16[4096,1024]{1,0:T(8,128)(2,1)}) %all-gather.5.cloned.1.call-update) | async-done | bytes 8388624 | tf_op jit(solution)/shard_map/all_gather | solution.py:67
  238.3 131.4 %all-reduce.3.cloned.1.call-done = bf16[512,4096]{1,0:T(8,128)(2,1)} async-done(((bf16[512,4096]{1,0:T(8,128)(2,1)}), bf16[512,4096]{1,0:T(8,128)(2,1)}) %all-reduce.3.cloned.1.call-update) | async-done | bytes 4194320 | tf_op jit(solution)/shard_map/psum | solution.py:127
  369.7 5.7 %fusion.47 = f32[1,512]{1,0:T(1,128)S(1)} fusion(bf16[512,4096]{1,0:T(8,128)(2,1)} %all-reduce.3.cloned.1.call-done, f32[4096,1]{0,1:T(1,128)S(1)} %bitcast.61), kind=kOutput, calls=%fused_computation.78 | convolution fusion | flops 25165824 | bytes 4212736 | tf_op jit(solution)/shard_map/dot_general | solution.py:129
  379.0 5.6 %fusion.24 = bf16[512,1024]{1,0:T(8,128)(2,1)} fusion(bf16[4096,1024]{1,0:T(8,128)(2,1)S(1)} %copy-done.14, bf16[512,4096]{1,0:T(8,128)(2,1)S(1)} %get-tuple-element.15, f32[4096]{0:T(1024)S(1)} %copy-done.15, f32[512]{0:T(512)S(1)} %add_rsqrt_fusion), kind=kOutput, calls=%fused_computation.31 | convolution fusion | flops 4303880192 | bytes 13649920 | tf_op jit(solution)/shard_map/dot_general | solution.py:138
  (93 shorter events, 35.4 us)
Async XLA Ops:
  7.2 187.5 %copy-start = (bf16[512,1,256]{2,0,1:T(8,128)(2,1)S(1)}, bf16[512,1,256]{2,0,1:T(8,128)(2,1)}, u32[]{:S(2)}) copy-start(bf16[512,1,256]{2,0,1:T(8,128)(2,1)} %param.15) | copy-start | bytes 786436
  7.2 204.1 %all-gather.3.cloned.1.call-start = ((), (), s32[]{:S(2)}) async-start(), calls=%async_computation | async-start | bytes 8650752 | tf_op jit(solution)/shard_map/all_gather | solution.py:65
  7.9 229.1 %all-gather.5.cloned.1.call-start = ((), (), s32[]{:S(2)}) async-start(), calls=%async_computation.1 | async-start | bytes 8650752 | tf_op jit(solution)/shard_map/all_gather | solution.py:67
  26.0 15.7 %collective-permute-start.5 = (bf16[16,16384]{1,0:T(8,128)(2,1)S(1)}, bf16[16,16384]{1,0:T(8,128)(2,1)S(1)}, u32[]{:S(2)}, u32[]{:S(2)}) collective-permute-start(bf16[16,16384]{1,0:T(8,128)(2,1)S(1)} %add_convert_fusion), channel_id=1, source_target_pairs={{0,8},{8,16},{16,24},{24,32},{32,40},{40,48},{48,56},{56,64},{64,7... | collective-permute-start | bytes 1572872 | tf_op jit(solution)/shard_map/ppermute | solution.py:17
  41.7 22.8 %collective-permute-start.6 = (bf16[16,16384]{1,0:T(8,128)(2,1)S(1)}, bf16[16,16384]{1,0:T(8,128)(2,1)S(1)}, u32[]{:S(2)}, u32[]{:S(2)}) collective-permute-start(bf16[16,16384]{1,0:T(8,128)(2,1)S(1)} %collective-permute-done.5), channel_id=1, source_target_pairs={{0,8},{8,16},{16,24},{24,32},{32,40},{40,48},{48,56},{56,64},{64,7... | collective-permute-start | bytes 1572872 | tf_op jit(solution)/shard_map/ppermute | solution.py:17
  47.0 10.1 %collective-permute-start = (f32[16]{0:T(128)S(1)}, f32[16]{0:T(128)S(1)}, u32[]{:S(2)}, u32[]{:S(2)}) collective-permute-start(f32[16]{0:T(128)S(1)} %get-tuple-element.10), channel_id=1, source_target_pairs={{0,8},{8,16},{16,24},{24,32},{32,40},{40,48},{48,56},{56,64},{64,7... | collective-permute-start | bytes 200 | tf_op jit(solution)/shard_map/ppermute | solution.py:16
  57.1 7.4 %collective-permute-start.1 = (f32[16]{0:T(128)S(1)}, f32[16]{0:T(128)S(1)}, u32[]{:S(2)}, u32[]{:S(2)}) collective-permute-start(f32[16]{0:T(128)S(1)} %collective-permute-done), channel_id=1, source_target_pairs={{0,8},{8,16},{16,24},{24,32},{32,40},{40,48},{48,56},{56,64},{64,7... | collective-permute-start | bytes 200 | tf_op jit(solution)/shard_map/ppermute | solution.py:16
  64.7 68.1 %collective-permute-start.7 = (bf16[16,16384]{1,0:T(8,128)(2,1)S(1)}, bf16[16,16384]{1,0:T(8,128)(2,1)S(1)}, u32[]{:S(2)}, u32[]{:S(2)}) collective-permute-start(bf16[16,16384]{1,0:T(8,128)(2,1)S(1)} %fusion.32), channel_id=1, source_target_pairs={{0,16},{8,24},{16,32},{24,40},{32,48},{40,56},{48,64},{56,72},{64,... | collective-permute-start | bytes 1572872 | tf_op jit(solution)/shard_map/ppermute | solution.py:17
  119.0 250.7 %all-reduce.3.cloned.1.call-start = ((), (), s32[]{:S(2)}) async-start(), calls=%async_computation.2 | async-start | bytes 8388608 | tf_op jit(solution)/shard_map/psum | solution.py:127
  133.1 8.3 %collective-permute-start.8 = (bf16[16,16384]{1,0:T(8,128)(2,1)S(1)}, bf16[16,16384]{1,0:T(8,128)(2,1)S(1)}, u32[]{:S(2)}, u32[]{:S(2)}) collective-permute-start(bf16[16,16384]{1,0:T(8,128)(2,1)S(1)} %fusion.40), channel_id=1, source_target_pairs={{0,32},{8,40},{16,48},{24,56},{32,64},{40,72},{48,80},{56,88},{64,... | collective-permute-start | bytes 1572872 | tf_op jit(solution)/shard_map/ppermute | solution.py:17
  134.5 7.0 %collective-permute-start.2 = (f32[16]{0:T(128)S(1)}, f32[16]{0:T(128)S(1)}, u32[]{:S(2)}, u32[]{:S(2)}) collective-permute-start(f32[16]{0:T(128)S(1)} %get-tuple-element.21), channel_id=1, source_target_pairs={{0,16},{8,24},{16,32},{24,40},{32,48},{40,56},{48,64},{56,72},{64,... | collective-permute-start | bytes 200 | tf_op jit(solution)/shard_map/ppermute | solution.py:16
  141.9 36.9 %collective-permute-start.9 = (bf16[16,16384]{1,0:T(8,128)(2,1)S(1)}, bf16[16,16384]{1,0:T(8,128)(2,1)S(1)}, u32[]{:S(2)}, u32[]{:S(2)}) collective-permute-start(bf16[16,16384]{1,0:T(8,128)(2,1)S(1)} %fusion.33), channel_id=1, source_target_pairs={{0,64},{8,72},{16,80},{24,88},{32,96},{40,104},{48,112},{56,120},{... | collective-permute-start | bytes 1572872 | tf_op jit(solution)/shard_map/ppermute | solution.py:17
  165.9 2.0 collective-permute-start.3
  178.8 11.3 %copy-start.4 = (bf16[16,16384]{1,0:T(8,128)(2,1)}, bf16[16,16384]{1,0:T(8,128)(2,1)S(1)}, u32[]{:S(2)}) copy-start(bf16[16,16384]{1,0:T(8,128)(2,1)S(1)} %collective-permute-done.9) | copy-start | bytes 1572868
  180.1 17.6 %collective-permute-start.10 = (bf16[16,16384]{1,0:T(8,128)(2,1)}, bf16[16,16384]{1,0:T(8,128)(2,1)}, u32[]{:S(2)}, u32[]{:S(2)}) collective-permute-start(bf16[16,16384]{1,0:T(8,128)(2,1)} %fusion.39), channel_id=1, source_target_pairs={{0,128},{8,136},{16,144},{24,152},{32,160},{40,168},{48,176},{56,1... | collective-permute-start | bytes 1572872 | tf_op jit(solution)/shard_map/ppermute | solution.py:17
  190.0 5.7 %copy-start.13 = (f32[16]{0:T(128)S(1)}, f32[16]{0:T(128)}, u32[]{:S(2)}) copy-start(f32[16]{0:T(128)} %get-tuple-element.17) | copy-start | bytes 196
  195.7 2.0 collective-permute-start.4
  200.4 6.0 %copy-start.16 = (f32[16]{0:T(128)S(1)}, f32[16]{0:T(128)}, u32[]{:S(2)}) copy-start(f32[16]{0:T(128)} %param.17) | copy-start | bytes 196
  201.0 5.4 %copy-start.3 = (f32[2,256,16,64]{1,3,2,0:T(8,128)S(1)}, f32[2,256,16,64]{1,3,2,0:T(8,128)}, u32[]{:S(2)}) copy-start(f32[2,256,16,64]{1,3,2,0:T(8,128)} %copy.44) | copy-start | bytes 6291460
  201.0 5.4 %copy-start.6 = (bf16[2,256,16,64]{1,3,2,0:T(8,128)(2,1)S(1)}, bf16[2,256,16,64]{1,3,2,0:T(8,128)(2,1)}, u32[]{:S(2)}) copy-start(bf16[2,256,16,64]{1,3,2,0:T(8,128)(2,1)} %copy-done.5) | copy-start | bytes 3145732
  211.3 7.6 %copy-start.9 = (bf16[64,4096]{1,0:T(8,128)(2,1)S(1)}, bf16[64,4096]{1,0:T(8,128)(2,1)}, u32[]{:S(2)}) copy-start(bf16[64,4096]{1,0:T(8,128)(2,1)} %param.20) | copy-start | bytes 1572868
  221.7 15.3 %copy-start.10 = (f32[4096]{0:T(1024)S(1)}, f32[4096]{0:T(1024)}, u32[]{:S(2)}) copy-start(f32[4096]{0:T(1024)} %param.21) | copy-start | bytes 49156
  369.7 5.7 %copy-start.2 = (bf16[512,4096]{1,0:T(8,128)(2,1)S(1)}, bf16[512,4096]{1,0:T(8,128)(2,1)}, u32[]{:S(2)}) copy-start(bf16[512,4096]{1,0:T(8,128)(2,1)} %all-reduce.3.cloned.1.call-done) | copy-start | bytes 12582916
  379.0 5.6 %copy-start.1 = (bf16[512,1,256]{2,0,1:T(8,128)(2,1)S(1)}, bf16[512,1,256]{2,0,1:T(8,128)(2,1)}, u32[]{:S(2)}) copy-start(bf16[512,1,256]{2,0,1:T(8,128)(2,1)} %param.15) | copy-start | bytes 786436
  (7 other events, 25.5 us)
Sparse Core Ops, SparseCore 0:
  10.5 132.9 all-gather.2
  146.0 90.9 all-gather.4
  239.7 130.0 all-reduce.2

commit v11 on v8

--- a/solution.py
+++ b/solution.py
@@ -19,6 +19,9 @@
 
     acc = shifted((decay, state), 1)
     distance = 1
+    if devices > 2:
+        acc = carry_combine(shifted((decay, state), 2), acc)
+        distance = 2
     while distance < devices:
         acc = carry_combine(shifted(acc, distance), acc)
         distance *= 2

time: 366 us -> 379 us (1.036)
  waiting for transfers between devices: 199 us -> 233 us
  starting transfers between devices: 80.9 us -> 59.8 us
    ppermute x6, starting transfers between devices: 67.8 us -> 46.4 us  [shifted(): lax.ppermute(s.astype(jnp.bfloat16), axis, pairs).astype(jnp.float32)]
    ppermute x6, waiting for transfers between devices: 36.8 us -> 52.7 us  [shifted(): lax.ppermute(s.astype(jnp.bfloat16), axis, pairs).astype(jnp.float32)]
    all_gather x1, waiting for transfers between devices: 12.6 us -> 24.2 us  [body(): lax.all_gather(w_out, 'seq', axis=1, tiled=True)]
    ppermute x5, waiting for transfers between devices: 42.3 us -> 48.9 us  [shifted(): lax.ppermute(a, axis, pairs)]
  transfers between devices with their start and end apart: 14 -> 14, of which waited for: 10 -> 8; matrix products, arithmetic and copies ran while one was open for 12% -> 12% of each run, Pallas kernels for 0% -> 0%
where the time goes in v11:
time: 379 us; the launch traced here: 378 us
  waiting for transfers between devices  233 us (61%)
  starting transfers between devices  59.8 us (16%)
  matrix products  29.5 us (8%)
  local copies, waits for them, and re-layouts  24.7 us (7%)
  other arithmetic  16.3 us (4%)
  between operations  14.9 us (4%)
    psum x1, waiting for transfers between devices, body(): hidden = lax.psum(with_residual, 'head').astype(jnp.float32)  106 us
    ppermute x6, waiting for transfers between devices, shifted(): lax.ppermute(s.astype(jnp.bfloat16), axis, pairs).astype(jnp.float32)  52.7 us
    ppermute x5, waiting for transfers between devices, shifted(): lax.ppermute(a, axis, pairs)  48.9 us
    ppermute x6, starting transfers between devices, shifted(): lax.ppermute(s.astype(jnp.bfloat16), axis, pairs).astype(jnp.float32)  46.4 us
    all_gather x1, waiting for transfers between devices, body(): lax.all_gather(w_out, 'seq', axis=1, tiled=True)  24.2 us
    ppermute x5, starting transfers between devices, shifted(): lax.ppermute(a, axis, pairs)  13.2 us
    convert_element_type x2, local copies, waits for them, and re-layouts, body(): gate_z.reshape(block_count, SPAN, head_count, head_width)  8.73 us
  transfers between devices with their start and end apart: 14, of which 8 were waited for; matrix products, arithmetic and copies ran while one was open for 12% of the time, Pallas kernels for 0%

profile of v11, /device:TPU:1, one launch (start us, length us, event | category | flops | bytes accessed | tf_op | source)
XLA Modules:
  0.0 378.0 jit_solution(9773590898595245796)
XLA Ops:
  10.1 3.0 reshape.178
  26.5 5.8 %collective-permute-start.5 = (bf16[16,16384]{1,0:T(8,128)(2,1)S(1)}, bf16[16,16384]{1,0:T(8,128)(2,1)S(1)}, u32[]{:S(2)}, u32[]{:S(2)}) collective-permute-start(bf16[16,16384]{1,0:T(8,128)(2,1)S(1)} %add_convert_fusion), channel_id=1, source_target_pairs={{0,16},{8,24},{16,32},{24,40},{32,48},{40,56},{48,64},{56,72},{64,... | collective-permute-start | bytes 1572872 | tf_op jit(solution)/shard_map/ppermute | solution.py:17
  32.3 6.9 %collective-permute-start.6 = (bf16[16,16384]{1,0:T(8,128)(2,1)S(1)}, bf16[16,16384]{1,0:T(8,128)(2,1)S(1)}, u32[]{:S(2)}, u32[]{:S(2)}) collective-permute-start(bf16[16,16384]{1,0:T(8,128)(2,1)S(1)} %add_convert_fusion), channel_id=1, source_target_pairs={{0,8},{8,16},{16,24},{24,32},{32,40},{40,48},{48,56},{56,64},{64,7... | collective-permute-start | bytes 1572872 | tf_op jit(solution)/shard_map/ppermute | solution.py:17
  39.3 3.0 collective-permute-start
  42.3 2.2 collective-permute-start.1
  44.5 24.6 %collective-permute-done = f32[16]{0:T(128)S(1)} collective-permute-done((f32[16]{0:T(128)S(1)}, f32[16]{0:T(128)S(1)}, u32[]{:S(2)}, u32[]{:S(2)}) %collective-permute-start) | collective-permute-done | bytes 96 | tf_op jit(solution)/shard_map/ppermute | solution.py:16
  69.5 10.0 %collective-permute-start.7 = (bf16[16,16384]{1,0:T(8,128)(2,1)S(1)}, bf16[16,16384]{1,0:T(8,128)(2,1)S(1)}, u32[]{:S(2)}, u32[]{:S(2)}) collective-permute-start(bf16[16,16384]{1,0:T(8,128)(2,1)S(1)} %fusion.29), channel_id=1, source_target_pairs={{0,16},{8,24},{16,32},{24,40},{32,48},{40,56},{48,64},{56,72},{64,... | collective-permute-start | bytes 1572872 | tf_op jit(solution)/shard_map/ppermute | solution.py:17
  79.6 44.5 %collective-permute-done.7 = bf16[16,16384]{1,0:T(8,128)(2,1)S(1)} collective-permute-done((bf16[16,16384]{1,0:T(8,128)(2,1)S(1)}, bf16[16,16384]{1,0:T(8,128)(2,1)S(1)}, u32[]{:S(2)}, u32[]{:S(2)}) %collective-permute-start.7) | collective-permute-done | bytes 524320 | tf_op jit(solution)/shard_map/ppermute | solution.py:17
  124.4 13.2 %collective-permute-start.8 = (bf16[16,16384]{1,0:T(8,128)(2,1)S(1)}, bf16[16,16384]{1,0:T(8,128)(2,1)S(1)}, u32[]{:S(2)}, u32[]{:S(2)}) collective-permute-start(bf16[16,16384]{1,0:T(8,128)(2,1)S(1)} %fusion.37), channel_id=1, source_target_pairs={{0,32},{8,40},{16,48},{24,56},{32,64},{40,72},{48,80},{56,88},{64,... | collective-permute-start | bytes 1572872 | tf_op jit(solution)/shard_map/ppermute | solution.py:17
  138.9 21.4 %collective-permute-done.2 = f32[16]{0:T(128)S(1)} collective-permute-done((f32[16]{0:T(128)S(1)}, f32[16]{0:T(128)S(1)}, u32[]{:S(2)}, u32[]{:S(2)}) %collective-permute-start.2) | collective-permute-done | bytes 96 | tf_op jit(solution)/shard_map/ppermute | solution.py:16
  160.8 4.0 %collective-permute-start.9 = (bf16[16,16384]{1,0:T(8,128)(2,1)S(1)}, bf16[16,16384]{1,0:T(8,128)(2,1)S(1)}, u32[]{:S(2)}, u32[]{:S(2)}) collective-permute-start(bf16[16,16384]{1,0:T(8,128)(2,1)S(1)} %fusion.30), channel_id=1, source_target_pairs={{0,64},{8,72},{16,80},{24,88},{32,96},{40,104},{48,112},{56,120},{... | collective-permute-start | bytes 1572872 | tf_op jit(solution)/shard_map/ppermute | solution.py:17
  164.8 5.2 %collective-permute-start.3 = (f32[16]{0:T(128)S(1)}, f32[16]{0:T(128)S(1)}, u32[]{:S(2)}, u32[]{:S(2)}) collective-permute-start(f32[16]{0:T(128)S(1)} %get-tuple-element.15), channel_id=1, source_target_pairs={{0,32},{8,40},{16,48},{24,56},{32,64},{40,72},{48,80},{56,88},{64,... | collective-permute-start | bytes 200 | tf_op jit(solution)/shard_map/ppermute | solution.py:16
  170.8 8.2 %collective-permute-done.9 = bf16[16,16384]{1,0:T(8,128)(2,1)S(1)} collective-permute-done((bf16[16,16384]{1,0:T(8,128)(2,1)S(1)}, bf16[16,16384]{1,0:T(8,128)(2,1)S(1)}, u32[]{:S(2)}, u32[]{:S(2)}) %collective-permute-start.9) | collective-permute-done | bytes 524320 | tf_op jit(solution)/shard_map/ppermute | solution.py:17
  180.3 6.4 %collective-permute-start.10 = (bf16[16,16384]{1,0:T(8,128)(2,1)}, bf16[16,16384]{1,0:T(8,128)(2,1)}, u32[]{:S(2)}, u32[]{:S(2)}) collective-permute-start(bf16[16,16384]{1,0:T(8,128)(2,1)} %fusion.36), channel_id=1, source_target_pairs={{0,128},{8,136},{16,144},{24,152},{32,160},{40,168},{48,176},{56,1... | collective-permute-start | bytes 1572872 | tf_op jit(solution)/shard_map/ppermute | solution.py:17
  186.8 4.1 %reshape.179 = f32[2,256,16,64]{3,2,1,0:T(8,128)} reshape(bf16[512,1024]{1,0:T(8,128)(2,1)} %param.13) | data formatting | bytes 3145728 | tf_op jit(solution)/shard_map/convert_element_type | solution.py:107
  190.9 4.6 %copy.44 = f32[2,256,16,64]{1,3,2,0:T(8,128)} copy(f32[2,256,16,64]{3,2,1,0:T(8,128)} %reshape.179) | data formatting | bytes 4194304 | tf_op jit(solution)/shard_map/convert_element_type | solution.py:107
  203.5 5.3 %fusion.19 = f32[2,16,64,256]{3,2,1,0:T(8,128)S(1)} fusion(bf16[2,256,256]{2,1,0:T(8,128)(2,1)S(1)} %bitcast.60, f32[1,16,256,64]{2,3,1,0:T(8,128)} %get-tuple-element.19, f32[16,256,64]{1,2,0:T(8,128)S(1)} %copy.40, f32[2,16]{1,0:T(2,128)S(1)} %subtract_exponential_fusion), kind=kOutput, calls=%fused_computation.26 | convolution fusion | flops 1611661312 | bytes 4456576 | tf_op jit(solution)/shard_map/klhn,khnp->klhp/dot_general | solution.py:103
  208.9 3.1 multiply_reduce_fusion
  214.1 24.2 %all-gather.5.cloned.1.call-done = bf16[1024,4096]{1,0:T(8,128)(2,1)} async-done(((bf16[1024,128]{1,0:T(8,128)(2,1)}), bf16[1024,4096]{1,0:T(8,128)(2,1)}) %all-gather.5.cloned.1.call-update) | async-done | bytes 8388624 | tf_op jit(solution)/shard_map/all_gather | solution.py:124
  238.3 7.1 %fusion.43 = f32[512,4096]{1,0:T(8,128)S(1)} fusion(bf16[512,1024]{0,1:T(8,128)(2,1)S(1)} %multiply_convert_fusion.4, bf16[1024,4096]{1,0:T(8,128)(2,1)} %all-gather.5.cloned.1.call-done), kind=kOutput, calls=%fused_computation.75 | convolution fusion | flops 4294967296 | bytes 17825792 | tf_op jit(solution)/shard_map/dot_general | solution.py:122
  245.6 2.6 convert_element_type.97
  250.2 106.4 %all-reduce.3.cloned.1.call-done = bf16[512,4096]{1,0:T(8,128)(2,1)} async-done(((bf16[512,4096]{1,0:T(8,128)(2,1)}), bf16[512,4096]{1,0:T(8,128)(2,1)}) %all-reduce.3.cloned.1.call-update) | async-done | bytes 4194320 | tf_op jit(solution)/shard_map/psum | solution.py:128
  356.6 5.7 %fusion.44 = f32[1,512]{1,0:T(1,128)S(1)} fusion(bf16[512,4096]{1,0:T(8,128)(2,1)} %all-reduce.3.cloned.1.call-done, f32[4096,1]{0,1:T(1,128)S(1)} %bitcast.65), kind=kOutput, calls=%fused_computation.76 | convolution fusion | flops 25165824 | bytes 4212736 | tf_op jit(solution)/shard_map/dot_general | solution.py:130
  365.9 5.6 %fusion.24 = bf16[512,1024]{1,0:T(8,128)(2,1)} fusion(bf16[4096,1024]{1,0:T(8,128)(2,1)S(1)} %copy-done.13, bf16[512,4096]{1,0:T(8,128)(2,1)S(1)} %get-tuple-element.11, f32[4096]{0:T(1024)S(1)} %copy-done.14, f32[512]{0:T(512)S(1)} %add_rsqrt_fusion), kind=kOutput, calls=%fused_computation.31 | convolution fusion | flops 4303880192 | bytes 13649920 | tf_op jit(solution)/shard_map/dot_general | solution.py:139
  (92 shorter events, 35.9 us)
Async XLA Ops:
  7.2 188.3 %copy-start = (bf16[512,1,256]{2,0,1:T(8,128)(2,1)S(1)}, bf16[512,1,256]{2,0,1:T(8,128)(2,1)}, u32[]{:S(2)}) copy-start(bf16[512,1,256]{2,0,1:T(8,128)(2,1)} %param.15) | copy-start | bytes 786436
  7.2 206.9 %all-gather.3.cloned.1.call-start = ((), (), s32[]{:S(2)}) async-start(), calls=%async_computation | async-start | bytes 8650752 | tf_op jit(solution)/shard_map/all_gather | solution.py:112
  7.9 230.4 %all-gather.5.cloned.1.call-start = ((), (), s32[]{:S(2)}) async-start(), calls=%async_computation.1 | async-start | bytes 8650752 | tf_op jit(solution)/shard_map/all_gather | solution.py:124
  14.7 5.6 %copy-start.5 = (bf16[2,256,16,64]{1,3,2,0:T(8,128)(2,1)}, bf16[2,256,16,64]{1,3,2,0:T(8,128)(2,1)S(1)}, u32[]{:S(2)}) copy-start(bf16[2,256,16,64]{1,3,2,0:T(8,128)(2,1)S(1)} %copy.36) | copy-start | bytes 3145732
  26.5 42.7 %collective-permute-start.5 = (bf16[16,16384]{1,0:T(8,128)(2,1)S(1)}, bf16[16,16384]{1,0:T(8,128)(2,1)S(1)}, u32[]{:S(2)}, u32[]{:S(2)}) collective-permute-start(bf16[16,16384]{1,0:T(8,128)(2,1)S(1)} %add_convert_fusion), channel_id=1, source_target_pairs={{0,16},{8,24},{16,32},{24,40},{32,48},{40,56},{48,64},{56,72},{64,... | collective-permute-start | bytes 1572872 | tf_op jit(solution)/shard_map/ppermute | solution.py:17
  32.3 36.9 %collective-permute-start.6 = (bf16[16,16384]{1,0:T(8,128)(2,1)S(1)}, bf16[16,16384]{1,0:T(8,128)(2,1)S(1)}, u32[]{:S(2)}, u32[]{:S(2)}) collective-permute-start(bf16[16,16384]{1,0:T(8,128)(2,1)S(1)} %add_convert_fusion), channel_id=1, source_target_pairs={{0,8},{8,16},{16,24},{24,32},{32,40},{40,48},{48,56},{56,64},{64,7... | collective-permute-start | bytes 1572872 | tf_op jit(solution)/shard_map/ppermute | solution.py:17
  39.3 29.9 %collective-permute-start = (f32[16]{0:T(128)S(1)}, f32[16]{0:T(128)S(1)}, u32[]{:S(2)}, u32[]{:S(2)}) collective-permute-start(f32[16]{0:T(128)S(1)} %get-tuple-element.6), channel_id=1, source_target_pairs={{0,16},{8,24},{16,32},{24,40},{32,48},{40,56},{48,64},{56,72},{64,... | collective-permute-start | bytes 200 | tf_op jit(solution)/shard_map/ppermute | solution.py:16
  42.3 26.9 %collective-permute-start.1 = (f32[16]{0:T(128)S(1)}, f32[16]{0:T(128)S(1)}, u32[]{:S(2)}, u32[]{:S(2)}) collective-permute-start(f32[16]{0:T(128)S(1)} %get-tuple-element.6), channel_id=1, source_target_pairs={{0,8},{8,16},{16,24},{24,32},{32,40},{40,48},{48,56},{56,64},{64,7... | collective-permute-start | bytes 200 | tf_op jit(solution)/shard_map/ppermute | solution.py:16
  69.5 54.6 %collective-permute-start.7 = (bf16[16,16384]{1,0:T(8,128)(2,1)S(1)}, bf16[16,16384]{1,0:T(8,128)(2,1)S(1)}, u32[]{:S(2)}, u32[]{:S(2)}) collective-permute-start(bf16[16,16384]{1,0:T(8,128)(2,1)S(1)} %fusion.29), channel_id=1, source_target_pairs={{0,16},{8,24},{16,32},{24,40},{32,48},{40,56},{48,64},{56,72},{64,... | collective-permute-start | bytes 1572872 | tf_op jit(solution)/shard_map/ppermute | solution.py:17
  79.5 277.1 %all-reduce.3.cloned.1.call-start = ((), (), s32[]{:S(2)}) async-start(), calls=%async_computation.2 | async-start | bytes 8388608 | tf_op jit(solution)/shard_map/psum | solution.py:128
  124.4 35.9 %collective-permute-start.8 = (bf16[16,16384]{1,0:T(8,128)(2,1)S(1)}, bf16[16,16384]{1,0:T(8,128)(2,1)S(1)}, u32[]{:S(2)}, u32[]{:S(2)}) collective-permute-start(bf16[16,16384]{1,0:T(8,128)(2,1)S(1)} %fusion.37), channel_id=1, source_target_pairs={{0,32},{8,40},{16,48},{24,56},{32,64},{40,72},{48,80},{56,88},{64,... | collective-permute-start | bytes 1572872 | tf_op jit(solution)/shard_map/ppermute | solution.py:17
  137.6 22.7 %collective-permute-start.2 = (f32[16]{0:T(128)S(1)}, f32[16]{0:T(128)S(1)}, u32[]{:S(2)}, u32[]{:S(2)}) collective-permute-start(f32[16]{0:T(128)S(1)} %get-tuple-element.17), channel_id=1, source_target_pairs={{0,16},{8,24},{16,32},{24,40},{32,48},{40,56},{48,64},{56,72},{64,... | collective-permute-start | bytes 200 | tf_op jit(solution)/shard_map/ppermute | solution.py:16
  160.8 18.2 %collective-permute-start.9 = (bf16[16,16384]{1,0:T(8,128)(2,1)S(1)}, bf16[16,16384]{1,0:T(8,128)(2,1)S(1)}, u32[]{:S(2)}, u32[]{:S(2)}) collective-permute-start(bf16[16,16384]{1,0:T(8,128)(2,1)S(1)} %fusion.30), channel_id=1, source_target_pairs={{0,64},{8,72},{16,80},{24,88},{32,96},{40,104},{48,112},{56,120},{... | collective-permute-start | bytes 1572872 | tf_op jit(solution)/shard_map/ppermute | solution.py:17
  164.8 5.9 %collective-permute-start.3 = (f32[16]{0:T(128)S(1)}, f32[16]{0:T(128)S(1)}, u32[]{:S(2)}, u32[]{:S(2)}) collective-permute-start(f32[16]{0:T(128)S(1)} %get-tuple-element.15), channel_id=1, source_target_pairs={{0,32},{8,40},{16,48},{24,56},{32,64},{40,72},{48,80},{56,88},{64,... | collective-permute-start | bytes 200 | tf_op jit(solution)/shard_map/ppermute | solution.py:16
  179.0 11.9 %copy-start.4 = (bf16[16,16384]{1,0:T(8,128)(2,1)}, bf16[16,16384]{1,0:T(8,128)(2,1)S(1)}, u32[]{:S(2)}) copy-start(bf16[16,16384]{1,0:T(8,128)(2,1)S(1)} %collective-permute-done.9) | copy-start | bytes 1572868
  180.3 19.9 %collective-permute-start.10 = (bf16[16,16384]{1,0:T(8,128)(2,1)}, bf16[16,16384]{1,0:T(8,128)(2,1)}, u32[]{:S(2)}, u32[]{:S(2)}) collective-permute-start(bf16[16,16384]{1,0:T(8,128)(2,1)} %fusion.36), channel_id=1, source_target_pairs={{0,128},{8,136},{16,144},{24,152},{32,160},{40,168},{48,176},{56,1... | collective-permute-start | bytes 1572872 | tf_op jit(solution)/shard_map/ppermute | solution.py:17
  196.6 3.6 collective-permute-start.4
  202.8 6.0 %copy-start.11 = (f32[2,256,16]{1,2,0:T(8,128)S(1)}, f32[2,256,16]{1,2,0:T(8,128)}, u32[]{:S(2)}) copy-start(f32[2,256,16]{1,2,0:T(8,128)} %get-tuple-element.21) | copy-start | bytes 98308
  202.9 6.0 %copy-start.15 = (f32[16]{0:T(128)S(1)}, f32[16]{0:T(128)}, u32[]{:S(2)}) copy-start(f32[16]{0:T(128)} %param.17) | copy-start | bytes 196
  203.5 5.4 %copy-start.3 = (f32[2,256,16,64]{1,3,2,0:T(8,128)S(1)}, f32[2,256,16,64]{1,3,2,0:T(8,128)}, u32[]{:S(2)}) copy-start(f32[2,256,16,64]{1,3,2,0:T(8,128)} %copy.44) | copy-start | bytes 6291460
  203.5 5.4 %copy-start.6 = (bf16[2,256,16,64]{1,3,2,0:T(8,128)(2,1)S(1)}, bf16[2,256,16,64]{1,3,2,0:T(8,128)(2,1)}, u32[]{:S(2)}) copy-start(bf16[2,256,16,64]{1,3,2,0:T(8,128)(2,1)} %copy-done.5) | copy-start | bytes 3145732
  214.1 31.4 %copy-start.9 = (bf16[64,4096]{1,0:T(8,128)(2,1)S(1)}, bf16[64,4096]{1,0:T(8,128)(2,1)}, u32[]{:S(2)}) copy-start(bf16[64,4096]{1,0:T(8,128)(2,1)} %param.20) | copy-start | bytes 1572868
  356.6 5.7 %copy-start.2 = (bf16[512,4096]{1,0:T(8,128)(2,1)S(1)}, bf16[512,4096]{1,0:T(8,128)(2,1)}, u32[]{:S(2)}) copy-start(bf16[512,4096]{1,0:T(8,128)(2,1)} %all-reduce.3.cloned.1.call-done) | copy-start | bytes 12582916
  365.9 5.6 %copy-start.1 = (bf16[512,1,256]{2,0,1:T(8,128)(2,1)S(1)}, bf16[512,1,256]{2,0,1:T(8,128)(2,1)}, u32[]{:S(2)}) copy-start(bf16[512,1,256]{2,0,1:T(8,128)(2,1)} %param.15) | copy-start | bytes 786436
  (6 other events, 19.7 us)
Sparse Core Ops, SparseCore 0:
  10.6 122.6 all-gather.2
  135.7 102.5 all-gather.4
  248.3 108.2 all-reduce.2

commit v12 on v8

--- a/solution.py
+++ b/solution.py
@@ -124,7 +124,7 @@
     with_residual = (partial_sum + residual_rows).astype(jnp.bfloat16)
     hidden = lax.psum(with_residual, "head").astype(jnp.float32)
     unit = refusal / jnp.sqrt(jnp.sum(refusal * refusal) + 1e-06)
-    coef = jnp.dot(hidden, unit, precision=lax.Precision.HIGHEST)
+    coef = jnp.dot(hidden, unit, precision=lax.Precision.HIGH)
     stream_all = (hidden - coef[:, None] * unit[None, :]).astype(jnp.bfloat16)
     stream_float = stream_all.astype(jnp.float32)
     all_rows = (

time: 366 us -> 365 us (level)
  no operation moved by 1% of the time
where the time goes in v12:
time: 365 us; the launch traced here: 364 us
  waiting for transfers between devices  199 us (55%)
  starting transfers between devices  80.9 us (22%)
  matrix products  28.4 us (8%)
  local copies, waits for them, and re-layouts  24.7 us (7%)
  other arithmetic  16.3 us (4%)
  between operations  14.8 us (4%)
    psum x1, waiting for transfers between devices, body(): hidden = lax.psum(with_residual, 'head').astype(jnp.float32)  106 us
    ppermute x6, starting transfers between devices, shifted(): lax.ppermute(s.astype(jnp.bfloat16), axis, pairs).astype(jnp.float32)  67.8 us
    ppermute x5, waiting for transfers between devices, shifted(): lax.ppermute(a, axis, pairs)  42.3 us
    ppermute x6, waiting for transfers between devices, shifted(): lax.ppermute(s.astype(jnp.bfloat16), axis, pairs).astype(jnp.float32)  36.8 us
    ppermute x5, starting transfers between devices, shifted(): lax.ppermute(a, axis, pairs)  13 us
    all_gather x1, waiting for transfers between devices, body(): lax.all_gather(w_out, 'seq', axis=1, tiled=True)  12.6 us
    convert_element_type x2, local copies, waits for them, and re-layouts, body(): gate_z.reshape(block_count, SPAN, head_count, head_width)  8.72 us
  transfers between devices with their start and end apart: 14, of which 10 were waited for; matrix products, arithmetic and copies ran while one was open for 12% of the time, Pallas kernels for 0%

profile of v12, /device:TPU:1, one launch (start us, length us, event | category | flops | bytes accessed | tf_op | source)
XLA Modules:
  0.0 364.0 jit_solution(16059761605591196990)
XLA Ops:
  10.1 3.0 reshape.178
  26.5 6.3 %collective-permute-start.5 = (bf16[16,16384]{1,0:T(8,128)(2,1)S(1)}, bf16[16,16384]{1,0:T(8,128)(2,1)S(1)}, u32[]{:S(2)}, u32[]{:S(2)}) collective-permute-start(bf16[16,16384]{1,0:T(8,128)(2,1)S(1)} %add_convert_fusion), channel_id=1, source_target_pairs={{0,8},{8,16},{16,24},{24,32},{32,40},{40,48},{48,56},{56,64},{64,7... | collective-permute-start | bytes 1572872 | tf_op jit(solution)/shard_map/ppermute | solution.py:17
  32.9 15.5 %collective-permute-done.5 = bf16[16,16384]{1,0:T(8,128)(2,1)S(1)} collective-permute-done((bf16[16,16384]{1,0:T(8,128)(2,1)S(1)}, bf16[16,16384]{1,0:T(8,128)(2,1)S(1)}, u32[]{:S(2)}, u32[]{:S(2)}) %collective-permute-start.5) | collective-permute-done | bytes 524320 | tf_op jit(solution)/shard_map/ppermute | solution.py:17
  48.4 6.2 %collective-permute-start.6 = (bf16[16,16384]{1,0:T(8,128)(2,1)S(1)}, bf16[16,16384]{1,0:T(8,128)(2,1)S(1)}, u32[]{:S(2)}, u32[]{:S(2)}) collective-permute-start(bf16[16,16384]{1,0:T(8,128)(2,1)S(1)} %collective-permute-done.5), channel_id=1, source_target_pairs={{0,8},{8,16},{16,24},{24,32},{32,40},{40,48},{48,56},{56,64},{64,7... | collective-permute-start | bytes 1572872 | tf_op jit(solution)/shard_map/ppermute | solution.py:17
  54.6 2.5 collective-permute-start
  57.1 31.9 %collective-permute-done = f32[16]{0:T(128)S(1)} collective-permute-done((f32[16]{0:T(128)S(1)}, f32[16]{0:T(128)S(1)}, u32[]{:S(2)}, u32[]{:S(2)}) %collective-permute-start) | collective-permute-done | bytes 96 | tf_op jit(solution)/shard_map/ppermute | solution.py:16
  89.0 5.4 %collective-permute-start.1 = (f32[16]{0:T(128)S(1)}, f32[16]{0:T(128)S(1)}, u32[]{:S(2)}, u32[]{:S(2)}) collective-permute-start(f32[16]{0:T(128)S(1)} %collective-permute-done), channel_id=1, source_target_pairs={{0,8},{8,16},{16,24},{24,32},{32,40},{40,48},{48,56},{56,64},{64,7... | collective-permute-start | bytes 200 | tf_op jit(solution)/shard_map/ppermute | solution.py:16
  95.4 14.9 %collective-permute-start.7 = (bf16[16,16384]{1,0:T(8,128)(2,1)S(1)}, bf16[16,16384]{1,0:T(8,128)(2,1)S(1)}, u32[]{:S(2)}, u32[]{:S(2)}) collective-permute-start(bf16[16,16384]{1,0:T(8,128)(2,1)S(1)} %fusion.29), channel_id=1, source_target_pairs={{0,16},{8,24},{16,32},{24,40},{32,48},{40,56},{48,64},{56,72},{64,... | collective-permute-start | bytes 1572872 | tf_op jit(solution)/shard_map/ppermute | solution.py:17
  110.4 12.5 %collective-permute-done.7 = bf16[16,16384]{1,0:T(8,128)(2,1)S(1)} collective-permute-done((bf16[16,16384]{1,0:T(8,128)(2,1)S(1)}, bf16[16,16384]{1,0:T(8,128)(2,1)S(1)}, u32[]{:S(2)}, u32[]{:S(2)}) %collective-permute-start.7) | collective-permute-done | bytes 524320 | tf_op jit(solution)/shard_map/ppermute | solution.py:17
  123.2 8.5 %collective-permute-start.8 = (bf16[16,16384]{1,0:T(8,128)(2,1)S(1)}, bf16[16,16384]{1,0:T(8,128)(2,1)S(1)}, u32[]{:S(2)}, u32[]{:S(2)}) collective-permute-start(bf16[16,16384]{1,0:T(8,128)(2,1)S(1)} %fusion.37), channel_id=1, source_target_pairs={{0,32},{8,40},{16,48},{24,56},{32,64},{40,72},{48,80},{56,88},{64,... | collective-permute-start | bytes 1572872 | tf_op jit(solution)/shard_map/ppermute | solution.py:17
  134.1 8.4 %collective-permute-done.2 = f32[16]{0:T(128)S(1)} collective-permute-done((f32[16]{0:T(128)S(1)}, f32[16]{0:T(128)S(1)}, u32[]{:S(2)}, u32[]{:S(2)}) %collective-permute-start.2) | collective-permute-done | bytes 96 | tf_op jit(solution)/shard_map/ppermute | solution.py:16
  142.9 26.6 %collective-permute-start.9 = (bf16[16,16384]{1,0:T(8,128)(2,1)S(1)}, bf16[16,16384]{1,0:T(8,128)(2,1)S(1)}, u32[]{:S(2)}, u32[]{:S(2)}) collective-permute-start(bf16[16,16384]{1,0:T(8,128)(2,1)S(1)} %fusion.30), channel_id=1, source_target_pairs={{0,64},{8,72},{16,80},{24,88},{32,96},{40,104},{48,112},{56,120},{... | collective-permute-start | bytes 1572872 | tf_op jit(solution)/shard_map/ppermute | solution.py:17
  171.6 8.8 %collective-permute-done.9 = bf16[16,16384]{1,0:T(8,128)(2,1)S(1)} collective-permute-done((bf16[16,16384]{1,0:T(8,128)(2,1)S(1)}, bf16[16,16384]{1,0:T(8,128)(2,1)S(1)}, u32[]{:S(2)}, u32[]{:S(2)}) %collective-permute-start.9) | collective-permute-done | bytes 524320 | tf_op jit(solution)/shard_map/ppermute | solution.py:17
  181.7 5.3 %collective-permute-start.10 = (bf16[16,16384]{1,0:T(8,128)(2,1)}, bf16[16,16384]{1,0:T(8,128)(2,1)}, u32[]{:S(2)}, u32[]{:S(2)}) collective-permute-start(bf16[16,16384]{1,0:T(8,128)(2,1)} %fusion.36), channel_id=1, source_target_pairs={{0,128},{8,136},{16,144},{24,152},{32,160},{40,168},{48,176},{56,1... | collective-permute-start | bytes 1572872 | tf_op jit(solution)/shard_map/ppermute | solution.py:17
  187.1 4.1 %reshape.179 = f32[2,256,16,64]{3,2,1,0:T(8,128)} reshape(bf16[512,1024]{1,0:T(8,128)(2,1)} %param.13) | data formatting | bytes 3145728 | tf_op jit(solution)/shard_map/convert_element_type | solution.py:104
  191.2 4.6 %copy.44 = f32[2,256,16,64]{1,3,2,0:T(8,128)} copy(f32[2,256,16,64]{3,2,1,0:T(8,128)} %reshape.179) | data formatting | bytes 4194304 | tf_op jit(solution)/shard_map/convert_element_type | solution.py:104
  202.2 5.3 %fusion.19 = f32[2,16,64,256]{3,2,1,0:T(8,128)S(1)} fusion(bf16[2,256,256]{2,1,0:T(8,128)(2,1)S(1)} %bitcast.60, f32[1,16,256,64]{2,3,1,0:T(8,128)} %get-tuple-element.19, f32[16,256,64]{1,2,0:T(8,128)S(1)} %copy.40, f32[2,16]{1,0:T(2,128)S(1)} %subtract_exponential_fusion), kind=kOutput, calls=%fused_computation.26 | convolution fusion | flops 1611661312 | bytes 4456576 | tf_op jit(solution)/shard_map/klhn,khnp->klhp/dot_general | solution.py:100
  207.5 3.0 multiply_reduce_fusion
  212.8 12.6 %all-gather.5.cloned.1.call-done = bf16[1024,4096]{1,0:T(8,128)(2,1)} async-done(((bf16[1024,128]{1,0:T(8,128)(2,1)}), bf16[1024,4096]{1,0:T(8,128)(2,1)}) %all-gather.5.cloned.1.call-update) | async-done | bytes 8388624 | tf_op jit(solution)/shard_map/all_gather | solution.py:121
  225.4 7.1 %fusion.43 = f32[512,4096]{1,0:T(8,128)S(1)} fusion(bf16[512,1024]{0,1:T(8,128)(2,1)S(1)} %multiply_convert_fusion.4, bf16[1024,4096]{1,0:T(8,128)(2,1)} %all-gather.5.cloned.1.call-done), kind=kOutput, calls=%fused_computation.75 | convolution fusion | flops 4294967296 | bytes 17825792 | tf_op jit(solution)/shard_map/dot_general | solution.py:119
  232.7 2.6 convert_element_type.97
  237.3 106.3 %all-reduce.3.cloned.1.call-done = bf16[512,4096]{1,0:T(8,128)(2,1)} async-done(((bf16[512,4096]{1,0:T(8,128)(2,1)}), bf16[512,4096]{1,0:T(8,128)(2,1)}) %all-reduce.3.cloned.1.call-update) | async-done | bytes 4194320 | tf_op jit(solution)/shard_map/psum | solution.py:125
  343.6 4.6 %fusion.44 = f32[1,512]{1,0:T(1,128)S(1)} fusion(bf16[512,4096]{1,0:T(8,128)(2,1)} %all-reduce.3.cloned.1.call-done, f32[4096,1]{0,1:T(1,128)S(1)} %bitcast.65), kind=kOutput, calls=%fused_computation.76 | convolution fusion | flops 12582912 | bytes 4212736 | tf_op jit(solution)/shard_map/dot_general | solution.py:127
  351.8 5.6 %fusion.24 = bf16[512,1024]{1,0:T(8,128)(2,1)} fusion(bf16[4096,1024]{1,0:T(8,128)(2,1)S(1)} %copy-done.13, bf16[512,4096]{1,0:T(8,128)(2,1)S(1)} %get-tuple-element.11, f32[4096]{0:T(1024)S(1)} %copy-done.14, f32[512]{0:T(512)S(1)} %add_rsqrt_fusion), kind=kOutput, calls=%fused_computation.31 | convolution fusion | flops 4303880192 | bytes 13649920 | tf_op jit(solution)/shard_map/dot_general | solution.py:136
  (92 shorter events, 37.3 us)
Async XLA Ops:
  7.2 188.6 %copy-start = (bf16[512,1,256]{2,0,1:T(8,128)(2,1)S(1)}, bf16[512,1,256]{2,0,1:T(8,128)(2,1)}, u32[]{:S(2)}) copy-start(bf16[512,1,256]{2,0,1:T(8,128)(2,1)} %param.15) | copy-start | bytes 786436
  7.2 205.6 %all-gather.3.cloned.1.call-start = ((), (), s32[]{:S(2)}) async-start(), calls=%async_computation | async-start | bytes 8650752 | tf_op jit(solution)/shard_map/all_gather | solution.py:109
  7.9 217.4 %all-gather.5.cloned.1.call-start = ((), (), s32[]{:S(2)}) async-start(), calls=%async_computation.1 | async-start | bytes 8650752 | tf_op jit(solution)/shard_map/all_gather | solution.py:121
  14.7 5.6 %copy-start.5 = (bf16[2,256,16,64]{1,3,2,0:T(8,128)(2,1)}, bf16[2,256,16,64]{1,3,2,0:T(8,128)(2,1)S(1)}, u32[]{:S(2)}) copy-start(bf16[2,256,16,64]{1,3,2,0:T(8,128)(2,1)S(1)} %copy.36) | copy-start | bytes 3145732
  26.5 21.8 %collective-permute-start.5 = (bf16[16,16384]{1,0:T(8,128)(2,1)S(1)}, bf16[16,16384]{1,0:T(8,128)(2,1)S(1)}, u32[]{:S(2)}, u32[]{:S(2)}) collective-permute-start(bf16[16,16384]{1,0:T(8,128)(2,1)S(1)} %add_convert_fusion), channel_id=1, source_target_pairs={{0,8},{8,16},{16,24},{24,32},{32,40},{40,48},{48,56},{56,64},{64,7... | collective-permute-start | bytes 1572872 | tf_op jit(solution)/shard_map/ppermute | solution.py:17
  48.4 46.8 %collective-permute-start.6 = (bf16[16,16384]{1,0:T(8,128)(2,1)S(1)}, bf16[16,16384]{1,0:T(8,128)(2,1)S(1)}, u32[]{:S(2)}, u32[]{:S(2)}) collective-permute-start(bf16[16,16384]{1,0:T(8,128)(2,1)S(1)} %collective-permute-done.5), channel_id=1, source_target_pairs={{0,8},{8,16},{16,24},{24,32},{32,40},{40,48},{48,56},{56,64},{64,7... | collective-permute-start | bytes 1572872 | tf_op jit(solution)/shard_map/ppermute | solution.py:17
  54.6 34.5 %collective-permute-start = (f32[16]{0:T(128)S(1)}, f32[16]{0:T(128)S(1)}, u32[]{:S(2)}, u32[]{:S(2)}) collective-permute-start(f32[16]{0:T(128)S(1)} %get-tuple-element.6), channel_id=1, source_target_pairs={{0,8},{8,16},{16,24},{24,32},{32,40},{40,48},{48,56},{56,64},{64,7... | collective-permute-start | bytes 200 | tf_op jit(solution)/shard_map/ppermute | solution.py:16
  89.0 6.1 %collective-permute-start.1 = (f32[16]{0:T(128)S(1)}, f32[16]{0:T(128)S(1)}, u32[]{:S(2)}, u32[]{:S(2)}) collective-permute-start(f32[16]{0:T(128)S(1)} %collective-permute-done), channel_id=1, source_target_pairs={{0,8},{8,16},{16,24},{24,32},{32,40},{40,48},{48,56},{56,64},{64,7... | collective-permute-start | bytes 200 | tf_op jit(solution)/shard_map/ppermute | solution.py:16
  95.4 27.5 %collective-permute-start.7 = (bf16[16,16384]{1,0:T(8,128)(2,1)S(1)}, bf16[16,16384]{1,0:T(8,128)(2,1)S(1)}, u32[]{:S(2)}, u32[]{:S(2)}) collective-permute-start(bf16[16,16384]{1,0:T(8,128)(2,1)S(1)} %fusion.29), channel_id=1, source_target_pairs={{0,16},{8,24},{16,32},{24,40},{32,48},{40,56},{48,64},{56,72},{64,... | collective-permute-start | bytes 1572872 | tf_op jit(solution)/shard_map/ppermute | solution.py:17
  110.3 233.3 %all-reduce.3.cloned.1.call-start = ((), (), s32[]{:S(2)}) async-start(), calls=%async_computation.2 | async-start | bytes 8388608 | tf_op jit(solution)/shard_map/psum | solution.py:125
  123.2 19.3 %collective-permute-start.8 = (bf16[16,16384]{1,0:T(8,128)(2,1)S(1)}, bf16[16,16384]{1,0:T(8,128)(2,1)S(1)}, u32[]{:S(2)}, u32[]{:S(2)}) collective-permute-start(bf16[16,16384]{1,0:T(8,128)(2,1)S(1)} %fusion.37), channel_id=1, source_target_pairs={{0,32},{8,40},{16,48},{24,56},{32,64},{40,72},{48,80},{56,88},{64,... | collective-permute-start | bytes 1572872 | tf_op jit(solution)/shard_map/ppermute | solution.py:17
  131.8 10.7 %collective-permute-start.2 = (f32[16]{0:T(128)S(1)}, f32[16]{0:T(128)S(1)}, u32[]{:S(2)}, u32[]{:S(2)}) collective-permute-start(f32[16]{0:T(128)S(1)} %get-tuple-element.17), channel_id=1, source_target_pairs={{0,16},{8,24},{16,32},{24,40},{32,48},{40,56},{48,64},{56,72},{64,... | collective-permute-start | bytes 200 | tf_op jit(solution)/shard_map/ppermute | solution.py:16
  142.9 37.5 %collective-permute-start.9 = (bf16[16,16384]{1,0:T(8,128)(2,1)S(1)}, bf16[16,16384]{1,0:T(8,128)(2,1)S(1)}, u32[]{:S(2)}, u32[]{:S(2)}) collective-permute-start(bf16[16,16384]{1,0:T(8,128)(2,1)S(1)} %fusion.30), channel_id=1, source_target_pairs={{0,64},{8,72},{16,80},{24,88},{32,96},{40,104},{48,112},{56,120},{... | collective-permute-start | bytes 1572872 | tf_op jit(solution)/shard_map/ppermute | solution.py:17
  169.6 2.0 collective-permute-start.3
  180.4 10.8 %copy-start.4 = (bf16[16,16384]{1,0:T(8,128)(2,1)}, bf16[16,16384]{1,0:T(8,128)(2,1)S(1)}, u32[]{:S(2)}) copy-start(bf16[16,16384]{1,0:T(8,128)(2,1)S(1)} %collective-permute-done.9) | copy-start | bytes 1572868
  181.7 17.1 %collective-permute-start.10 = (bf16[16,16384]{1,0:T(8,128)(2,1)}, bf16[16,16384]{1,0:T(8,128)(2,1)}, u32[]{:S(2)}, u32[]{:S(2)}) collective-permute-start(bf16[16,16384]{1,0:T(8,128)(2,1)} %fusion.36), channel_id=1, source_target_pairs={{0,128},{8,136},{16,144},{24,152},{32,160},{40,168},{48,176},{56,1... | collective-permute-start | bytes 1572872 | tf_op jit(solution)/shard_map/ppermute | solution.py:17
  196.9 2.0 collective-permute-start.4
  201.5 6.0 %copy-start.11 = (f32[2,256,16]{1,2,0:T(8,128)S(1)}, f32[2,256,16]{1,2,0:T(8,128)}, u32[]{:S(2)}) copy-start(f32[2,256,16]{1,2,0:T(8,128)} %get-tuple-element.21) | copy-start | bytes 98308
  201.5 6.0 %copy-start.15 = (f32[16]{0:T(128)S(1)}, f32[16]{0:T(128)}, u32[]{:S(2)}) copy-start(f32[16]{0:T(128)} %param.17) | copy-start | bytes 196
  202.1 5.4 %copy-start.3 = (f32[2,256,16,64]{1,3,2,0:T(8,128)S(1)}, f32[2,256,16,64]{1,3,2,0:T(8,128)}, u32[]{:S(2)}) copy-start(f32[2,256,16,64]{1,3,2,0:T(8,128)} %copy.44) | copy-start | bytes 6291460
  202.1 5.4 %copy-start.6 = (bf16[2,256,16,64]{1,3,2,0:T(8,128)(2,1)S(1)}, bf16[2,256,16,64]{1,3,2,0:T(8,128)(2,1)}, u32[]{:S(2)}) copy-start(bf16[2,256,16,64]{1,3,2,0:T(8,128)(2,1)} %copy-done.5) | copy-start | bytes 3145732
  202.1 5.4 %copy-start.8 = (f32[2,256,256]{2,1,0:T(8,128)S(1)}, f32[2,256,256]{2,1,0:T(8,128)}, u32[]{:S(2)}) copy-start(f32[2,256,256]{2,1,0:T(8,128)} %fusion.42) | copy-start | bytes 1572868
  212.7 19.8 %copy-start.9 = (bf16[64,4096]{1,0:T(8,128)(2,1)S(1)}, bf16[64,4096]{1,0:T(8,128)(2,1)}, u32[]{:S(2)}) copy-start(bf16[64,4096]{1,0:T(8,128)(2,1)} %param.20) | copy-start | bytes 1572868
  351.8 5.6 %copy-start.1 = (bf16[512,1,256]{2,0,1:T(8,128)(2,1)S(1)}, bf16[512,1,256]{2,0,1:T(8,128)(2,1)}, u32[]{:S(2)}) copy-start(bf16[512,1,256]{2,0,1:T(8,128)(2,1)} %param.15) | copy-start | bytes 786436
  (6 other events, 19.0 us)
Sparse Core Ops, SparseCore 0:
  10.6 103.8 all-gather.2
  116.9 108.4 all-gather.4
  235.4 108.1 all-reduce.2

commit v13 on v12

--- a/solution.py
+++ b/solution.py
@@ -110,12 +110,11 @@
     ssd_out, w_in_all = lax.optimization_barrier((ssd_out, w_in_all))
     own_rows = residual.shape[0]
     mine = lax.axis_index("head")
-    residual_rows = lax.dynamic_update_slice_in_dim(
-        jnp.zeros((seq_rows, residual.shape[1]), jnp.float32),
-        residual.astype(jnp.float32),
-        mine * own_rows,
-        axis=0,
-    )
+    head_devices = seq_rows // own_rows
+    in_block = lax.broadcasted_iota(jnp.int32, (head_devices, 1, 1), 0) == mine
+    residual_rows = jnp.where(
+        in_block, residual.astype(jnp.float32)[None], 0.0
+    ).reshape(seq_rows, residual.shape[1])
     partial_sum = jnp.dot(
         ssd_out,
         lax.all_gather(w_out, "seq", axis=1, tiled=True),

time: 365 us -> 364 us (level)
  waiting for transfers between devices: 199 us -> 192 us
    ppermute x6, waiting for transfers between devices: 36.8 us -> 29.4 us  [shifted(): lax.ppermute(s.astype(jnp.bfloat16), axis, pairs).astype(jnp.float32)]
    ppermute x5, starting transfers between devices: 13 us -> 20 us  [shifted(): lax.ppermute(a, axis, pairs)]
    ppermute x5, waiting for transfers between devices: 42.3 us -> 47 us  [shifted(): lax.ppermute(a, axis, pairs)]
    ppermute x6, starting transfers between devices: 67.8 us -> 63.3 us  [shifted(): lax.ppermute(s.astype(jnp.bfloat16), axis, pairs).astype(jnp.float32)]
    all_gather x1, waiting for transfers between devices: 12.6 us -> 8.23 us  [body(): lax.all_gather(w_out, 'seq', axis=1, tiled=True)]
  transfers between devices with their start and end apart: 14 -> 14, of which waited for: 10 -> 9; matrix products, arithmetic and copies ran while one was open for 12% -> 14% of each run, Pallas kernels for 0% -> 0%
where the time goes in v13:
time: 364 us
  waiting for transfers between devices  192 us (53%)
  starting transfers between devices  83.4 us (23%)
  matrix products  31 us (9%)
  local copies, waits for them, and re-layouts  26.1 us (7%)
  other arithmetic  16.6 us (5%)
  between operations  14.8 us (4%)
    psum x1, waiting for transfers between devices, body(): hidden = lax.psum(with_residual, 'head').astype(jnp.float32)  106 us
    ppermute x6, starting transfers between devices, shifted(): lax.ppermute(s.astype(jnp.bfloat16), axis, pairs).astype(jnp.float32)  63.3 us
    ppermute x5, waiting for transfers between devices, shifted(): lax.ppermute(a, axis, pairs)  47 us
    ppermute x6, waiting for transfers between devices, shifted(): lax.ppermute(s.astype(jnp.bfloat16), axis, pairs).astype(jnp.float32)  29.4 us
    ppermute x5, starting transfers between devices, shifted(): lax.ppermute(a, axis, pairs)  20 us
    dot_general x1, matrix products, body(): jnp.dot(ssd_out, lax.all_gather(w_out, 'seq', axis=1, tiled=True), prefer...  9.75 us
    convert_element_type x2, local copies, waits for them, and re-layouts, body(): gate_z.reshape(block_count, SPAN, head_count, head_width)  8.7 us
    all_gather x1, waiting for transfers between devices, body(): lax.all_gather(w_out, 'seq', axis=1, tiled=True)  8.23 us
  transfers between devices with their start and end apart: 14, of which 9 were waited for; matrix products, arithmetic and copies ran while one was open for 14% of the time, Pallas kernels for 0%

profile of v13, /device:TPU:1, one launch (start us, length us, event | category | flops | bytes accessed | tf_op | source)
XLA Modules:
  0.0 363.6 jit_solution(14837152535283461224)
XLA Ops:
  10.1 3.0 reshape.187
  26.6 6.3 %collective-permute-start.5 = (bf16[16,16384]{1,0:T(8,128)(2,1)S(1)}, bf16[16,16384]{1,0:T(8,128)(2,1)S(1)}, u32[]{:S(2)}, u32[]{:S(2)}) collective-permute-start(bf16[16,16384]{1,0:T(8,128)(2,1)S(1)} %add_convert_fusion), channel_id=1, source_target_pairs={{0,8},{8,16},{16,24},{24,32},{32,40},{40,48},{48,56},{56,64},{64,7... | collective-permute-start | bytes 1572872 | tf_op jit(solution)/shard_map/ppermute | solution.py:17
  32.9 15.5 %collective-permute-done.5 = bf16[16,16384]{1,0:T(8,128)(2,1)S(1)} collective-permute-done((bf16[16,16384]{1,0:T(8,128)(2,1)S(1)}, bf16[16,16384]{1,0:T(8,128)(2,1)S(1)}, u32[]{:S(2)}, u32[]{:S(2)}) %collective-permute-start.5) | collective-permute-done | bytes 524320 | tf_op jit(solution)/shard_map/ppermute | solution.py:17
  48.4 6.1 %collective-permute-start.6 = (bf16[16,16384]{1,0:T(8,128)(2,1)S(1)}, bf16[16,16384]{1,0:T(8,128)(2,1)S(1)}, u32[]{:S(2)}, u32[]{:S(2)}) collective-permute-start(bf16[16,16384]{1,0:T(8,128)(2,1)S(1)} %collective-permute-done.5), channel_id=1, source_target_pairs={{0,8},{8,16},{16,24},{24,32},{32,40},{40,48},{48,56},{56,64},{64,7... | collective-permute-start | bytes 1572872 | tf_op jit(solution)/shard_map/ppermute | solution.py:17
  54.5 2.5 collective-permute-start
  57.1 20.6 %collective-permute-done = f32[16]{0:T(128)S(1)} collective-permute-done((f32[16]{0:T(128)S(1)}, f32[16]{0:T(128)S(1)}, u32[]{:S(2)}, u32[]{:S(2)}) %collective-permute-start) | collective-permute-done | bytes 96 | tf_op jit(solution)/shard_map/ppermute | solution.py:16
  77.7 5.7 %collective-permute-start.1 = (f32[16]{0:T(128)S(1)}, f32[16]{0:T(128)S(1)}, u32[]{:S(2)}, u32[]{:S(2)}) collective-permute-start(f32[16]{0:T(128)S(1)} %collective-permute-done), channel_id=1, source_target_pairs={{0,8},{8,16},{16,24},{24,32},{32,40},{40,48},{48,56},{56,64},{64,7... | collective-permute-start | bytes 200 | tf_op jit(solution)/shard_map/ppermute | solution.py:16
  84.3 23.8 %collective-permute-start.7 = (bf16[16,16384]{1,0:T(8,128)(2,1)S(1)}, bf16[16,16384]{1,0:T(8,128)(2,1)S(1)}, u32[]{:S(2)}, u32[]{:S(2)}) collective-permute-start(bf16[16,16384]{1,0:T(8,128)(2,1)S(1)} %fusion.31), channel_id=1, source_target_pairs={{0,16},{8,24},{16,32},{24,40},{32,48},{40,56},{48,64},{56,72},{64,... | collective-permute-start | bytes 1572872 | tf_op jit(solution)/shard_map/ppermute | solution.py:17
  108.2 13.9 %collective-permute-done.7 = bf16[16,16384]{1,0:T(8,128)(2,1)S(1)} collective-permute-done((bf16[16,16384]{1,0:T(8,128)(2,1)S(1)}, bf16[16,16384]{1,0:T(8,128)(2,1)S(1)}, u32[]{:S(2)}, u32[]{:S(2)}) %collective-permute-start.7) | collective-permute-done | bytes 524320 | tf_op jit(solution)/shard_map/ppermute | solution.py:17
  122.5 10.4 %collective-permute-start.8 = (bf16[16,16384]{1,0:T(8,128)(2,1)S(1)}, bf16[16,16384]{1,0:T(8,128)(2,1)S(1)}, u32[]{:S(2)}, u32[]{:S(2)}) collective-permute-start(bf16[16,16384]{1,0:T(8,128)(2,1)S(1)} %fusion.39), channel_id=1, source_target_pairs={{0,32},{8,40},{16,48},{24,56},{32,64},{40,72},{48,80},{56,88},{64,... | collective-permute-start | bytes 1572872 | tf_op jit(solution)/shard_map/ppermute | solution.py:17
  135.0 24.5 %collective-permute-done.2 = f32[16]{0:T(128)S(1)} collective-permute-done((f32[16]{0:T(128)S(1)}, f32[16]{0:T(128)S(1)}, u32[]{:S(2)}, u32[]{:S(2)}) %collective-permute-start.2) | collective-permute-done | bytes 96 | tf_op jit(solution)/shard_map/ppermute | solution.py:16
  161.5 8.3 %collective-permute-start.3 = (f32[16]{0:T(128)S(1)}, f32[16]{0:T(128)S(1)}, u32[]{:S(2)}, u32[]{:S(2)}) collective-permute-start(f32[16]{0:T(128)S(1)} %get-tuple-element.15), channel_id=1, source_target_pairs={{0,32},{8,40},{16,48},{24,56},{32,64},{40,72},{48,80},{56,88},{64,... | collective-permute-start | bytes 200 | tf_op jit(solution)/shard_map/ppermute | solution.py:16
  171.9 15.1 %collective-permute-start.10 = (bf16[16,16384]{1,0:T(8,128)(2,1)}, bf16[16,16384]{1,0:T(8,128)(2,1)}, u32[]{:S(2)}, u32[]{:S(2)}) collective-permute-start(bf16[16,16384]{1,0:T(8,128)(2,1)} %fusion.38), channel_id=1, source_target_pairs={{0,128},{8,136},{16,144},{24,152},{32,160},{40,168},{48,176},{56,1... | collective-permute-start | bytes 1572872 | tf_op jit(solution)/shard_map/ppermute | solution.py:17
  186.9 4.1 %reshape.188 = f32[2,256,16,64]{3,2,1,0:T(8,128)} reshape(bf16[512,1024]{1,0:T(8,128)(2,1)} %param.13) | data formatting | bytes 3145728 | tf_op jit(solution)/shard_map/convert_element_type | solution.py:104
  191.0 4.6 %copy.44 = f32[2,256,16,64]{1,3,2,0:T(8,128)} copy(f32[2,256,16,64]{3,2,1,0:T(8,128)} %reshape.188) | data formatting | bytes 4194304 | tf_op jit(solution)/shard_map/convert_element_type | solution.py:104
  198.3 2.1 convert_element_type.96
  200.9 2.7 multiply_add_fusion
  206.3 5.3 %fusion.21 = f32[2,16,64,256]{3,2,1,0:T(8,128)S(1)} fusion(bf16[2,256,256]{2,1,0:T(8,128)(2,1)S(1)} %bitcast.66, f32[1,16,256,64]{2,3,1,0:T(8,128)} %get-tuple-element.19, f32[16,256,64]{1,2,0:T(8,128)S(1)} %copy.40, f32[2,16]{1,0:T(2,128)S(1)} %subtract_exponential_fusion), kind=kOutput, calls=%fused_computation.29 | convolution fusion | flops 1611661312 | bytes 4456576 | tf_op jit(solution)/shard_map/klhn,khnp->klhp/dot_general | solution.py:100
  211.7 3.1 multiply_reduce_fusion
  216.9 8.2 %all-gather.5.cloned.1.call-done = bf16[1024,4096]{1,0:T(8,128)(2,1)} async-done(((bf16[1024,128]{1,0:T(8,128)(2,1)}), bf16[1024,4096]{1,0:T(8,128)(2,1)}) %all-gather.5.cloned.1.call-update) | async-done | bytes 8388624 | tf_op jit(solution)/shard_map/all_gather | solution.py:120
  225.2 9.7 %fusion.4 = bf16[512,4096]{1,0:T(8,128)(2,1)} fusion(bf16[512,1024]{0,1:T(8,128)(2,1)S(1)} %multiply_convert_fusion.4, bf16[1024,4096]{1,0:T(8,128)(2,1)} %all-gather.5.cloned.1.call-done, f32[64,4096]{1,0:T(8,128)S(1)} %copy-done.6, pred[512]{0:T(512)(128)(4,1)S(1)} %broadcast_in_dim.63), kind=kOutput, calls=%fused_computation.7 | convolution fusion | flops 4301258752 | bytes 14680576 | tf_op jit(solution)/shard_map/dot_general | solution.py:118
  236.9 106.3 %all-reduce.3.cloned.1.call-done = bf16[512,4096]{1,0:T(8,128)(2,1)} async-done(((bf16[512,4096]{1,0:T(8,128)(2,1)}), bf16[512,4096]{1,0:T(8,128)(2,1)}) %all-reduce.3.cloned.1.call-update) | async-done | bytes 4194320 | tf_op jit(solution)/shard_map/psum | solution.py:124
  343.3 4.6 %fusion.45 = f32[1,512]{1,0:T(1,128)S(1)} fusion(bf16[512,4096]{1,0:T(8,128)(2,1)} %all-reduce.3.cloned.1.call-done, f32[4096,1]{0,1:T(1,128)S(1)} %bitcast.71), kind=kOutput, calls=%fused_computation.78 | convolution fusion | flops 12582912 | bytes 4212736 | tf_op jit(solution)/shard_map/dot_general | solution.py:126
  351.5 5.6 %fusion.26 = bf16[512,1024]{1,0:T(8,128)(2,1)} fusion(bf16[4096,1024]{1,0:T(8,128)(2,1)S(1)} %copy-done.12, bf16[512,4096]{1,0:T(8,128)(2,1)S(1)} %get-tuple-element.11, f32[4096]{0:T(1024)S(1)} %copy-done.13, f32[512]{0:T(512)S(1)} %add_rsqrt_fusion), kind=kOutput, calls=%fused_computation.34 | convolution fusion | flops 4303880192 | bytes 13649920 | tf_op jit(solution)/shard_map/dot_general | solution.py:135
  (92 shorter events, 36.6 us)
Async XLA Ops:
  7.2 188.6 %copy-start = (bf16[512,1,256]{2,0,1:T(8,128)(2,1)S(1)}, bf16[512,1,256]{2,0,1:T(8,128)(2,1)}, u32[]{:S(2)}) copy-start(bf16[512,1,256]{2,0,1:T(8,128)(2,1)} %param.15) | copy-start | bytes 786436
  7.2 209.7 %all-gather.3.cloned.1.call-start = ((), (), s32[]{:S(2)}) async-start(), calls=%async_computation | async-start | bytes 8650752 | tf_op jit(solution)/shard_map/all_gather | solution.py:109
  7.9 217.2 %all-gather.5.cloned.1.call-start = ((), (), s32[]{:S(2)}) async-start(), calls=%async_computation.1 | async-start | bytes 8650752 | tf_op jit(solution)/shard_map/all_gather | solution.py:120
  14.7 5.6 %copy-start.4 = (bf16[2,256,16,64]{1,3,2,0:T(8,128)(2,1)}, bf16[2,256,16,64]{1,3,2,0:T(8,128)(2,1)S(1)}, u32[]{:S(2)}) copy-start(bf16[2,256,16,64]{1,3,2,0:T(8,128)(2,1)S(1)} %copy.36) | copy-start | bytes 3145732
  26.6 21.8 %collective-permute-start.5 = (bf16[16,16384]{1,0:T(8,128)(2,1)S(1)}, bf16[16,16384]{1,0:T(8,128)(2,1)S(1)}, u32[]{:S(2)}, u32[]{:S(2)}) collective-permute-start(bf16[16,16384]{1,0:T(8,128)(2,1)S(1)} %add_convert_fusion), channel_id=1, source_target_pairs={{0,8},{8,16},{16,24},{24,32},{32,40},{40,48},{48,56},{56,64},{64,7... | collective-permute-start | bytes 1572872 | tf_op jit(solution)/shard_map/ppermute | solution.py:17
  48.4 35.7 %collective-permute-start.6 = (bf16[16,16384]{1,0:T(8,128)(2,1)S(1)}, bf16[16,16384]{1,0:T(8,128)(2,1)S(1)}, u32[]{:S(2)}, u32[]{:S(2)}) collective-permute-start(bf16[16,16384]{1,0:T(8,128)(2,1)S(1)} %collective-permute-done.5), channel_id=1, source_target_pairs={{0,8},{8,16},{16,24},{24,32},{32,40},{40,48},{48,56},{56,64},{64,7... | collective-permute-start | bytes 1572872 | tf_op jit(solution)/shard_map/ppermute | solution.py:17
  54.5 23.2 %collective-permute-start = (f32[16]{0:T(128)S(1)}, f32[16]{0:T(128)S(1)}, u32[]{:S(2)}, u32[]{:S(2)}) collective-permute-start(f32[16]{0:T(128)S(1)} %get-tuple-element.6), channel_id=1, source_target_pairs={{0,8},{8,16},{16,24},{24,32},{32,40},{40,48},{48,56},{56,64},{64,7... | collective-permute-start | bytes 200 | tf_op jit(solution)/shard_map/ppermute | solution.py:16
  77.7 6.4 %collective-permute-start.1 = (f32[16]{0:T(128)S(1)}, f32[16]{0:T(128)S(1)}, u32[]{:S(2)}, u32[]{:S(2)}) collective-permute-start(f32[16]{0:T(128)S(1)} %collective-permute-done), channel_id=1, source_target_pairs={{0,8},{8,16},{16,24},{24,32},{32,40},{40,48},{48,56},{56,64},{64,7... | collective-permute-start | bytes 200 | tf_op jit(solution)/shard_map/ppermute | solution.py:16
  84.3 37.8 %collective-permute-start.7 = (bf16[16,16384]{1,0:T(8,128)(2,1)S(1)}, bf16[16,16384]{1,0:T(8,128)(2,1)S(1)}, u32[]{:S(2)}, u32[]{:S(2)}) collective-permute-start(bf16[16,16384]{1,0:T(8,128)(2,1)S(1)} %fusion.31), channel_id=1, source_target_pairs={{0,16},{8,24},{16,32},{24,40},{32,48},{40,56},{48,64},{56,72},{64,... | collective-permute-start | bytes 1572872 | tf_op jit(solution)/shard_map/ppermute | solution.py:17
  108.2 235.1 %all-reduce.3.cloned.1.call-start = ((), (), s32[]{:S(2)}) async-start(), calls=%async_computation.2 | async-start | bytes 8388608 | tf_op jit(solution)/shard_map/psum | solution.py:124
  122.5 37.0 %collective-permute-start.8 = (bf16[16,16384]{1,0:T(8,128)(2,1)S(1)}, bf16[16,16384]{1,0:T(8,128)(2,1)S(1)}, u32[]{:S(2)}, u32[]{:S(2)}) collective-permute-start(bf16[16,16384]{1,0:T(8,128)(2,1)S(1)} %fusion.39), channel_id=1, source_target_pairs={{0,32},{8,40},{16,48},{24,56},{32,64},{40,72},{48,80},{56,88},{64,... | collective-permute-start | bytes 1572872 | tf_op jit(solution)/shard_map/ppermute | solution.py:17
  133.0 26.5 %collective-permute-start.2 = (f32[16]{0:T(128)S(1)}, f32[16]{0:T(128)S(1)}, u32[]{:S(2)}, u32[]{:S(2)}) collective-permute-start(f32[16]{0:T(128)S(1)} %get-tuple-element.17), channel_id=1, source_target_pairs={{0,16},{8,24},{16,32},{24,40},{32,48},{40,56},{48,64},{56,72},{64,... | collective-permute-start | bytes 200 | tf_op jit(solution)/shard_map/ppermute | solution.py:16
  160.0 10.6 %collective-permute-start.9 = (bf16[16,16384]{1,0:T(8,128)(2,1)S(1)}, bf16[16,16384]{1,0:T(8,128)(2,1)S(1)}, u32[]{:S(2)}, u32[]{:S(2)}) collective-permute-start(bf16[16,16384]{1,0:T(8,128)(2,1)S(1)} %fusion.32), channel_id=1, source_target_pairs={{0,64},{8,72},{16,80},{24,88},{32,96},{40,104},{48,112},{56,120},{... | collective-permute-start | bytes 1572872 | tf_op jit(solution)/shard_map/ppermute | solution.py:17
  161.5 9.0 %collective-permute-start.3 = (f32[16]{0:T(128)S(1)}, f32[16]{0:T(128)S(1)}, u32[]{:S(2)}, u32[]{:S(2)}) collective-permute-start(f32[16]{0:T(128)S(1)} %get-tuple-element.15), channel_id=1, source_target_pairs={{0,32},{8,40},{16,48},{24,56},{32,64},{40,72},{48,80},{56,88},{64,... | collective-permute-start | bytes 200 | tf_op jit(solution)/shard_map/ppermute | solution.py:16
  171.9 29.1 %collective-permute-start.10 = (bf16[16,16384]{1,0:T(8,128)(2,1)}, bf16[16,16384]{1,0:T(8,128)(2,1)}, u32[]{:S(2)}, u32[]{:S(2)}) collective-permute-start(bf16[16,16384]{1,0:T(8,128)(2,1)} %fusion.38), channel_id=1, source_target_pairs={{0,128},{8,136},{16,144},{24,152},{32,160},{40,168},{48,176},{56,1... | collective-permute-start | bytes 1572872 | tf_op jit(solution)/shard_map/ppermute | solution.py:17
  191.0 4.8 %copy-start.7 = (bf16[512,1,256]{2,0,1:T(8,128)(2,1)S(1)}, bf16[512,1,256]{2,0,1:T(8,128)(2,1)}, u32[]{:S(2)}) copy-start(bf16[512,1,256]{2,0,1:T(8,128)(2,1)} %param.14) | copy-start | bytes 786436
  196.9 4.1 %collective-permute-start.4 = (f32[16]{0:T(128)S(1)}, f32[16]{0:T(128)S(1)}, u32[]{:S(2)}, u32[]{:S(2)}) collective-permute-start(f32[16]{0:T(128)S(1)} %get-tuple-element.13), channel_id=1, source_target_pairs={{0,64},{8,72},{16,80},{24,88},{32,96},{40,104},{48,112},{56,120},{... | collective-permute-start | bytes 200 | tf_op jit(solution)/shard_map/ppermute | solution.py:16
  205.7 6.0 %copy-start.10 = (f32[2,256,16]{1,2,0:T(8,128)S(1)}, f32[2,256,16]{1,2,0:T(8,128)}, u32[]{:S(2)}) copy-start(f32[2,256,16]{1,2,0:T(8,128)} %get-tuple-element.21) | copy-start | bytes 98308
  205.7 6.0 %copy-start.14 = (f32[16]{0:T(128)S(1)}, f32[16]{0:T(128)}, u32[]{:S(2)}) copy-start(f32[16]{0:T(128)} %param.17) | copy-start | bytes 196
  206.3 5.4 %copy-start.3 = (f32[2,256,16,64]{1,3,2,0:T(8,128)S(1)}, f32[2,256,16,64]{1,3,2,0:T(8,128)}, u32[]{:S(2)}) copy-start(f32[2,256,16,64]{1,3,2,0:T(8,128)} %copy.44) | copy-start | bytes 6291460
  206.3 5.4 %copy-start.5 = (bf16[2,256,16,64]{1,3,2,0:T(8,128)(2,1)S(1)}, bf16[2,256,16,64]{1,3,2,0:T(8,128)(2,1)}, u32[]{:S(2)}) copy-start(bf16[2,256,16,64]{1,3,2,0:T(8,128)(2,1)} %copy-done.4) | copy-start | bytes 3145732
  206.3 5.4 %copy-start.8 = (f32[2,256,256]{2,1,0:T(8,128)S(1)}, f32[2,256,256]{2,1,0:T(8,128)}, u32[]{:S(2)}) copy-start(f32[2,256,256]{2,1,0:T(8,128)} %fusion.44) | copy-start | bytes 1572868
  216.4 8.8 %copy-start.6 = (f32[64,4096]{1,0:T(8,128)S(1)}, f32[64,4096]{1,0:T(8,128)}, u32[]{:S(2)}) copy-start(f32[64,4096]{1,0:T(8,128)} %convert_element_type.96) | copy-start | bytes 3145732
  351.5 5.6 %copy-start.1 = (bf16[512,1,256]{2,0,1:T(8,128)(2,1)S(1)}, bf16[512,1,256]{2,0,1:T(8,128)(2,1)}, u32[]{:S(2)}) copy-start(bf16[512,1,256]{2,0,1:T(8,128)(2,1)} %param.15) | copy-start | bytes 786436
  (5 other events, 14.4 us)
Sparse Core Ops, SparseCore 0:
  10.6 109.2 all-gather.2
  122.3 102.8 all-gather.4
  235.1 108.1 all-reduce.2
